TPU v7x, 512 devices: a whole 4x8x8 slice. The times are simulated.
512 devices in a mesh: cells: 128 (over x, z_hi, y), modes: 4 (over z_lo, core).
Axes of the slice: x: 4, y: 8, z: 8 (z_hi: 4, z_lo: 2; z = z_hi * 2 + z_lo), core: 2. Of those that a mesh axis runs over, the one named last changes fastest.
Arguments:
- fields: bfloat16 [84, 4, 2048, 128], P('modes', None, 'cells'), may hold values from -1.5 to 1.5
- coupling: bfloat16 [7, 84, 84], replicated, may hold values from -0.625 to 0.625
- kl_field: float32 [7, 2048, 128], P(None, 'cells'), may hold values from -5 to 5
- material: int32 [2048, 128], P('cells'), may hold values from 0 to 7
- char_state: int32 [2048, 128], P('cells'), may hold values from 0 to 2
- material_table: float32 [7, 8], replicated, may hold values from 0.5 to 2
- char_table: float32 [7, 3], replicated, may hold values from 0.3 to 1.5
- expansion_table: float32 [7, 8], replicated, may hold values from 1 to 4
Outputs:
- response: bfloat16 [84, 4, 2048, 128], P('modes', None, 'cells')
All inputs are finite; a program needn't handle non-finite values.
Results may differ from a plain program's by a relative error of at most 0.0049.
Values may be sent and summed in bfloat16 or wider, within the bound.
No kernel may reach another device: no remote copies, remote signals or barrier semaphores. Data moves between devices by JAX's collectives and lax.ppermute only.
A program may use at most 64 MiB of HBM per device.

v0:
```python
import math

import jax
import jax.numpy as jnp
from jax import lax
from jax.sharding import PartitionSpec as P


def laid_out(blocks, dim):
    lengths = list(blocks.shape[1:])
    lengths[dim] *= blocks.shape[0]
    return jnp.moveaxis(blocks, 0, dim).reshape(lengths)


def copy_for_each(value, axis):
    copies = jnp.broadcast_to(value, (lax.axis_size(axis), *value.shape))
    return lax.all_to_all(copies, axis, split_axis=0, concat_axis=0, tiled=True)


def gather_directly(value, axis, dim):
    return laid_out(copy_for_each(value, axis), dim)


def with_halo(cells, sides, width):
    for axis, dim in sides:
        count = lax.axis_size(axis)
        ends = count - 1
        head = lax.slice_in_dim(cells, 0, width, axis=dim)
        tail = lax.slice_in_dim(cells, cells.shape[dim] - width, cells.shape[dim], axis=dim)
        cells = jnp.concatenate(
            [
                lax.ppermute(tail, axis, [(i, (i + 1) % count) for i in range(ends)]),
                cells,
                lax.ppermute(head, axis, [((i + 1) % count, i) for i in range(ends)]),
            ],
            axis=dim,
        )
    return cells


def derive(rimmed):
    center = rimmed[:, :, 1:-1].astype(jnp.float32)
    above_row = rimmed[:, :, :-2].astype(jnp.float32)
    below_row = rimmed[:, :, 2:].astype(jnp.float32)
    zero_col = jnp.zeros(center.shape[:3] + (1,), jnp.float32)
    left_col = jnp.concatenate([zero_col, center[..., :-1]], axis=3)
    right_col = jnp.concatenate([center[..., 1:], zero_col], axis=3)
    laplace = 4.0 * center - above_row - below_row - left_col - right_col
    grad_x = 0.5 * (below_row[:, 0:1] - above_row[:, 0:1])
    grad_y = 0.5 * (right_col[:, 0:1] - left_col[:, 0:1])
    return jnp.concatenate([laplace, grad_x, grad_y], axis=1).astype(jnp.bfloat16)


def lookup(table, idents):
    kinds = table.shape[1]
    onehot = (idents.reshape(1, -1) == jnp.arange(kinds, dtype=jnp.int32)[:, None]).astype(
        jnp.float32
    )
    return jnp.dot(table, onehot, precision=lax.Precision.HIGHEST)


def mix_modes(stacked, weights, cond, expand, out_modes, nfield):
    total_modes = stacked.shape[0]
    comps = stacked.shape[1]
    terms = cond.shape[0]
    cell_count = stacked.shape[2] * stacked.shape[3]
    flat_ops = stacked.reshape(total_modes, comps, cell_count)
    span = math.gcd(cell_count, 1024)

    def advance(block_index, result):
        offset = block_index * span
        piece = lax.dynamic_slice_in_dim(flat_ops, offset, span, 2)
        mixed = jnp.einsum("rm,mfc->rfc", weights, piece, preferred_element_type=jnp.float32)
        mixed = mixed.reshape(terms, out_modes, comps, span)
        cond_part = lax.dynamic_slice_in_dim(cond, offset, span, 1)
        expand_part = lax.dynamic_slice_in_dim(expand, offset, span, 1)
        diffuse = jnp.sum(cond_part[:, None, None, :] * mixed[:, :, :nfield], axis=0)
        strain = jnp.sum(expand_part[:, None, None, :] * mixed[:, :, nfield:], axis=0)
        value = jnp.concatenate([diffuse[:, 0:1], diffuse[:, 1:3] - strain, diffuse[:, 3:]], axis=1)
        return lax.dynamic_update_slice_in_dim(result, value.astype(jnp.bfloat16), offset, 2)

    start_value = jnp.zeros((out_modes, nfield, cell_count), jnp.bfloat16)
    return lax.fori_loop(0, cell_count // span, advance, start_value)


def body(
    fields, coupling, kl_field, material, char_state, material_table, char_table, expansion_table
):
    local_modes, nfield, row_count, width = fields.shape
    terms = coupling.shape[0]
    total_modes = coupling.shape[1]
    kl_flat = kl_field.reshape(terms, row_count * width)
    cond = kl_flat * lookup(material_table, material) * lookup(char_table, char_state)
    expand = kl_flat * lookup(expansion_table, material)
    gathered = gather_directly(fields, "modes", 0)
    rimmed = with_halo(gathered, (("cells", 2),), 1)
    stacked = derive(rimmed)
    first_mode = lax.axis_index("modes") * local_modes
    weights = lax.dynamic_slice_in_dim(coupling, first_mode, local_modes, 1).reshape(
        terms * local_modes, total_modes
    )
    result = mix_modes(stacked, weights, cond, expand, local_modes, nfield)
    return result.reshape(local_modes, nfield, row_count, width)


def solution(mesh):
    return jax.shard_map(
        body,
        mesh=mesh,
        in_specs=(
            P("modes", None, "cells", None),
            P(),
            P(None, "cells", None),
            P("cells", None),
            P("cells", None),
            P(),
            P(),
            P(),
        ),
        out_specs=P("modes", None, "cells", None),
        check_vma=False,
    )
```

profile of v0, /device:TPU:6, one launch (start us, length us, event | category | flops | bytes accessed | tf_op | source)
XLA Modules:
  0.0 78.0 jit_solution(7833858917979496273)
XLA Ops:
  0.1 1.1 %copy.13 = bf16[21,4,16,128]{3,2,0,1:T(8,128)(2,1)S(1)} copy(bf16[21,4,16,128]{3,2,1,0:T(8,128)(2,1)} %param.10) | data formatting | bytes 688128 | tf_op args[0]
  1.2 1.3 %broadcast_in_dim.17 = bf16[4,21,4,16,128]{4,3,1,2,0:T(8,128)(2,1)} broadcast(bf16[21,4,16,128]{3,2,0,1:T(8,128)(2,1)S(1)} %copy.13), dimensions={1,2,3,4} | broadcast | bytes 1720320 | tf_op jit(solution)/shard_map/broadcast_in_dim | solution.py:16
  2.5 3.6 %all-to-all-start = ((bf16[4,21,4,16,128]{4,3,1,2,0:T(8,128)(2,1)}), bf16[4,21,4,16,128]{4,3,1,2,0:T(8,128)(2,1)S(1)}, u32[]{:S(2)}, u32[]{:S(2)}) async-start(bf16[4,21,4,16,128]{4,3,1,2,0:T(8,128)(2,1)} %broadcast_in_dim.17), calls=%async_computation | async-start | bytes 2752512 | tf_op jit(solution)/shard_map/all_to_all | solution.py:17
  6.8 17.3 %all-to-all-done = bf16[4,21,4,16,128]{4,3,1,2,0:T(8,128)(2,1)S(1)} async-done(((bf16[4,21,4,16,128]{4,3,1,2,0:T(8,128)(2,1)}), bf16[4,21,4,16,128]{4,3,1,2,0:T(8,128)(2,1)S(1)}, u32[]{:S(2)}, u32[]{:S(2)}) %all-to-all-start) | async-done | bytes 1376288 | tf_op jit(solution)/shard_map/all_to_all | solution.py:17
  25.2 3.5 %collective-permute-start = (bf16[84,4,1,128]{3,2,1,0:T(2,128)(2,1)S(1)}, bf16[84,4,1,128]{3,2,1,0:T(2,128)(2,1)S(1)}, u32[]{:S(2)}, u32[]{:S(2)}) collective-permute-start(bf16[84,4,1,128]{3,2,1,0:T(2,128)(2,1)S(1)} %get-tuple-element.136), channel_id=1, source_target_pairs={{0,4},{4,8},{8,12},{12,16},{16,20},{20,24},{24,28},{28,32},{32,36}... | collective-permute-start | bytes 258056 | tf_op jit(solution)/shard_map/ppermute | solution.py:32
  28.7 12.4 %collective-permute-start.1 = (bf16[84,4,1,128]{3,2,1,0:T(2,128)(2,1)S(1)}, bf16[84,4,1,128]{3,2,1,0:T(2,128)(2,1)S(1)}, u32[]{:S(2)}, u32[]{:S(2)}) collective-permute-start(bf16[84,4,1,128]{3,2,1,0:T(2,128)(2,1)S(1)} %get-tuple-element.135), channel_id=1, source_target_pairs={{4,0},{8,4},{12,8},{16,12},{20,16},{24,20},{28,24},{32,28},{36,32}... | collective-permute-start | bytes 258056 | tf_op jit(solution)/shard_map/ppermute | solution.py:34
  41.1 1.1 %fusion.20 = (f32[84,4,16,127]{3,2,1,0:T(8,128)S(1)}, f32[84,4,16,127]{3,2,1,0:T(8,128)S(1)}) fusion(f32[84,4,16,128]{3,2,1,0:T(8,128)S(1)} %bitcast_convert_fusion), kind=kLoop, calls=%fused_computation.41 | loop fusion | bytes 10924032 | tf_op jit(solution)/shard_map/slice | solution.py:47
  42.3 1.5 %copy-done.1 = f32[84,4,16,127]{3,2,1,0:T(8,128)} copy-done((f32[84,4,16,127]{3,2,1,0:T(8,128)}, f32[84,4,16,127]{3,2,1,0:T(8,128)S(1)}, u32[]{:S(2)}) %copy-start.1) | copy-done | bytes 2731032
  43.8 0.9 %copy-done.2 = f32[84,4,16,127]{3,2,1,0:T(8,128)} copy-done((f32[84,4,16,127]{3,2,1,0:T(8,128)}, f32[84,4,16,127]{3,2,1,0:T(8,128)S(1)}, u32[]{:S(2)}) %copy-start.2) | copy-done | bytes 2731032
  45.1 1.1 %collective-permute-done = bf16[84,4,1,128]{3,2,1,0:T(2,128)(2,1)S(1)} collective-permute-done((bf16[84,4,1,128]{3,2,1,0:T(2,128)(2,1)S(1)}, bf16[84,4,1,128]{3,2,1,0:T(2,128)(2,1)S(1)}, u32[]{:S(2)}, u32[]{:S(2)}) %collective-permute-start) | collective-permute-done | bytes 86048 | tf_op jit(solution)/shard_map/ppermute | solution.py:32
  46.2 1.4 %fusion.9 = (f32[84,4,16,128]{3,2,1,0:T(8,128)S(1)}, f32[84,4,16,128]{3,2,1,0:T(8,128)S(1)}) fusion(bf16[84,4,1,128]{3,2,1,0:T(2,128)(2,1)S(1)} %collective-permute-done.1, bf16[84,4,16,128]{3,2,1,0:T(8,128)(2,1)S(1)} %bitcast.43, bf16[84,4,1,128]{3,2,1,0:T(2,128)(2,1)S(1)} %collective-permute-done), kind=kLoop, calls=%fused_computation.24 | loop fusion | flops 5505024 | bytes 7053312 | tf_op jit(solution)/shard_map/convert_element_type | solution.py:44
  47.9 0.9 %concatenate.37 = bf16[84,1,2048]{2,0,1:T(8,128)(2,1)} reshape(bf16[84,1,16,128]{3,2,1,0:T(8,128)(2,1)S(1)} %fusion.15) | data formatting | bytes 688128 | tf_op jit(solution)/shard_map/concatenate | solution.py:51
  48.8 4.0 %subtract_convert_fusion = bf16[84,4,16,128]{3,2,1,0:T(8,128)(2,1)S(1)} fusion(f32[84,4,16,127]{3,2,1,0:T(8,128)} %copy-done.1, f32[84,4,16,127]{3,2,1,0:T(8,128)} %copy-done.2, bf16[84,4,16,128]{3,2,1,0:T(8,128)(2,1)S(1)} %bitcast.44, bf16[84,4,1,128]{3,2,1,0:T(2,128)(2,1)} %copy-done.4, bf16[84,4,1,128]{3,2,1,0:T(2,128)(2,1)} %copy-done.5), kind=kLoop, calls=%fused_computation.13 | loop fusion | flops 10321920 | bytes 8386560 | tf_op jit(solution)/shard_map/convert.10
  53.2 0.8 copy.17
  54.5 22.5 %while.13 = (s32[]{:T(128)}, bf16[21,4,2048]{2,0,1:T(8,128)(2,1)S(1)}, f32[7,2048]{1,0:T(8,128)S(1)}, bf16[84,6,2048]{2,0,1:T(8,128)(2,1)S(1)}, bf16[147,84]{1,0...) while((s32[]{:T(128)}, ...), condition=%wide.region_3.0_spmd, body=%wide.region_0.0_spmd.sunk | while | flops 154097664 | bytes 17770656 | solution.py:83
  54.5 2.5 %convolution_bitcast_fusion.5 = f32[147,6,1024]{2,0,1:T(8,128)} fusion(bf16[84,6,2048]{2,0,1:T(8,128)(2,1)S(1)} %get-tuple-element.205, s32[]{:T(128)S(6)} %select_n.15, bf16[147,84]{1,0:T(8,128)(2,1)S(1)} %get-tuple-element.206), kind=kOutput, calls=%fused_computation.2.clone.1 | convolution fusion | flops 151732224 | bytes 4732932 | tf_op jit(solution)/shard_map/while/body/eval_jaxpr/rm,mfc->rfc/dot_general | solution.py:73
  57.0 5.0 %reshape.41 = f32[7,21,6,1024]{3,1,0,2:T(8,128)} reshape(f32[147,6,1024]{2,0,1:T(8,128)} %convolution_bitcast_fusion.5) | data formatting | bytes 7225344 | tf_op jit(solution)/shard_map/while/body/eval_jaxpr/reshape | solution.py:74
  61.9 2.2 %fusion.33 = f32[21,4,1024]{2,0,1:T(8,128)S(1)} fusion(f32[7,21,6,1024]{3,1,0,2:T(8,128)} %reshape.41, f32[7,1024]{1,0:T(8,128)S(1)} %get-tuple-element.178), kind=kLoop, calls=%fused_computation.1.clone.1 | loop fusion | flops 1118208 | bytes 2781184 | tf_op jit(solution)/shard_map/while/body/eval_jaxpr/reduce_sum | solution.py:77
  64.1 1.5 %fusion.35 = f32[21,2,1024]{2,0,1:T(8,128)S(1)} fusion(f32[7,21,6,1024]{3,1,0,2:T(8,128)} %reshape.41, f32[7,1024]{1,0:T(8,128)S(1)} %get-tuple-element.180), kind=kLoop, calls=%fused_computation.4.clone.1 | loop fusion | flops 559104 | bytes 1404928 | tf_op jit(solution)/shard_map/while/body/eval_jaxpr/reduce_sum | solution.py:78
  65.7 2.5 %convolution_bitcast_fusion.5 = f32[147,6,1024]{2,0,1:T(8,128)} fusion(bf16[84,6,2048]{2,0,1:T(8,128)(2,1)S(1)} %get-tuple-element.205, s32[]{:T(128)S(6)} %select_n.15, bf16[147,84]{1,0:T(8,128)(2,1)S(1)} %get-tuple-element.206), kind=kOutput, calls=%fused_computation.2.clone.1 | convolution fusion | flops 151732224 | bytes 4732932 | tf_op jit(solution)/shard_map/while/body/eval_jaxpr/rm,mfc->rfc/dot_general | solution.py:73
  68.2 5.0 %reshape.41 = f32[7,21,6,1024]{3,1,0,2:T(8,128)} reshape(f32[147,6,1024]{2,0,1:T(8,128)} %convolution_bitcast_fusion.5) | data formatting | bytes 7225344 | tf_op jit(solution)/shard_map/while/body/eval_jaxpr/reshape | solution.py:74
  73.2 2.2 %fusion.33 = f32[21,4,1024]{2,0,1:T(8,128)S(1)} fusion(f32[7,21,6,1024]{3,1,0,2:T(8,128)} %reshape.41, f32[7,1024]{1,0:T(8,128)S(1)} %get-tuple-element.178), kind=kLoop, calls=%fused_computation.1.clone.1 | loop fusion | flops 1118208 | bytes 2781184 | tf_op jit(solution)/shard_map/while/body/eval_jaxpr/reduce_sum | solution.py:77
  75.4 1.5 %fusion.35 = f32[21,2,1024]{2,0,1:T(8,128)S(1)} fusion(f32[7,21,6,1024]{3,1,0,2:T(8,128)} %reshape.41, f32[7,1024]{1,0:T(8,128)S(1)} %get-tuple-element.180), kind=kLoop, calls=%fused_computation.4.clone.1 | loop fusion | flops 559104 | bytes 1404928 | tf_op jit(solution)/shard_map/while/body/eval_jaxpr/reduce_sum | solution.py:78
  77.3 0.8 copy.18
  (48 shorter events, 3.6 us)
Async XLA Ops:
  0.0 6.1 %copy-start = (bf16[7,84,84]{2,1,0:T(8,128)(2,1)S(1)}, bf16[7,84,84]{2,1,0:T(8,128)(2,1)}, u32[]{:S(2)}) copy-start(bf16[7,84,84]{2,1,0:T(8,128)(2,1)} %param.11) | copy-start | bytes 296356
  0.0 6.2 %copy-start.7 = (s32[16,128]{1,0:T(8,128)S(1)}, s32[16,128]{1,0:T(8,128)}, u32[]{:S(2)}) copy-start(s32[16,128]{1,0:T(8,128)} %param.13) | copy-start | bytes 24580
  0.0 6.2 %copy-start.6 = (f32[7,16,128]{2,1,0:T(8,128)S(1)}, f32[7,16,128]{2,1,0:T(8,128)}, u32[]{:S(2)}) copy-start(f32[7,16,128]{2,1,0:T(8,128)} %param.12) | copy-start | bytes 172036
  0.0 6.2 %copy-start.9 = (f32[7,8]{1,0:T(8,128)S(1)}, f32[7,8]{1,0:T(8,128)}, u32[]{:S(2)}) copy-start(f32[7,8]{1,0:T(8,128)} %param.15) | copy-start | bytes 676
  0.0 6.3 %copy-start.8 = (s32[16,128]{1,0:T(8,128)S(1)}, s32[16,128]{1,0:T(8,128)}, u32[]{:S(2)}) copy-start(s32[16,128]{1,0:T(8,128)} %param.14) | copy-start | bytes 24580
  0.0 6.3 %copy-start.11 = (f32[7,3]{0,1:T(4,128)S(1)}, f32[7,3]{0,1:T(4,128)}, u32[]{:S(2)}) copy-start(f32[7,3]{0,1:T(4,128)} %param.16) | copy-start | bytes 256
  0.0 6.6 %copy-start.10 = (f32[7,8]{1,0:T(8,128)S(1)}, f32[7,8]{1,0:T(8,128)}, u32[]{:S(2)}) copy-start(f32[7,8]{1,0:T(8,128)} %param.17) | copy-start | bytes 676
  2.5 21.6 %all-to-all-start = ((bf16[4,21,4,16,128]{4,3,1,2,0:T(8,128)(2,1)}), bf16[4,21,4,16,128]{4,3,1,2,0:T(8,128)(2,1)S(1)}, u32[]{:S(2)}, u32[]{:S(2)}) async-start(bf16[4,21,4,16,128]{4,3,1,2,0:T(8,128)(2,1)} %broadcast_in_dim.17), calls=%async_computation | async-start | bytes 2752512 | tf_op jit(solution)/shard_map/all_to_all | solution.py:17
  25.2 21.0 %collective-permute-start = (bf16[84,4,1,128]{3,2,1,0:T(2,128)(2,1)S(1)}, bf16[84,4,1,128]{3,2,1,0:T(2,128)(2,1)S(1)}, u32[]{:S(2)}, u32[]{:S(2)}) collective-permute-start(bf16[84,4,1,128]{3,2,1,0:T(2,128)(2,1)S(1)} %get-tuple-element.136), channel_id=1, source_target_pairs={{0,4},{4,8},{8,12},{12,16},{16,20},{20,24},{24,28},{28,32},{32,36}... | collective-permute-start | bytes 258056 | tf_op jit(solution)/shard_map/ppermute | solution.py:32
  28.7 17.5 %collective-permute-start.1 = (bf16[84,4,1,128]{3,2,1,0:T(2,128)(2,1)S(1)}, bf16[84,4,1,128]{3,2,1,0:T(2,128)(2,1)S(1)}, u32[]{:S(2)}, u32[]{:S(2)}) collective-permute-start(bf16[84,4,1,128]{3,2,1,0:T(2,128)(2,1)S(1)} %get-tuple-element.135), channel_id=1, source_target_pairs={{4,0},{8,4},{12,8},{16,12},{20,16},{24,20},{28,24},{32,28},{36,32}... | collective-permute-start | bytes 258056 | tf_op jit(solution)/shard_map/ppermute | solution.py:34
  42.2 1.6 %copy-start.1 = (f32[84,4,16,127]{3,2,1,0:T(8,128)}, f32[84,4,16,127]{3,2,1,0:T(8,128)S(1)}, u32[]{:S(2)}) copy-start(f32[84,4,16,127]{3,2,1,0:T(8,128)S(1)} %get-tuple-element.131) | copy-start | bytes 8193028
  42.3 2.4 %copy-start.2 = (f32[84,4,16,127]{3,2,1,0:T(8,128)}, f32[84,4,16,127]{3,2,1,0:T(8,128)S(1)}, u32[]{:S(2)}) copy-start(f32[84,4,16,127]{3,2,1,0:T(8,128)S(1)} %get-tuple-element.132) | copy-start | bytes 8193028
  46.2 1.4 %copy-start.4 = (bf16[84,4,1,128]{3,2,1,0:T(2,128)(2,1)}, bf16[84,4,1,128]{3,2,1,0:T(2,128)(2,1)S(1)}, u32[]{:S(2)}) copy-start(bf16[84,4,1,128]{3,2,1,0:T(2,128)(2,1)S(1)} %collective-permute-done) | copy-start | bytes 258052
  46.2 1.4 %copy-start.5 = (bf16[84,4,1,128]{3,2,1,0:T(2,128)(2,1)}, bf16[84,4,1,128]{3,2,1,0:T(2,128)(2,1)S(1)}, u32[]{:S(2)}) copy-start(bf16[84,4,1,128]{3,2,1,0:T(2,128)(2,1)S(1)} %collective-permute-done.1) | copy-start | bytes 258052
  53.2 1.0 %copy-start.3 = (bf16[84,1,2048]{2,0,1:T(8,128)(2,1)S(1)}, bf16[84,1,2048]{2,0,1:T(8,128)(2,1)}, u32[]{:S(2)}) copy-start(bf16[84,1,2048]{2,0,1:T(8,128)(2,1)} %concatenate.37) | copy-start | bytes 1032196
where the time goes:
time: 78.7 us; the launch traced here: 78 us
  local copies, waits for them, and re-layouts  20.1 us (26%)
  starting transfers between devices  19.5 us (25%)
  waiting for transfers between devices  18.4 us (23%)
  other arithmetic  14.1 us (18%)
  matrix products  5.51 us (7%)
    all_to_all x1, waiting for transfers between devices, copy_for_each(): return lax.all_to_all(copies, axis, split_axis=0, concat_axis=0, tiled=True)  17.3 us
    ppermute x1, starting transfers between devices, with_halo(): lax.ppermute(head, axis, [((i + 1) % count, i) for i in range(ends)])  12.4 us
    reshape x2, local copies, waits for them, and re-layouts, advance(): mixed = mixed.reshape(terms, out_modes, comps, span)  9.91 us
    dot_general x2, matrix products, advance(): jnp.einsum('rm,mfc->rfc', weights, piece, preferred_element_type=jnp.floa...  4.97 us
    another operation x7, other arithmetic  4.55 us
    reduce_sum x2, other arithmetic, advance(): jnp.sum(cond_part[:, None, None, :] * mixed[:, :, :nfield], axis=0)  4.32 us
    unnamed x25, local copies, waits for them, and re-layouts  3.78 us
    all_to_all x1, starting transfers between devices, copy_for_each(): return lax.all_to_all(copies, axis, split_axis=0, concat_axis=0, tiled=True)  3.64 us
  transfers between devices with their start and end apart: 3, of which 2 were waited for; matrix products, arithmetic and copies ran while one was open for 3% of the time, Pallas kernels for 0%

commit v1 on v0

v1 whole, which is shorter than its diff:
```python
import functools

import jax
import jax.numpy as jnp
from jax import lax
from jax.experimental import pallas as pl
from jax.experimental.pallas import tpu as pltpu
from jax.sharding import PartitionSpec as P

PAD_I = 24
SLOT = 24


def laid_out(blocks, dim):
    lengths = list(blocks.shape[1:])
    lengths[dim] *= blocks.shape[0]
    return jnp.moveaxis(blocks, 0, dim).reshape(lengths)


def copy_for_each(value, axis):
    copies = jnp.broadcast_to(value, (lax.axis_size(axis), *value.shape))
    return lax.all_to_all(copies, axis, split_axis=0, concat_axis=0, tiled=True)


def gather_directly(value, axis, dim):
    return laid_out(copy_for_each(value, axis), dim)


def edge_rows(cells, axis, dim):
    count = lax.axis_size(axis)
    ends = count - 1
    head = lax.slice_in_dim(cells, 0, 1, axis=dim)
    tail = lax.slice_in_dim(cells, cells.shape[dim] - 1, cells.shape[dim], axis=dim)
    above = lax.ppermute(tail, axis, [(i, (i + 1) % count) for i in range(ends)])
    below = lax.ppermute(head, axis, [((i + 1) % count, i) for i in range(ends)])
    return above, below


def kernel(nmode, nfield, rows, width, terms, nmat, nchar,
           fg_ref, top_ref, bot_ref, cp_ref, kl_ref, mat_ref, chr_ref,
           mt_ref, ct_ref, et_ref, out_ref, fs, os, cs, es):
    nloc = out_ref.shape[0]
    mat = mat_ref[...]
    chs = chr_ref[...]
    for k in range(terms):
        mv = jnp.zeros((rows, width), jnp.float32)
        ev = jnp.zeros((rows, width), jnp.float32)
        for m in range(nmat):
            hit = mat == m
            mv = jnp.where(hit, mt_ref[k, m], mv)
            ev = jnp.where(hit, et_ref[k, m], ev)
        cv = jnp.zeros((rows, width), jnp.float32)
        for q in range(nchar):
            cv = jnp.where(chs == q, ct_ref[k, q], cv)
        kl = kl_ref[k]
        cs[k] = kl * mv * cv
        es[k] = kl * ev

    def fill(jf, carry):
        src = pl.multiple_of(jf * rows, rows)
        dst = pl.multiple_of(jf * SLOT, 8)
        fs[pl.ds(dst, rows), :] = fg_ref[pl.ds(src, rows), :].astype(jnp.float32)
        return carry

    lax.fori_loop(0, nmode * nfield, fill, 0)
    fs[pl.ds(rows, nmode * nfield, stride=SLOT), :] = top_ref[...].astype(jnp.float32)
    fs[pl.ds(rows + 1, nmode * nfield, stride=SLOT), :] = bot_ref[...].astype(jnp.float32)

    lane = lax.broadcasted_iota(jnp.int32, (nmode, width), 1)
    first = lane == 0
    last = lane == width - 1
    stride = nfield * SLOT

    def row(f, r):
        return fs[pl.ds(f * SLOT + r, nmode, stride=stride), :]

    def step(x, carry):
        up = jnp.where(x == 0, rows, x - 1)
        down = jnp.where(x == rows - 1, rows + 1, x + 1)
        comps = []
        grads = None
        for f in range(nfield):
            center = row(f, x)
            above = row(f, up)
            below = row(f, down)
            left = jnp.where(first, 0.0, pltpu.roll(center, 1, 1))
            right = jnp.where(last, 0.0, pltpu.roll(center, width - 1, 1))
            lap = 4.0 * center - above - below - left - right
            comps.append(lap.astype(jnp.bfloat16))
            if f == 0:
                gx = 0.5 * (below - above)
                gy = 0.5 * (right - left)
                grads = (gx.astype(jnp.bfloat16), gy.astype(jnp.bfloat16))
        operand = jnp.concatenate(comps + list(grads), axis=1)
        mixed = jnp.dot(cp_ref[...], operand, preferred_element_type=jnp.float32)
        cvals = [jnp.broadcast_to(cs[k, pl.ds(x, 1), :], (PAD_I, width)) for k in range(terms)]
        evals = [jnp.broadcast_to(es[k, pl.ds(x, 1), :], (PAD_I, width)) for k in range(terms)]
        for f in range(nfield):
            diffuse = None
            for k in range(terms):
                part = cvals[k] * mixed[k * PAD_I:(k + 1) * PAD_I, f * width:(f + 1) * width]
                diffuse = part if diffuse is None else diffuse + part
            if f in (1, 2):
                c = nfield + f - 1
                strain = None
                for k in range(terms):
                    part = evals[k] * mixed[k * PAD_I:(k + 1) * PAD_I, c * width:(c + 1) * width]
                    strain = part if strain is None else strain + part
                diffuse = diffuse - strain
            os[pl.ds(f * rows + x, PAD_I, stride=nfield * rows), :] = diffuse
        return carry

    lax.fori_loop(0, rows, step, 0)

    def emit(i, carry):
        base = pl.multiple_of(i * nfield * rows, 8)
        out_ref[i] = os[pl.ds(base, nfield * rows), :].reshape(nfield, rows, width).astype(out_ref.dtype)
        return carry

    lax.fori_loop(0, nloc, emit, 0)


def body(
    fields, coupling, kl_field, material, char_state, material_table, char_table, expansion_table
):
    local_modes, nfield, rows, width = fields.shape
    terms = coupling.shape[0]
    total_modes = coupling.shape[1]
    gathered = gather_directly(fields, "modes", 0)
    above, below = edge_rows(gathered, "cells", 2)
    first_mode = lax.axis_index("modes") * local_modes
    weights = lax.dynamic_slice_in_dim(coupling, first_mode, local_modes, 1)
    weights = jnp.pad(weights, ((0, 0), (0, PAD_I - local_modes), (0, 0)))
    weights = weights.reshape(terms * PAD_I, total_modes)
    vmem = pl.BlockSpec(memory_space=pltpu.VMEM)
    smem = pl.BlockSpec(memory_space=pltpu.SMEM)
    run = pl.pallas_call(
        functools.partial(kernel, total_modes, nfield, rows, width, terms,
                          material_table.shape[1], char_table.shape[1]),
        out_shape=jax.ShapeDtypeStruct(fields.shape, fields.dtype),
        in_specs=[vmem] * 7 + [smem] * 3,
        out_specs=vmem,
        scratch_shapes=[
            pltpu.VMEM((total_modes * nfield * SLOT, width), jnp.float32),
            pltpu.VMEM((PAD_I * nfield * rows, width), jnp.float32),
            pltpu.VMEM((terms, rows, width), jnp.float32),
            pltpu.VMEM((terms, rows, width), jnp.float32),
        ],
        compiler_params=pltpu.CompilerParams(vmem_limit_bytes=48 * 1024 * 1024),
    )
    return run(
        gathered.reshape(total_modes * nfield * rows, width),
        above.reshape(total_modes * nfield, width),
        below.reshape(total_modes * nfield, width),
        weights,
        kl_field,
        material,
        char_state,
        material_table,
        char_table,
        expansion_table,
    )


def solution(mesh):
    return jax.shard_map(
        body,
        mesh=mesh,
        in_specs=(
            P("modes", None, "cells", None),
            P(),
            P(None, "cells", None),
            P("cells", None),
            P("cells", None),
            P(),
            P(),
            P(),
        ),
        out_specs=P("modes", None, "cells", None),
        check_vma=False,
    )
```

time: 78.7 us -> 55.3 us (0.70)
  local copies, waits for them, and re-layouts: 20.1 us -> 3.21 us
  other arithmetic: 14.1 us -> 0 us
  Pallas kernels: 0 us -> 12.2 us
  matrix products: 5.51 us -> 0 us
  waiting for transfers between devices: 18.4 us -> 19.8 us
    pallas_call x0 -> x1, Pallas kernels: none -> 12.2 us  [body(): run(gathered.reshape(total_modes * nfield * rows, width), above.reshape(t...]
    reshape x5 -> x0, local copies, waits for them, and re-layouts: 10.9 us -> none  [the longest x2 9.91 us: advance(): mixed = mixed.reshape(terms, out_modes, comps, span)]
    reduce_sum x4 -> x0, other arithmetic: 7.37 us -> none  [the longest x2 4.32 us: advance(): jnp.sum(cond_part[:, None, None, :] * mixed[:, :, :nfield], axis=0)]
    dot_general x5 -> x0, matrix products: 5.51 us -> none  [the longest x2 4.97 us: advance(): jnp.einsum('rm,mfc->rfc', weights, piece, preferred_element_type=jnp.floa...]
    another operation x7 -> x0, other arithmetic: 4.55 us -> none
    unnamed x25 -> x15, local copies, waits for them, and re-layouts: 3.78 us -> 0.12 us
    concatenate x4 -> x0, local copies, waits for them, and re-layouts: 2.19 us -> none  [derive(): jnp.concatenate([laplace, grad_x, grad_y], axis=1).astype(jnp.bfloat16)]
    convert_element_type x2 -> x0, other arithmetic: 1.87 us -> none  [the longest x1 1.42 us: derive(): below_row = rimmed[:, :, 2:].astype(jnp.float32)]
  transfers between devices with their start and end apart: 3 -> 3, of which waited for: 2 -> 3; matrix products, arithmetic and copies ran while one was open for 3% -> 0% of each run, Pallas kernels for 0% -> 0%
where the time goes in v1:
time: 55.3 us; the launch traced here: 55 us
  waiting for transfers between devices  19.8 us (36%)
  starting transfers between devices  19.7 us (36%)
  Pallas kernels  12.2 us (22%)
  local copies, waits for them, and re-layouts  3.21 us (6%)
    all_to_all x1, waiting for transfers between devices, copy_for_each(): return lax.all_to_all(copies, axis, split_axis=0, concat_axis=0, tiled=True)  17.8 us
    ppermute x1, starting transfers between devices, edge_rows(): lax.ppermute(head, axis, [((i + 1) % count, i) for i in range(ends)])  12.4 us
    pallas_call x1, Pallas kernels, body(): run(gathered.reshape(total_modes * nfield * rows, width), above.reshape(t...  12.2 us
    all_to_all x1, starting transfers between devices, copy_for_each(): return lax.all_to_all(copies, axis, split_axis=0, concat_axis=0, tiled=True)  3.77 us
    ppermute x1, starting transfers between devices, edge_rows(): lax.ppermute(tail, axis, [(i, (i + 1) % count) for i in range(ends)])  3.48 us
    broadcast_in_dim x1, local copies, waits for them, and re-layouts, copy_for_each(): copies = jnp.broadcast_to(value, (lax.axis_size(axis), *value.shape))  2.45 us
    ppermute x1, waiting for transfers between devices, edge_rows(): lax.ppermute(tail, axis, [(i, (i + 1) % count) for i in range(ends)])  1.38 us
  transfers between devices with their start and end apart: 3, of which 3 were waited for; matrix products, arithmetic and copies ran while one was open for 0% of the time, Pallas kernels for 0%

profile of v1, /device:TPU:6, one launch (start us, length us, event | category | flops | bytes accessed | tf_op | source)
XLA Modules:
  0.0 55.0 jit_solution(6016932423228186620)
XLA Ops:
  0.0 0.0 copy-start
  0.0 2.5 %broadcast_in_dim.3 = bf16[4,21,4,16,128]{4,3,2,1,0:T(8,128)(2,1)} broadcast(bf16[21,4,16,128]{3,2,1,0:T(8,128)(2,1)} %param.8), dimensions={1,2,3,4} | broadcast | bytes 1720320 | tf_op jit(solution)/shard_map/broadcast_in_dim | solution.py:21
  2.5 0.0 copy-start.6
  2.5 3.8 %all-to-all-start = ((bf16[4,21,4,16,128]{4,3,2,1,0:T(8,128)(2,1)}), bf16[4,21,4,16,128]{4,3,2,1,0:T(8,128)(2,1)S(1)}, u32[]{:S(2)}, u32[]{:S(2)}) async-start(bf16[4,21,4,16,128]{4,3,2,1,0:T(8,128)(2,1)} %broadcast_in_dim.3), calls=%async_computation | async-start | bytes 2752512 | tf_op jit(solution)/shard_map/all_to_all | solution.py:22
  6.2 0.0 copy-done.6
  6.2 0.1 copy.10.ct_ref
  6.3 0.0 copy-start.1
  6.3 0.0 copy-start.2
  6.3 0.0 copy-start.3
  6.3 0.0 copy-start.5
  6.3 17.8 %all-to-all-done = bf16[4,21,4,16,128]{4,3,2,1,0:T(8,128)(2,1)S(1)} async-done(((bf16[4,21,4,16,128]{4,3,2,1,0:T(8,128)(2,1)}), bf16[4,21,4,16,128]{4,3,2,1,0:T(8,128)(2,1)S(1)}, u32[]{:S(2)}, u32[]{:S(2)}) %all-to-all-start) | async-done | bytes 1376288 | tf_op jit(solution)/shard_map/all_to_all | solution.py:22
  24.2 0.5 copy.9
  24.7 0.1 fusion
  24.8 3.5 %collective-permute-start = (bf16[84,4,1,128]{3,1,0,2:T(4,128)(2,1)S(1)}, bf16[84,4,1,128]{3,1,0,2:T(4,128)(2,1)S(1)}, u32[]{:S(2)}, u32[]{:S(2)}) collective-permute-start(bf16[84,4,1,128]{3,1,0,2:T(4,128)(2,1)S(1)} %get-tuple-element.6), channel_id=1, source_target_pairs={{0,4},{4,8},{8,12},{12,16},{16,20},{20,24},{24,28},{28,32},{32,36}... | collective-permute-start | bytes 258056 | tf_op jit(solution)/shard_map/ppermute | solution.py:34
  28.3 12.4 %collective-permute-start.1 = (bf16[84,4,1,128]{3,1,0,2:T(4,128)(2,1)S(1)}, bf16[84,4,1,128]{3,1,0,2:T(4,128)(2,1)S(1)}, u32[]{:S(2)}, u32[]{:S(2)}) collective-permute-start(bf16[84,4,1,128]{3,1,0,2:T(4,128)(2,1)S(1)} %get-tuple-element.5), channel_id=1, source_target_pairs={{4,0},{8,4},{12,8},{16,12},{20,16},{24,20},{28,24},{32,28},{36,32}... | collective-permute-start | bytes 258056 | tf_op jit(solution)/shard_map/ppermute | solution.py:35
  40.7 0.0 copy-done
  40.8 1.4 %collective-permute-done = bf16[84,4,1,128]{3,1,0,2:T(4,128)(2,1)S(1)} collective-permute-done((bf16[84,4,1,128]{3,1,0,2:T(4,128)(2,1)S(1)}, bf16[84,4,1,128]{3,1,0,2:T(4,128)(2,1)S(1)}, u32[]{:S(2)}, u32[]{:S(2)}) %collective-permute-start) | collective-permute-done | bytes 86048 | tf_op jit(solution)/shard_map/ppermute | solution.py:34
  42.1 0.6 %collective-permute-done.1 = bf16[84,4,1,128]{3,1,0,2:T(4,128)(2,1)S(1)} collective-permute-done((bf16[84,4,1,128]{3,1,0,2:T(4,128)(2,1)S(1)}, bf16[84,4,1,128]{3,1,0,2:T(4,128)(2,1)S(1)}, u32[]{:S(2)}, u32[]{:S(2)}) %collective-permute-start.1) | collective-permute-done | bytes 86048 | tf_op jit(solution)/shard_map/ppermute | solution.py:35
  42.8 0.0 copy-done.1
  42.8 0.0 copy-done.2
  42.8 0.0 copy-done.3
  42.8 0.0 copy-done.4
  42.8 0.0 copy-done.5
  42.8 12.2 %shard_map.82 = bf16[21,4,16,128]{3,2,1,0:T(8,128)(2,1)} custom-call(bf16[5376,128]{1,0:T(8,128)(2,1)S(1)} %bitcast.5, bf16[336,128]{1,0:T(8,128)(2,1)S(1)} %bitcast.7, bf16[336,128]{1,0:T(8,128)(2,1)S(1)} %bitcast.8, bf16[168,84]{1,0:T(8,128)(2,1)S(1)} %bitcast.6, f32[7,16,128]{2,1,0:T(8,128)S(1)} %copy-done.1, s32[16,128]{1,0:T(8,128)S(1)} %copy-done.2, ...), custom_call_target="tpu_custom_call" | custom-call | tf_op jit(solution)/shard_map/pallas_call | solution.py:151
  (3 shorter events, 0.0 us)
Async XLA Ops:
  0.0 40.7 %copy-start = (bf16[7,84,84]{2,1,0:T(8,128)(2,1)S(1)}, bf16[7,84,84]{2,1,0:T(8,128)(2,1)}, u32[]{:S(2)}) copy-start(bf16[7,84,84]{2,1,0:T(8,128)(2,1)} %param.9) | copy-start | bytes 296356
  2.5 3.8 %copy-start.6 = (f32[7,3]{0,1:T(4,128)S(1)}, f32[7,3]{0,1:T(4,128)}, u32[]{:S(2)}) copy-start(f32[7,3]{0,1:T(4,128)} %param.14) | copy-start | bytes 256
  2.5 21.7 %all-to-all-start = ((bf16[4,21,4,16,128]{4,3,2,1,0:T(8,128)(2,1)}), bf16[4,21,4,16,128]{4,3,2,1,0:T(8,128)(2,1)S(1)}, u32[]{:S(2)}, u32[]{:S(2)}) async-start(bf16[4,21,4,16,128]{4,3,2,1,0:T(8,128)(2,1)} %broadcast_in_dim.3), calls=%async_computation | async-start | bytes 2752512 | tf_op jit(solution)/shard_map/all_to_all | solution.py:22
  6.3 36.5 %copy-start.1 = (f32[7,16,128]{2,1,0:T(8,128)S(1)}, f32[7,16,128]{2,1,0:T(8,128)}, u32[]{:S(2)}) copy-start(f32[7,16,128]{2,1,0:T(8,128)} %kl_ref.1) | copy-start | bytes 172036
  6.3 36.5 %copy-start.2 = (s32[16,128]{1,0:T(8,128)S(1)}, s32[16,128]{1,0:T(8,128)}, u32[]{:S(2)}) copy-start(s32[16,128]{1,0:T(8,128)} %mat_ref.1) | copy-start | bytes 24580
  6.3 36.5 %copy-start.3 = (s32[16,128]{1,0:T(8,128)S(1)}, s32[16,128]{1,0:T(8,128)}, u32[]{:S(2)}) copy-start(s32[16,128]{1,0:T(8,128)} %chr_ref.1) | copy-start | bytes 24580
  6.3 36.5 %copy-start.4 = (f32[7,8]{1,0:T(8,128)S(1)}, f32[7,8]{1,0:T(8,128)}, u32[]{:S(2)}) copy-start(f32[7,8]{1,0:T(8,128)} %mt_ref.1) | copy-start | bytes 676
  6.3 36.5 %copy-start.5 = (f32[7,8]{1,0:T(8,128)S(1)}, f32[7,8]{1,0:T(8,128)}, u32[]{:S(2)}) copy-start(f32[7,8]{1,0:T(8,128)} %et_ref.1) | copy-start | bytes 676
  24.8 17.4 %collective-permute-start = (bf16[84,4,1,128]{3,1,0,2:T(4,128)(2,1)S(1)}, bf16[84,4,1,128]{3,1,0,2:T(4,128)(2,1)S(1)}, u32[]{:S(2)}, u32[]{:S(2)}) collective-permute-start(bf16[84,4,1,128]{3,1,0,2:T(4,128)(2,1)S(1)} %get-tuple-element.6), channel_id=1, source_target_pairs={{0,4},{4,8},{8,12},{12,16},{16,20},{20,24},{24,28},{28,32},{32,36}... | collective-permute-start | bytes 258056 | tf_op jit(solution)/shard_map/ppermute | solution.py:34
  28.3 14.5 %collective-permute-start.1 = (bf16[84,4,1,128]{3,1,0,2:T(4,128)(2,1)S(1)}, bf16[84,4,1,128]{3,1,0,2:T(4,128)(2,1)S(1)}, u32[]{:S(2)}, u32[]{:S(2)}) collective-permute-start(bf16[84,4,1,128]{3,1,0,2:T(4,128)(2,1)S(1)} %get-tuple-element.5), channel_id=1, source_target_pairs={{4,0},{8,4},{12,8},{16,12},{20,16},{24,20},{28,24},{32,28},{36,32}... | collective-permute-start | bytes 258056 | tf_op jit(solution)/shard_map/ppermute | solution.py:35

commit v2 on v1

--- a/solution.py
+++ b/solution.py
@@ -11,21 +11,6 @@
 SLOT = 24
 
 
-def laid_out(blocks, dim):
-    lengths = list(blocks.shape[1:])
-    lengths[dim] *= blocks.shape[0]
-    return jnp.moveaxis(blocks, 0, dim).reshape(lengths)
-
-
-def copy_for_each(value, axis):
-    copies = jnp.broadcast_to(value, (lax.axis_size(axis), *value.shape))
-    return lax.all_to_all(copies, axis, split_axis=0, concat_axis=0, tiled=True)
-
-
-def gather_directly(value, axis, dim):
-    return laid_out(copy_for_each(value, axis), dim)
-
-
 def edge_rows(cells, axis, dim):
     count = lax.axis_size(axis)
     ends = count - 1
@@ -37,9 +22,10 @@
 
 
 def kernel(nmode, nfield, rows, width, terms, nmat, nchar,
-           fg_ref, top_ref, bot_ref, cp_ref, kl_ref, mat_ref, chr_ref,
+           b0_ref, b1_ref, b2_ref, b3_ref, cp_ref, kl_ref, mat_ref, chr_ref,
            mt_ref, ct_ref, et_ref, out_ref, fs, os, cs, es):
     nloc = out_ref.shape[0]
+    blocks = (b0_ref, b1_ref, b2_ref, b3_ref)
     mat = mat_ref[...]
     chs = chr_ref[...]
     for k in range(terms):
@@ -56,15 +42,18 @@
         cs[k] = kl * mv * cv
         es[k] = kl * ev
 
-    def fill(jf, carry):
-        src = pl.multiple_of(jf * rows, rows)
-        dst = pl.multiple_of(jf * SLOT, 8)
-        fs[pl.ds(dst, rows), :] = fg_ref[pl.ds(src, rows), :].astype(jnp.float32)
-        return carry
+    per = nloc * nfield
+    for d, blk in enumerate(blocks):
+        def fill(jf, carry, blk=blk, d=d):
+            src = pl.multiple_of(jf * rows, rows)
+            dst = pl.multiple_of((d * per + jf) * SLOT, 8)
+            fs[pl.ds(dst, rows), :] = blk[pl.ds(src, rows), :].astype(jnp.float32)
+            return carry
 
-    lax.fori_loop(0, nmode * nfield, fill, 0)
-    fs[pl.ds(rows, nmode * nfield, stride=SLOT), :] = top_ref[...].astype(jnp.float32)
-    fs[pl.ds(rows + 1, nmode * nfield, stride=SLOT), :] = bot_ref[...].astype(jnp.float32)
+        lax.fori_loop(0, per, fill, 0, unroll=12)
+        halo = per * rows
+        fs[pl.ds(d * per * SLOT + rows, per, stride=SLOT), :] = blk[pl.ds(halo, per), :].astype(jnp.float32)
+        fs[pl.ds(d * per * SLOT + rows + 1, per, stride=SLOT), :] = blk[pl.ds(halo + per, per), :].astype(jnp.float32)
 
     lane = lax.broadcasted_iota(jnp.int32, (nmode, width), 1)
     first = lane == 0
@@ -126,10 +115,30 @@
     local_modes, nfield, rows, width = fields.shape
     terms = coupling.shape[0]
     total_modes = coupling.shape[1]
-    gathered = gather_directly(fields, "modes", 0)
-    above, below = edge_rows(gathered, "cells", 2)
-    first_mode = lax.axis_index("modes") * local_modes
+    groups = lax.axis_size("modes")
+    assert groups == 4
+    above, below = edge_rows(fields, "cells", 2)
+    pack = jnp.concatenate(
+        [
+            fields.reshape(local_modes * nfield * rows, width),
+            above.reshape(local_modes * nfield, width),
+            below.reshape(local_modes * nfield, width),
+        ],
+        axis=0,
+    )
+    partner = lax.ppermute(pack, "modes", [(i, i ^ 1) for i in range(groups)])
+    counter = lax.ppermute(pack, "modes", [(i, i ^ 2) for i in range(groups)])
+    diagonal = lax.ppermute(counter, "modes", [(i, i ^ 1) for i in range(groups)])
+    me = lax.axis_index("modes")
+    first_mode = me * local_modes
     weights = lax.dynamic_slice_in_dim(coupling, first_mode, local_modes, 1)
+    weights = jnp.concatenate(
+        [
+            lax.dynamic_slice_in_dim(weights, (me ^ flip) * local_modes, local_modes, 2)
+            for flip in range(groups)
+        ],
+        axis=2,
+    )
     weights = jnp.pad(weights, ((0, 0), (0, PAD_I - local_modes), (0, 0)))
     weights = weights.reshape(terms * PAD_I, total_modes)
     vmem = pl.BlockSpec(memory_space=pltpu.VMEM)
@@ -138,7 +147,7 @@
         functools.partial(kernel, total_modes, nfield, rows, width, terms,
                           material_table.shape[1], char_table.shape[1]),
         out_shape=jax.ShapeDtypeStruct(fields.shape, fields.dtype),
-        in_specs=[vmem] * 7 + [smem] * 3,
+        in_specs=[vmem] * 8 + [smem] * 3,
         out_specs=vmem,
         scratch_shapes=[
             pltpu.VMEM((total_modes * nfield * SLOT, width), jnp.float32),
@@ -149,9 +158,10 @@
         compiler_params=pltpu.CompilerParams(vmem_limit_bytes=48 * 1024 * 1024),
     )
     return run(
-        gathered.reshape(total_modes * nfield * rows, width),
-        above.reshape(total_modes * nfield, width),
-        below.reshape(total_modes * nfield, width),
+        pack,
+        partner,
+        counter,
+        diagonal,
         weights,
         kl_field,
         material,

time: 55.3 us -> 53.8 us (0.973); the launches traced: 55 us -> 52.8 us
  waiting for transfers between devices: 19.8 us -> 15.8 us
  starting transfers between devices: 19.7 us -> 23.2 us
  Pallas kernels: 12.2 us -> 10.6 us
  local copies, waits for them, and re-layouts: 3.21 us -> 2.61 us
    all_to_all x1 -> x0, waiting for transfers between devices: 17.8 us -> none  [copy_for_each(): return lax.all_to_all(copies, axis, split_axis=0, concat_axis=0, tiled=True)]
    ppermute x1, waiting for transfers between devices: 1.38 us -> 9.39 us  [edge_rows(): lax.ppermute(tail, axis, [(i, (i + 1) % count) for i in range(ends)])]
    ppermute x0 -> x3, starting transfers between devices: none -> 7.21 us  [the longest x1 3.38 us: body(): counter = lax.ppermute(pack, 'modes', [(i, i ^ 2) for i in range(groups)])]
    ppermute x0 -> x3, waiting for transfers between devices: none -> 6.43 us  [the longest x1 5.89 us: body(): counter = lax.ppermute(pack, 'modes', [(i, i ^ 2) for i in range(groups)])]
    all_to_all x1 -> x0, starting transfers between devices: 3.77 us -> none  [copy_for_each(): return lax.all_to_all(copies, axis, split_axis=0, concat_axis=0, tiled=True)]
    broadcast_in_dim x1 -> x0, local copies, waits for them, and re-layouts: 2.45 us -> none  [copy_for_each(): copies = jnp.broadcast_to(value, (lax.axis_size(axis), *value.shape))]
    ppermute x1, starting transfers between devices: 12.4 us -> 14.1 us  [edge_rows(): lax.ppermute(head, axis, [((i + 1) % count, i) for i in range(ends)])]
    pallas_call x1, Pallas kernels: 12.2 us -> 10.6 us  [body(): run(pack, partner, counter, diagonal, weights, kl_field, material, char_s...]
  transfers between devices with their start and end apart: 3 -> 5, of which waited for: 3 -> 3; matrix products, arithmetic and copies ran while one was open for 0% -> 1% of each run, Pallas kernels for 0% -> 0%
where the time goes in v2:
time: 53.8 us; the launch traced here: 52.8 us
  starting transfers between devices  23.2 us (43%)
  waiting for transfers between devices  15.8 us (29%)
  Pallas kernels  10.6 us (20%)
  local copies, waits for them, and re-layouts  2.61 us (5%)
    ppermute x1, starting transfers between devices, edge_rows(): lax.ppermute(head, axis, [((i + 1) % count, i) for i in range(ends)])  14.1 us
    pallas_call x1, Pallas kernels, body(): run(pack, partner, counter, diagonal, weights, kl_field, material, char_s...  10.6 us
    ppermute x1, waiting for transfers between devices, edge_rows(): lax.ppermute(tail, axis, [(i, (i + 1) % count) for i in range(ends)])  9.39 us
    ppermute x1, waiting for transfers between devices, body(): counter = lax.ppermute(pack, 'modes', [(i, i ^ 2) for i in range(groups)])  5.89 us
    ppermute x1, starting transfers between devices, body(): counter = lax.ppermute(pack, 'modes', [(i, i ^ 2) for i in range(groups)])  3.38 us
    ppermute x1, starting transfers between devices, edge_rows(): lax.ppermute(tail, axis, [(i, (i + 1) % count) for i in range(ends)])  1.92 us
    ppermute x1, starting transfers between devices, body(): partner = lax.ppermute(pack, 'modes', [(i, i ^ 1) for i in range(groups)])  1.92 us
    ppermute x1, starting transfers between devices, body(): lax.ppermute(counter, 'modes', [(i, i ^ 1) for i in range(groups)])  1.91 us
  transfers between devices with their start and end apart: 5, of which 3 were waited for; matrix products, arithmetic and copies ran while one was open for 1% of the time, Pallas kernels for 0%

profile of v2, /device:TPU:6, one launch (start us, length us, event | category | flops | bytes accessed | tf_op | source)
XLA Modules:
  0.0 52.8 jit_solution(16405750112427944965)
XLA Ops:
  0.0 1.1 %fusion.7 = (bf16[21,4,1,128]{3,2,1,0:T(2,128)(2,1)S(1)}, bf16[21,4,1,128]{3,2,1,0:T(2,128)(2,1)S(1)}) fusion(bf16[21,4,16,128]{3,2,1,0:T(8,128)(2,1)} %param.8), kind=kLoop, calls=%fused_computation.12 | loop fusion | bytes 86016 | tf_op jit(solution)/shard_map/slice | solution.py:17
  1.1 14.1 %collective-permute-start.1 = (bf16[21,4,1,128]{3,2,1,0:T(2,128)(2,1)S(1)}, bf16[21,4,1,128]{3,2,1,0:T(2,128)(2,1)S(1)}, u32[]{:S(2)}, u32[]{:S(2)}) collective-permute-start(bf16[21,4,1,128]{3,2,1,0:T(2,128)(2,1)S(1)} %get-tuple-element.5), channel_id=1, source_target_pairs={{4,0},{8,4},{12,8},{16,12},{20,16},{24,20},{28,24},{32,28},{36,32}... | collective-permute-start | bytes 64520 | tf_op jit(solution)/shard_map/ppermute | solution.py:20
  15.2 1.9 %collective-permute-start = (bf16[21,4,1,128]{3,2,1,0:T(2,128)(2,1)S(1)}, bf16[21,4,1,128]{3,2,1,0:T(2,128)(2,1)S(1)}, u32[]{:S(2)}, u32[]{:S(2)}) collective-permute-start(bf16[21,4,1,128]{3,2,1,0:T(2,128)(2,1)S(1)} %get-tuple-element.6), channel_id=1, source_target_pairs={{0,4},{4,8},{8,12},{12,16},{16,20},{20,24},{24,28},{28,32},{32,36}... | collective-permute-start | bytes 64520 | tf_op jit(solution)/shard_map/ppermute | solution.py:19
  17.2 0.1 reduce.1
  17.3 9.4 %collective-permute-done = bf16[21,4,1,128]{3,2,1,0:T(2,128)(2,1)S(1)} collective-permute-done((bf16[21,4,1,128]{3,2,1,0:T(2,128)(2,1)S(1)}, bf16[21,4,1,128]{3,2,1,0:T(2,128)(2,1)S(1)}, u32[]{:S(2)}, u32[]{:S(2)}) %collective-permute-start) | collective-permute-done | bytes 21536 | tf_op jit(solution)/shard_map/ppermute | solution.py:19
  26.7 0.1 reduce
  26.9 0.0 copy-start.6
  26.9 0.4 concatenate.6.b0_ref
  27.3 3.4 %collective-permute-start.3 = (bf16[1512,128]{1,0:T(8,128)(2,1)S(1)}, bf16[1512,128]{1,0:T(8,128)(2,1)S(1)}, u32[]{:S(2)}, u32[]{:S(2)}) collective-permute-start(bf16[1512,128]{1,0:T(8,128)(2,1)S(1)} %concatenate.6.b0_ref), channel_id=1, source_target_pairs={{0,2},{1,3},{2,0},{3,1},{4,6},{5,7},{6,4},{7,5},{8,10},{9,11},{10,... | collective-permute-start | bytes 1161224 | tf_op jit(solution)/shard_map/ppermute | solution.py:130
  30.7 1.9 %collective-permute-start.2 = (bf16[1512,128]{1,0:T(8,128)(2,1)S(1)}, bf16[1512,128]{1,0:T(8,128)(2,1)S(1)}, u32[]{:S(2)}, u32[]{:S(2)}) collective-permute-start(bf16[1512,128]{1,0:T(8,128)(2,1)S(1)} %concatenate.6.b0_ref), channel_id=1, source_target_pairs={{0,1},{1,0},{2,3},{3,2},{4,5},{5,4},{6,7},{7,6},{8,9},{9,8},{10,11... | collective-permute-start | bytes 1161224 | tf_op jit(solution)/shard_map/ppermute | solution.py:129
  32.6 5.9 %collective-permute-done.3.b2_ref = bf16[1512,128]{1,0:T(8,128)(2,1)S(1)} collective-permute-done((bf16[1512,128]{1,0:T(8,128)(2,1)S(1)}, bf16[1512,128]{1,0:T(8,128)(2,1)S(1)}, u32[]{:S(2)}, u32[]{:S(2)}) %collective-permute-start.3) | collective-permute-done | bytes 387104 | tf_op jit(solution)/shard_map/ppermute | solution.py:130
  38.5 1.9 %collective-permute-start.4 = (bf16[1512,128]{1,0:T(8,128)(2,1)S(1)}, bf16[1512,128]{1,0:T(8,128)(2,1)S(1)}, u32[]{:S(2)}, u32[]{:S(2)}) collective-permute-start(bf16[1512,128]{1,0:T(8,128)(2,1)S(1)} %collective-permute-done.3.b2_ref), channel_id=1, source_target_pairs={{0,1},{1,0},{2,3},{3,2},{4,5},{5,4},{6,7},{7,6},{8,9},{9,8},{10,11... | collective-permute-start | bytes 1161224 | tf_op jit(solution)/shard_map/ppermute | solution.py:131
  40.5 0.0 copy-start.7
  40.5 0.7 %copy-done.7 = f32[7,3]{0,1:T(4,128)S(1)} copy-done((f32[7,3]{0,1:T(4,128)S(1)}, f32[7,3]{0,1:T(4,128)}, u32[]{:S(2)}) %copy-start.7) | copy-done | bytes 108
  41.1 0.1 copy.10.ct_ref
  41.2 0.1 constant_dynamic-slice_fusion.3
  41.4 0.0 copy-start
  41.4 0.0 copy-start.1
  41.4 0.0 copy-start.3
  41.4 0.0 copy-start.4
  41.4 0.1 fusion.6
  41.6 0.5 %collective-permute-done.4.b3_ref = bf16[1512,128]{1,0:T(8,128)(2,1)S(1)} collective-permute-done((bf16[1512,128]{1,0:T(8,128)(2,1)S(1)}, bf16[1512,128]{1,0:T(8,128)(2,1)S(1)}, u32[]{:S(2)}, u32[]{:S(2)}) %collective-permute-start.4) | collective-permute-done | bytes 387104 | tf_op jit(solution)/shard_map/ppermute | solution.py:131
  42.1 0.1 copy-done
  42.2 10.6 %shard_map.82 = bf16[21,4,16,128]{3,2,1,0:T(8,128)(2,1)} custom-call(bf16[1512,128]{1,0:T(8,128)(2,1)S(1)} %concatenate.6.b0_ref, bf16[1512,128]{1,0:T(8,128)(2,1)S(1)} %collective-permute-done.2.b1_ref, bf16[1512,128]{1,0:T(8,128)(2,1)S(1)} %collective-permute-done.3.b2_ref, bf16[1512,128]{1,0:T(8,128)(2,1)S(1)} %collective-permute-done.4.b3_ref, ...), custom_call_target="tpu_custom_call" | custom-call | tf_op jit(solution)/shard_map/pallas_call | solution.py:160
  (12 shorter events, 0.1 us)
Async XLA Ops:
  0.0 26.9 %copy-start.5 = (bf16[21,4,16,128]{3,2,1,0:T(8,128)(2,1)S(1)}, bf16[21,4,16,128]{3,2,1,0:T(8,128)(2,1)}, u32[]{:S(2)}) copy-start(bf16[21,4,16,128]{3,2,1,0:T(8,128)(2,1)} %param.8) | copy-start | bytes 1032196
  1.1 16.0 %collective-permute-start.1 = (bf16[21,4,1,128]{3,2,1,0:T(2,128)(2,1)S(1)}, bf16[21,4,1,128]{3,2,1,0:T(2,128)(2,1)S(1)}, u32[]{:S(2)}, u32[]{:S(2)}) collective-permute-start(bf16[21,4,1,128]{3,2,1,0:T(2,128)(2,1)S(1)} %get-tuple-element.5), channel_id=1, source_target_pairs={{4,0},{8,4},{12,8},{16,12},{20,16},{24,20},{28,24},{32,28},{36,32}... | collective-permute-start | bytes 64520 | tf_op jit(solution)/shard_map/ppermute | solution.py:20
  15.2 11.5 %collective-permute-start = (bf16[21,4,1,128]{3,2,1,0:T(2,128)(2,1)S(1)}, bf16[21,4,1,128]{3,2,1,0:T(2,128)(2,1)S(1)}, u32[]{:S(2)}, u32[]{:S(2)}) collective-permute-start(bf16[21,4,1,128]{3,2,1,0:T(2,128)(2,1)S(1)} %get-tuple-element.6), channel_id=1, source_target_pairs={{0,4},{4,8},{8,12},{12,16},{16,20},{20,24},{24,28},{28,32},{32,36}... | collective-permute-start | bytes 64520 | tf_op jit(solution)/shard_map/ppermute | solution.py:19
  26.9 14.4 %copy-start.6 = (bf16[7,84,84]{2,1,0:T(8,128)(2,1)S(1)}, bf16[7,84,84]{2,1,0:T(8,128)(2,1)}, u32[]{:S(2)}) copy-start(bf16[7,84,84]{2,1,0:T(8,128)(2,1)} %param.9) | copy-start | bytes 296356
  27.3 11.2 %collective-permute-start.3 = (bf16[1512,128]{1,0:T(8,128)(2,1)S(1)}, bf16[1512,128]{1,0:T(8,128)(2,1)S(1)}, u32[]{:S(2)}, u32[]{:S(2)}) collective-permute-start(bf16[1512,128]{1,0:T(8,128)(2,1)S(1)} %concatenate.6.b0_ref), channel_id=1, source_target_pairs={{0,2},{1,3},{2,0},{3,1},{4,6},{5,7},{6,4},{7,5},{8,10},{9,11},{10,... | collective-permute-start | bytes 1161224 | tf_op jit(solution)/shard_map/ppermute | solution.py:130
  30.7 10.9 %collective-permute-start.2 = (bf16[1512,128]{1,0:T(8,128)(2,1)S(1)}, bf16[1512,128]{1,0:T(8,128)(2,1)S(1)}, u32[]{:S(2)}, u32[]{:S(2)}) collective-permute-start(bf16[1512,128]{1,0:T(8,128)(2,1)S(1)} %concatenate.6.b0_ref), channel_id=1, source_target_pairs={{0,1},{1,0},{2,3},{3,2},{4,5},{5,4},{6,7},{7,6},{8,9},{9,8},{10,11... | collective-permute-start | bytes 1161224 | tf_op jit(solution)/shard_map/ppermute | solution.py:129
  38.5 3.6 %collective-permute-start.4 = (bf16[1512,128]{1,0:T(8,128)(2,1)S(1)}, bf16[1512,128]{1,0:T(8,128)(2,1)S(1)}, u32[]{:S(2)}, u32[]{:S(2)}) collective-permute-start(bf16[1512,128]{1,0:T(8,128)(2,1)S(1)} %collective-permute-done.3.b2_ref), channel_id=1, source_target_pairs={{0,1},{1,0},{2,3},{3,2},{4,5},{5,4},{6,7},{7,6},{8,9},{9,8},{10,11... | collective-permute-start | bytes 1161224 | tf_op jit(solution)/shard_map/ppermute | solution.py:131
  40.5 0.7 %copy-start.7 = (f32[7,3]{0,1:T(4,128)S(1)}, f32[7,3]{0,1:T(4,128)}, u32[]{:S(2)}) copy-start(f32[7,3]{0,1:T(4,128)} %param.14) | copy-start | bytes 256
  41.4 0.8 %copy-start = (f32[7,16,128]{2,1,0:T(8,128)S(1)}, f32[7,16,128]{2,1,0:T(8,128)}, u32[]{:S(2)}) copy-start(f32[7,16,128]{2,1,0:T(8,128)} %kl_ref.1) | copy-start | bytes 172036
  41.4 0.8 %copy-start.1 = (s32[16,128]{1,0:T(8,128)S(1)}, s32[16,128]{1,0:T(8,128)}, u32[]{:S(2)}) copy-start(s32[16,128]{1,0:T(8,128)} %mat_ref.1) | copy-start | bytes 24580
  41.4 0.8 %copy-start.2 = (s32[16,128]{1,0:T(8,128)S(1)}, s32[16,128]{1,0:T(8,128)}, u32[]{:S(2)}) copy-start(s32[16,128]{1,0:T(8,128)} %chr_ref.1) | copy-start | bytes 24580
  41.4 0.8 %copy-start.3 = (f32[7,8]{1,0:T(8,128)S(1)}, f32[7,8]{1,0:T(8,128)}, u32[]{:S(2)}) copy-start(f32[7,8]{1,0:T(8,128)} %mt_ref.1) | copy-start | bytes 676
  41.4 0.8 %copy-start.4 = (f32[7,8]{1,0:T(8,128)S(1)}, f32[7,8]{1,0:T(8,128)}, u32[]{:S(2)}) copy-start(f32[7,8]{1,0:T(8,128)} %et_ref.1) | copy-start | bytes 676

commit v3 on v2

--- a/solution.py
+++ b/solution.py
@@ -8,7 +8,8 @@
 from jax.sharding import PartitionSpec as P
 
 PAD_I = 24
-SLOT = 24
+JS = 73
+OS = 65
 
 
 def edge_rows(cells, axis, dim):
@@ -23,7 +24,7 @@
 
 def kernel(nmode, nfield, rows, width, terms, nmat, nchar,
            b0_ref, b1_ref, b2_ref, b3_ref, cp_ref, kl_ref, mat_ref, chr_ref,
-           mt_ref, ct_ref, et_ref, out_ref, fs, os, cs, es):
+           mt_ref, ct_ref, et_ref, out_ref, fs, hs, os, cs, es):
     nloc = out_ref.shape[0]
     blocks = (b0_ref, b1_ref, b2_ref, b3_ref)
     mat = mat_ref[...]
@@ -43,35 +44,31 @@
         es[k] = kl * ev
 
     per = nloc * nfield
+    core = nfield * rows
     for d, blk in enumerate(blocks):
-        def fill(jf, carry, blk=blk, d=d):
-            src = pl.multiple_of(jf * rows, rows)
-            dst = pl.multiple_of((d * per + jf) * SLOT, 8)
-            fs[pl.ds(dst, rows), :] = blk[pl.ds(src, rows), :].astype(jnp.float32)
-            return carry
-
-        lax.fori_loop(0, per, fill, 0, unroll=12)
-        halo = per * rows
-        fs[pl.ds(d * per * SLOT + rows, per, stride=SLOT), :] = blk[pl.ds(halo, per), :].astype(jnp.float32)
-        fs[pl.ds(d * per * SLOT + rows + 1, per, stride=SLOT), :] = blk[pl.ds(halo + per, per), :].astype(jnp.float32)
+        for jl in range(nloc):
+            j = d * nloc + jl
+            fs[pl.ds(j * JS, core), :] = blk[pl.ds(jl * core, core), :].astype(jnp.float32)
+        hs[...] = blk[pl.ds(nloc * core, 2 * per), :].astype(jnp.float32)
+        for side in range(2 * nfield):
+            fs[pl.ds(d * nloc * JS + core + side, nloc, stride=JS), :] = hs[pl.ds(side * nloc, nloc), :]
 
     lane = lax.broadcasted_iota(jnp.int32, (nmode, width), 1)
     first = lane == 0
     last = lane == width - 1
-    stride = nfield * SLOT
 
-    def row(f, r):
-        return fs[pl.ds(f * SLOT + r, nmode, stride=stride), :]
+    def row(r):
+        return fs[pl.ds(r, nmode, stride=JS), :]
 
     def step(x, carry):
-        up = jnp.where(x == 0, rows, x - 1)
-        down = jnp.where(x == rows - 1, rows + 1, x + 1)
         comps = []
         grads = None
         for f in range(nfield):
-            center = row(f, x)
-            above = row(f, up)
-            below = row(f, down)
+            up = jnp.where(x == 0, core + 2 * f, f * rows + x - 1)
+            down = jnp.where(x == rows - 1, core + 2 * f + 1, f * rows + x + 1)
+            center = row(f * rows + x)
+            above = row(up)
+            below = row(down)
             left = jnp.where(first, 0.0, pltpu.roll(center, 1, 1))
             right = jnp.where(last, 0.0, pltpu.roll(center, width - 1, 1))
             lap = 4.0 * center - above - below - left - right
@@ -96,17 +93,13 @@
                     part = evals[k] * mixed[k * PAD_I:(k + 1) * PAD_I, c * width:(c + 1) * width]
                     strain = part if strain is None else strain + part
                 diffuse = diffuse - strain
-            os[pl.ds(f * rows + x, PAD_I, stride=nfield * rows), :] = diffuse
+            os[pl.ds(f * rows + x, PAD_I, stride=OS), :] = diffuse
         return carry
 
     lax.fori_loop(0, rows, step, 0)
 
-    def emit(i, carry):
-        base = pl.multiple_of(i * nfield * rows, 8)
-        out_ref[i] = os[pl.ds(base, nfield * rows), :].reshape(nfield, rows, width).astype(out_ref.dtype)
-        return carry
-
-    lax.fori_loop(0, nloc, emit, 0)
+    for i in range(nloc):
+        out_ref[i] = os[pl.ds(i * OS, core), :].reshape(nfield, rows, width).astype(out_ref.dtype)
 
 
 def body(
@@ -121,8 +114,9 @@
     pack = jnp.concatenate(
         [
             fields.reshape(local_modes * nfield * rows, width),
-            above.reshape(local_modes * nfield, width),
-            below.reshape(local_modes * nfield, width),
+            jnp.stack([above[:, :, 0], below[:, :, 0]], axis=1)
+            .transpose(2, 1, 0, 3)
+            .reshape(2 * nfield * local_modes, width),
         ],
         axis=0,
     )
@@ -150,8 +144,9 @@
         in_specs=[vmem] * 8 + [smem] * 3,
         out_specs=vmem,
         scratch_shapes=[
-            pltpu.VMEM((total_modes * nfield * SLOT, width), jnp.float32),
-            pltpu.VMEM((PAD_I * nfield * rows, width), jnp.float32),
+            pltpu.VMEM((total_modes * JS, width), jnp.float32),
+            pltpu.VMEM((2 * local_modes * nfield, width), jnp.float32),
+            pltpu.VMEM((PAD_I * OS, width), jnp.float32),
             pltpu.VMEM((terms, rows, width), jnp.float32),
             pltpu.VMEM((terms, rows, width), jnp.float32),
         ],

time: 53.8 us -> 49.6 us (0.922)
  Pallas kernels: 10.6 us -> 7.21 us
    pallas_call x1, Pallas kernels: 10.6 us -> 7.21 us  [body(): run(pack, partner, counter, diagonal, weights, kl_field, material, char_s...]
where the time goes in v3:
time: 49.6 us; the launch traced here: 48.7 us
  starting transfers between devices  23.4 us (47%)
  waiting for transfers between devices  15.5 us (31%)
  Pallas kernels  7.21 us (15%)
  local copies, waits for them, and re-layouts  2.21 us (4%)
    ppermute x1, starting transfers between devices, edge_rows(): lax.ppermute(head, axis, [((i + 1) % count, i) for i in range(ends)])  14.1 us
    ppermute x1, waiting for transfers between devices, edge_rows(): lax.ppermute(tail, axis, [(i, (i + 1) % count) for i in range(ends)])  9.07 us
    pallas_call x1, Pallas kernels, body(): run(pack, partner, counter, diagonal, weights, kl_field, material, char_s...  7.21 us
    ppermute x1, waiting for transfers between devices, body(): counter = lax.ppermute(pack, 'modes', [(i, i ^ 2) for i in range(groups)])  5.87 us
    ppermute x1, starting transfers between devices, body(): counter = lax.ppermute(pack, 'modes', [(i, i ^ 2) for i in range(groups)])  3.51 us
    ppermute x1, starting transfers between devices, edge_rows(): lax.ppermute(tail, axis, [(i, (i + 1) % count) for i in range(ends)])  1.92 us
    ppermute x1, starting transfers between devices, body(): partner = lax.ppermute(pack, 'modes', [(i, i ^ 1) for i in range(groups)])  1.92 us
    ppermute x1, starting transfers between devices, body(): lax.ppermute(counter, 'modes', [(i, i ^ 1) for i in range(groups)])  1.91 us
  transfers between devices with their start and end apart: 5, of which 3 were waited for; matrix products, arithmetic and copies ran while one was open for 1% of the time, Pallas kernels for 0%

profile of v3, /device:TPU:6, one launch (start us, length us, event | category | flops | bytes accessed | tf_op | source)
XLA Modules:
  0.0 48.7 jit_solution(15893350924456998827)
XLA Ops:
  0.0 1.1 %fusion.7 = (bf16[21,4,1,128]{3,2,1,0:T(2,128)(2,1)S(1)}, bf16[21,4,1,128]{3,2,1,0:T(2,128)(2,1)S(1)}) fusion(bf16[21,4,16,128]{3,2,1,0:T(8,128)(2,1)} %param.8), kind=kLoop, calls=%fused_computation.15 | loop fusion | bytes 86016 | tf_op jit(solution)/shard_map/slice | solution.py:19
  1.1 14.1 %collective-permute-start.1 = (bf16[21,4,1,128]{3,2,1,0:T(2,128)(2,1)S(1)}, bf16[21,4,1,128]{3,2,1,0:T(2,128)(2,1)S(1)}, u32[]{:S(2)}, u32[]{:S(2)}) collective-permute-start(bf16[21,4,1,128]{3,2,1,0:T(2,128)(2,1)S(1)} %get-tuple-element.6), channel_id=1, source_target_pairs={{4,0},{8,4},{12,8},{16,12},{20,16},{24,20},{28,24},{32,28},{36,32}... | collective-permute-start | bytes 64520 | tf_op jit(solution)/shard_map/ppermute | solution.py:21
  15.3 1.9 %collective-permute-start = (bf16[21,4,1,128]{3,1,0,2:T(4,128)(2,1)S(1)}, bf16[21,4,1,128]{3,1,0,2:T(4,128)(2,1)S(1)}, u32[]{:S(2)}, u32[]{:S(2)}) collective-permute-start(bf16[21,4,1,128]{3,1,0,2:T(4,128)(2,1)S(1)} %copy.16), channel_id=1, source_target_pairs={{0,4},{4,8},{8,12},{12,16},{16,20},{20,24},{24,28},{28,32},{32,36}... | collective-permute-start | bytes 64520 | tf_op jit(solution)/shard_map/ppermute | solution.py:20
  17.2 0.0 collective-permute-done.1
  17.2 9.1 %collective-permute-done = bf16[21,4,1,128]{3,1,0,2:T(4,128)(2,1)S(1)} collective-permute-done((bf16[21,4,1,128]{3,1,0,2:T(4,128)(2,1)S(1)}, bf16[21,4,1,128]{3,1,0,2:T(4,128)(2,1)S(1)}, u32[]{:S(2)}, u32[]{:S(2)}) %collective-permute-start) | collective-permute-done | bytes 21536 | tf_op jit(solution)/shard_map/ppermute | solution.py:20
  26.4 0.0 copy-start.6
  26.4 3.5 %collective-permute-start.3 = (bf16[1512,128]{1,0:T(8,128)(2,1)S(1)}, bf16[1512,128]{1,0:T(8,128)(2,1)S(1)}, u32[]{:S(2)}, u32[]{:S(2)}) collective-permute-start(bf16[1512,128]{1,0:T(8,128)(2,1)S(1)} %pad_maximum_fusion.b0_ref), channel_id=1, source_target_pairs={{0,2},{1,3},{2,0},{3,1},{4,6},{5,7},{6,4},{7,5},{8,10},{9,11},{10,... | collective-permute-start | bytes 1161224 | tf_op jit(solution)/shard_map/ppermute | solution.py:124
  30.0 1.9 %collective-permute-start.2 = (bf16[1512,128]{1,0:T(8,128)(2,1)S(1)}, bf16[1512,128]{1,0:T(8,128)(2,1)S(1)}, u32[]{:S(2)}, u32[]{:S(2)}) collective-permute-start(bf16[1512,128]{1,0:T(8,128)(2,1)S(1)} %pad_maximum_fusion.b0_ref), channel_id=1, source_target_pairs={{0,1},{1,0},{2,3},{3,2},{4,5},{5,4},{6,7},{7,6},{8,9},{9,8},{10,11... | collective-permute-start | bytes 1161224 | tf_op jit(solution)/shard_map/ppermute | solution.py:123
  31.9 5.9 %collective-permute-done.3.b2_ref = bf16[1512,128]{1,0:T(8,128)(2,1)S(1)} collective-permute-done((bf16[1512,128]{1,0:T(8,128)(2,1)S(1)}, bf16[1512,128]{1,0:T(8,128)(2,1)S(1)}, u32[]{:S(2)}, u32[]{:S(2)}) %collective-permute-start.3) | collective-permute-done | bytes 387104 | tf_op jit(solution)/shard_map/ppermute | solution.py:124
  37.8 1.9 %collective-permute-start.4 = (bf16[1512,128]{1,0:T(8,128)(2,1)S(1)}, bf16[1512,128]{1,0:T(8,128)(2,1)S(1)}, u32[]{:S(2)}, u32[]{:S(2)}) collective-permute-start(bf16[1512,128]{1,0:T(8,128)(2,1)S(1)} %collective-permute-done.3.b2_ref), channel_id=1, source_target_pairs={{0,1},{1,0},{2,3},{3,2},{4,5},{5,4},{6,7},{7,6},{8,9},{9,8},{10,11... | collective-permute-start | bytes 1161224 | tf_op jit(solution)/shard_map/ppermute | solution.py:125
  39.7 0.0 copy-start.7
  39.7 0.7 %copy-done.7 = f32[7,3]{0,1:T(4,128)S(1)} copy-done((f32[7,3]{0,1:T(4,128)S(1)}, f32[7,3]{0,1:T(4,128)}, u32[]{:S(2)}) %copy-start.7) | copy-done | bytes 108
  40.4 0.1 copy.14.ct_ref
  40.5 0.1 constant_dynamic-slice_fusion.3
  40.6 0.0 copy-start
  40.6 0.0 copy-start.1
  40.6 0.0 copy-start.2
  40.7 0.0 copy-start.3
  40.7 0.0 copy-start.4
  40.7 0.1 fusion.6
  40.8 0.0 collective-permute-done.2.b1_ref
  40.8 0.5 %collective-permute-done.4.b3_ref = bf16[1512,128]{1,0:T(8,128)(2,1)S(1)} collective-permute-done((bf16[1512,128]{1,0:T(8,128)(2,1)S(1)}, bf16[1512,128]{1,0:T(8,128)(2,1)S(1)}, u32[]{:S(2)}, u32[]{:S(2)}) %collective-permute-start.4) | collective-permute-done | bytes 387104 | tf_op jit(solution)/shard_map/ppermute | solution.py:125
  41.3 0.1 copy-done
  41.5 7.2 %shard_map.82 = bf16[21,4,16,128]{3,2,1,0:T(8,128)(2,1)} custom-call(bf16[1512,128]{1,0:T(8,128)(2,1)S(1)} %pad_maximum_fusion.b0_ref, bf16[1512,128]{1,0:T(8,128)(2,1)S(1)} %collective-permute-done.2.b1_ref, bf16[1512,128]{1,0:T(8,128)(2,1)S(1)} %collective-permute-done.3.b2_ref, bf16[1512,128]{1,0:T(8,128)(2,1)S(1)} %collective-permute-done.4.b3_ref, ...), custom_call_target="tpu_custom_call" | custom-call | tf_op jit(solution)/shard_map/pallas_call | solution.py:155
  (13 shorter events, 0.1 us)
Async XLA Ops:
  0.0 26.4 %copy-start.5 = (bf16[21,4,16,128]{3,2,1,0:T(8,128)(2,1)S(1)}, bf16[21,4,16,128]{3,2,1,0:T(8,128)(2,1)}, u32[]{:S(2)}) copy-start(bf16[21,4,16,128]{3,2,1,0:T(8,128)(2,1)} %param.8) | copy-start | bytes 1032196
  1.1 16.1 %collective-permute-start.1 = (bf16[21,4,1,128]{3,2,1,0:T(2,128)(2,1)S(1)}, bf16[21,4,1,128]{3,2,1,0:T(2,128)(2,1)S(1)}, u32[]{:S(2)}, u32[]{:S(2)}) collective-permute-start(bf16[21,4,1,128]{3,2,1,0:T(2,128)(2,1)S(1)} %get-tuple-element.6), channel_id=1, source_target_pairs={{4,0},{8,4},{12,8},{16,12},{20,16},{24,20},{28,24},{32,28},{36,32}... | collective-permute-start | bytes 64520 | tf_op jit(solution)/shard_map/ppermute | solution.py:21
  15.3 11.0 %collective-permute-start = (bf16[21,4,1,128]{3,1,0,2:T(4,128)(2,1)S(1)}, bf16[21,4,1,128]{3,1,0,2:T(4,128)(2,1)S(1)}, u32[]{:S(2)}, u32[]{:S(2)}) collective-permute-start(bf16[21,4,1,128]{3,1,0,2:T(4,128)(2,1)S(1)} %copy.16), channel_id=1, source_target_pairs={{0,4},{4,8},{8,12},{12,16},{16,20},{20,24},{24,28},{28,32},{32,36}... | collective-permute-start | bytes 64520 | tf_op jit(solution)/shard_map/ppermute | solution.py:20
  26.4 14.1 %copy-start.6 = (bf16[7,84,84]{2,1,0:T(8,128)(2,1)S(1)}, bf16[7,84,84]{2,1,0:T(8,128)(2,1)}, u32[]{:S(2)}) copy-start(bf16[7,84,84]{2,1,0:T(8,128)(2,1)} %param.9) | copy-start | bytes 296356
  26.4 11.3 %collective-permute-start.3 = (bf16[1512,128]{1,0:T(8,128)(2,1)S(1)}, bf16[1512,128]{1,0:T(8,128)(2,1)S(1)}, u32[]{:S(2)}, u32[]{:S(2)}) collective-permute-start(bf16[1512,128]{1,0:T(8,128)(2,1)S(1)} %pad_maximum_fusion.b0_ref), channel_id=1, source_target_pairs={{0,2},{1,3},{2,0},{3,1},{4,6},{5,7},{6,4},{7,5},{8,10},{9,11},{10,... | collective-permute-start | bytes 1161224 | tf_op jit(solution)/shard_map/ppermute | solution.py:124
  30.0 10.8 %collective-permute-start.2 = (bf16[1512,128]{1,0:T(8,128)(2,1)S(1)}, bf16[1512,128]{1,0:T(8,128)(2,1)S(1)}, u32[]{:S(2)}, u32[]{:S(2)}) collective-permute-start(bf16[1512,128]{1,0:T(8,128)(2,1)S(1)} %pad_maximum_fusion.b0_ref), channel_id=1, source_target_pairs={{0,1},{1,0},{2,3},{3,2},{4,5},{5,4},{6,7},{7,6},{8,9},{9,8},{10,11... | collective-permute-start | bytes 1161224 | tf_op jit(solution)/shard_map/ppermute | solution.py:123
  37.8 3.6 %collective-permute-start.4 = (bf16[1512,128]{1,0:T(8,128)(2,1)S(1)}, bf16[1512,128]{1,0:T(8,128)(2,1)S(1)}, u32[]{:S(2)}, u32[]{:S(2)}) collective-permute-start(bf16[1512,128]{1,0:T(8,128)(2,1)S(1)} %collective-permute-done.3.b2_ref), channel_id=1, source_target_pairs={{0,1},{1,0},{2,3},{3,2},{4,5},{5,4},{6,7},{7,6},{8,9},{9,8},{10,11... | collective-permute-start | bytes 1161224 | tf_op jit(solution)/shard_map/ppermute | solution.py:125
  39.7 0.7 %copy-start.7 = (f32[7,3]{0,1:T(4,128)S(1)}, f32[7,3]{0,1:T(4,128)}, u32[]{:S(2)}) copy-start(f32[7,3]{0,1:T(4,128)} %param.14) | copy-start | bytes 256
  40.6 0.8 %copy-start = (f32[7,16,128]{2,1,0:T(8,128)S(1)}, f32[7,16,128]{2,1,0:T(8,128)}, u32[]{:S(2)}) copy-start(f32[7,16,128]{2,1,0:T(8,128)} %kl_ref.1) | copy-start | bytes 172036
  40.6 0.8 %copy-start.1 = (s32[16,128]{1,0:T(8,128)S(1)}, s32[16,128]{1,0:T(8,128)}, u32[]{:S(2)}) copy-start(s32[16,128]{1,0:T(8,128)} %mat_ref.1) | copy-start | bytes 24580
  40.6 0.8 %copy-start.2 = (s32[16,128]{1,0:T(8,128)S(1)}, s32[16,128]{1,0:T(8,128)}, u32[]{:S(2)}) copy-start(s32[16,128]{1,0:T(8,128)} %chr_ref.1) | copy-start | bytes 24580
  40.7 0.8 %copy-start.3 = (f32[7,8]{1,0:T(8,128)S(1)}, f32[7,8]{1,0:T(8,128)}, u32[]{:S(2)}) copy-start(f32[7,8]{1,0:T(8,128)} %mt_ref.1) | copy-start | bytes 676
  40.7 0.8 %copy-start.4 = (f32[7,8]{1,0:T(8,128)S(1)}, f32[7,8]{1,0:T(8,128)}, u32[]{:S(2)}) copy-start(f32[7,8]{1,0:T(8,128)} %et_ref.1) | copy-start | bytes 676

commit v4 on v3

--- a/solution.py
+++ b/solution.py
@@ -6,6 +6,7 @@
 from jax.experimental import pallas as pl
 from jax.experimental.pallas import tpu as pltpu
 from jax.sharding import PartitionSpec as P
+
 
 PAD_I = 24
 JS = 73
@@ -22,29 +23,37 @@
     return above, below
 
 
-def kernel(nmode, nfield, rows, width, terms, nmat, nchar,
-           b0_ref, b1_ref, b2_ref, b3_ref, cp_ref, kl_ref, mat_ref, chr_ref,
-           mt_ref, ct_ref, et_ref, out_ref, fs, hs, os, cs, es):
-    nloc = out_ref.shape[0]
-    blocks = (b0_ref, b1_ref, b2_ref, b3_ref)
-    mat = mat_ref[...]
-    chs = chr_ref[...]
-    for k in range(terms):
-        mv = jnp.zeros((rows, width), jnp.float32)
-        ev = jnp.zeros((rows, width), jnp.float32)
-        for m in range(nmat):
-            hit = mat == m
-            mv = jnp.where(hit, mt_ref[k, m], mv)
-            ev = jnp.where(hit, et_ref[k, m], ev)
-        cv = jnp.zeros((rows, width), jnp.float32)
-        for q in range(nchar):
-            cv = jnp.where(chs == q, ct_ref[k, q], cv)
-        kl = kl_ref[k]
-        cs[k] = kl * mv * cv
-        es[k] = kl * ev
-
+def kernel(nblock, final, nfield, rows, width, terms, nmat, nchar, *refs):
+    blocks = refs[:nblock]
+    if final:
+        prev_ref, cp_ref, kl_ref, mat_ref, chr_ref, mt_ref, ct_ref, et_ref = refs[nblock:nblock + 8]
+        out_ref, fs, hs, os, cs, es = refs[nblock + 8:]
+        nloc = out_ref.shape[0]
+    else:
+        out_ref, fs, hs = refs[nblock:]
+    nloc = blocks[0].shape[0] // (nfield * (rows + 2))
+    nmode = nblock * nloc
+    span = fs.shape[0] // JS
+    core = nfield * rows
     per = nloc * nfield
-    core = nfield * rows
+
+    if final:
+        mat = mat_ref[...]
+        chs = chr_ref[...]
+        for k in range(terms):
+            mv = jnp.zeros((rows, width), jnp.float32)
+            ev = jnp.zeros((rows, width), jnp.float32)
+            for m in range(nmat):
+                hit = mat == m
+                mv = jnp.where(hit, mt_ref[k, m], mv)
+                ev = jnp.where(hit, et_ref[k, m], ev)
+            cv = jnp.zeros((rows, width), jnp.float32)
+            for q in range(nchar):
+                cv = jnp.where(chs == q, ct_ref[k, q], cv)
+            kl = kl_ref[k]
+            cs[k] = kl * mv * cv
+            es[k] = kl * ev
+
     for d, blk in enumerate(blocks):
         for jl in range(nloc):
             j = d * nloc + jl
@@ -52,15 +61,17 @@
         hs[...] = blk[pl.ds(nloc * core, 2 * per), :].astype(jnp.float32)
         for side in range(2 * nfield):
             fs[pl.ds(d * nloc * JS + core + side, nloc, stride=JS), :] = hs[pl.ds(side * nloc, nloc), :]
-
-    lane = lax.broadcasted_iota(jnp.int32, (nmode, width), 1)
+    if span > nmode:
+        fs[pl.ds(nmode * JS, (span - nmode) * JS), :] = jnp.zeros(((span - nmode) * JS, width), jnp.float32)
+
+    lane = lax.broadcasted_iota(jnp.int32, (span, width), 1)
     first = lane == 0
     last = lane == width - 1
 
     def row(r):
-        return fs[pl.ds(r, nmode, stride=JS), :]
-
-    def step(x, carry):
+        return fs[pl.ds(r, span, stride=JS), :]
+
+    def derive(x):
         comps = []
         grads = None
         for f in range(nfield):
@@ -77,7 +88,18 @@
                 gx = 0.5 * (below - above)
                 gy = 0.5 * (right - left)
                 grads = (gx.astype(jnp.bfloat16), gy.astype(jnp.bfloat16))
-        operand = jnp.concatenate(comps + list(grads), axis=1)
+        return jnp.concatenate(comps + list(grads), axis=1)
+
+    if not final:
+        def keep(x, carry):
+            out_ref[x] = derive(x)
+            return carry
+
+        lax.fori_loop(0, rows, keep, 0, unroll=8)
+        return
+
+    def step(x, carry):
+        operand = jnp.concatenate([prev_ref[x], derive(x)], axis=0)
         mixed = jnp.dot(cp_ref[...], operand, preferred_element_type=jnp.float32)
         cvals = [jnp.broadcast_to(cs[k, pl.ds(x, 1), :], (PAD_I, width)) for k in range(terms)]
         evals = [jnp.broadcast_to(es[k, pl.ds(x, 1), :], (PAD_I, width)) for k in range(terms)]
@@ -96,9 +118,9 @@
             os[pl.ds(f * rows + x, PAD_I, stride=OS), :] = diffuse
         return carry
 
-    lax.fori_loop(0, rows, step, 0)
-
-    for i in range(nloc):
+    lax.fori_loop(0, rows, step, 0, unroll=16)
+
+    for i in range(out_ref.shape[0]):
         out_ref[i] = os[pl.ds(i * OS, core), :].reshape(nfield, rows, width).astype(out_ref.dtype)
 
 
@@ -134,37 +156,54 @@
         axis=2,
     )
     weights = jnp.pad(weights, ((0, 0), (0, PAD_I - local_modes), (0, 0)))
-    weights = weights.reshape(terms * PAD_I, total_modes)
     vmem = pl.BlockSpec(memory_space=pltpu.VMEM)
     smem = pl.BlockSpec(memory_space=pltpu.SMEM)
-    run = pl.pallas_call(
-        functools.partial(kernel, total_modes, nfield, rows, width, terms,
+    half = groups // 2
+    span = -(-half * local_modes // 16) * 16
+    tables = (kl_field, material, char_state, material_table, char_table, expansion_table)
+    gap = span - half * local_modes
+    weights = weights.reshape(terms, PAD_I, total_modes)
+    zeros = jnp.zeros((terms, PAD_I, gap), weights.dtype)
+    cols = jnp.concatenate(
+        [weights[:, :, : half * local_modes], zeros, weights[:, :, half * local_modes:], zeros], axis=2
+    ).reshape(terms * PAD_I, 2 * span)
+    comps = nfield + 2
+    scratch = [
+        pltpu.VMEM((span * JS, width), jnp.float32),
+        pltpu.VMEM((2 * local_modes * nfield, width), jnp.float32),
+    ]
+    params = pltpu.CompilerParams(vmem_limit_bytes=48 * 1024 * 1024)
+
+    ops = pl.pallas_call(
+        functools.partial(kernel, half, False, nfield, rows, width, terms,
+                          material_table.shape[1], char_table.shape[1]),
+        out_shape=jax.ShapeDtypeStruct((rows, span, comps * width), jnp.bfloat16),
+        in_specs=[vmem] * half,
+        out_specs=vmem,
+        scratch_shapes=scratch,
+        compiler_params=params,
+        cost_estimate=pl.CostEstimate(
+            flops=12 * span * comps * rows * width, transcendentals=0,
+            bytes_accessed=half * pack.size * 2 + rows * span * comps * width * 2,
+        ),
+    )(pack, partner)
+    return pl.pallas_call(
+        functools.partial(kernel, half, True, nfield, rows, width, terms,
                           material_table.shape[1], char_table.shape[1]),
         out_shape=jax.ShapeDtypeStruct(fields.shape, fields.dtype),
-        in_specs=[vmem] * 8 + [smem] * 3,
+        in_specs=[vmem] * (half + 5) + [smem] * 3,
         out_specs=vmem,
-        scratch_shapes=[
-            pltpu.VMEM((total_modes * JS, width), jnp.float32),
-            pltpu.VMEM((2 * local_modes * nfield, width), jnp.float32),
+        scratch_shapes=scratch + [
             pltpu.VMEM((PAD_I * OS, width), jnp.float32),
             pltpu.VMEM((terms, rows, width), jnp.float32),
             pltpu.VMEM((terms, rows, width), jnp.float32),
         ],
-        compiler_params=pltpu.CompilerParams(vmem_limit_bytes=48 * 1024 * 1024),
-    )
-    return run(
-        pack,
-        partner,
-        counter,
-        diagonal,
-        weights,
-        kl_field,
-        material,
-        char_state,
-        material_table,
-        char_table,
-        expansion_table,
-    )
+        compiler_params=params,
+        cost_estimate=pl.CostEstimate(
+            flops=2 * terms * PAD_I * 2 * span * comps * rows * width, transcendentals=0,
+            bytes_accessed=half * pack.size * 2 + rows * span * comps * width * 2 + fields.size * 2,
+        ),
+    )(counter, diagonal, ops, cols, *tables)
 
 
 def solution(mesh):

time: 49.6 us -> 46.3 us (0.933)
  Pallas kernels: 7.21 us -> 4.28 us
  other arithmetic: 0.18 us -> 1.26 us
  waiting for transfers between devices: 15.5 us -> 14.8 us
  local copies, waits for them, and re-layouts: 2.21 us -> 1.53 us
    pallas_call x1 -> x2, Pallas kernels: 7.21 us -> 4.28 us  [the longest x1 3.12 us: body(): pl.pallas_call(functools.partial(kernel, half, True, nfield, rows, width,...]
    concatenate x1, other arithmetic: 0.03 us -> 1.01 us  [body(): jnp.concatenate([fields.reshape(local_modes * nfield * rows, width), jnp....]
    unnamed x19 -> x17, local copies, waits for them, and re-layouts: 0.92 us -> 0.15 us
    ppermute x1, waiting for transfers between devices: 0.54 us -> 0.01 us  [body(): lax.ppermute(counter, 'modes', [(i, i ^ 1) for i in range(groups)])]
  transfers between devices with their start and end apart: 5 -> 5, of which waited for: 3 -> 2; matrix products, arithmetic and copies ran while one was open for 1% -> 1% of each run, Pallas kernels for 0% -> 3%
where the time goes in v4:
time: 46.3 us; the launch traced here: 45.3 us
  starting transfers between devices  23.2 us (50%)
  waiting for transfers between devices  14.8 us (32%)
  Pallas kernels  4.28 us (9%)
  local copies, waits for them, and re-layouts  1.53 us (3%)
  other arithmetic  1.26 us (3%)
    ppermute x1, starting transfers between devices, edge_rows(): lax.ppermute(head, axis, [((i + 1) % count, i) for i in range(ends)])  14.1 us
    ppermute x1, waiting for transfers between devices, edge_rows(): lax.ppermute(tail, axis, [(i, (i + 1) % count) for i in range(ends)])  9.07 us
    ppermute x1, waiting for transfers between devices, body(): counter = lax.ppermute(pack, 'modes', [(i, i ^ 2) for i in range(groups)])  5.68 us
    ppermute x1, starting transfers between devices, body(): counter = lax.ppermute(pack, 'modes', [(i, i ^ 2) for i in range(groups)])  3.38 us
    pallas_call x1, Pallas kernels, body(): pl.pallas_call(functools.partial(kernel, half, True, nfield, rows, width,...  3.12 us
    ppermute x1, starting transfers between devices, body(): partner = lax.ppermute(pack, 'modes', [(i, i ^ 1) for i in range(groups)])  1.92 us
    ppermute x1, starting transfers between devices, edge_rows(): lax.ppermute(tail, axis, [(i, (i + 1) % count) for i in range(ends)])  1.92 us
    ppermute x1, starting transfers between devices, body(): lax.ppermute(counter, 'modes', [(i, i ^ 1) for i in range(groups)])  1.91 us
  transfers between devices with their start and end apart: 5, of which 2 were waited for; matrix products, arithmetic and copies ran while one was open for 1% of the time, Pallas kernels for 3%

profile of v4, /device:TPU:6, one launch (start us, length us, event | category | flops | bytes accessed | tf_op | source)
XLA Modules:
  0.0 45.3 jit_solution(4270357424302941931)
XLA Ops:
  0.0 1.1 %fusion.7 = (bf16[21,4,1,128]{3,2,1,0:T(2,128)(2,1)S(1)}, bf16[21,4,1,128]{3,2,1,0:T(2,128)(2,1)S(1)}) fusion(bf16[21,4,16,128]{3,2,1,0:T(8,128)(2,1)} %param.8), kind=kLoop, calls=%fused_computation.16 | loop fusion | bytes 86016 | tf_op jit(solution)/shard_map/slice | solution.py:20
  1.1 14.1 %collective-permute-start.1 = (bf16[21,4,1,128]{3,2,1,0:T(2,128)(2,1)S(1)}, bf16[21,4,1,128]{3,2,1,0:T(2,128)(2,1)S(1)}, u32[]{:S(2)}, u32[]{:S(2)}) collective-permute-start(bf16[21,4,1,128]{3,2,1,0:T(2,128)(2,1)S(1)} %get-tuple-element.6), channel_id=1, source_target_pairs={{4,0},{8,4},{12,8},{16,12},{20,16},{24,20},{28,24},{32,28},{36,32}... | collective-permute-start | bytes 64520 | tf_op jit(solution)/shard_map/ppermute | solution.py:22
  15.2 1.9 %collective-permute-start = (bf16[21,4,1,128]{3,1,0,2:T(4,128)(2,1)S(1)}, bf16[21,4,1,128]{3,1,0,2:T(4,128)(2,1)S(1)}, u32[]{:S(2)}, u32[]{:S(2)}) collective-permute-start(bf16[21,4,1,128]{3,1,0,2:T(4,128)(2,1)S(1)} %copy.16), channel_id=1, source_target_pairs={{0,4},{4,8},{8,12},{12,16},{16,20},{20,24},{24,28},{28,32},{32,36}... | collective-permute-start | bytes 64520 | tf_op jit(solution)/shard_map/ppermute | solution.py:21
  17.2 0.0 collective-permute-done.1
  17.2 9.1 %collective-permute-done = bf16[21,4,1,128]{3,1,0,2:T(4,128)(2,1)S(1)} collective-permute-done((bf16[21,4,1,128]{3,1,0,2:T(4,128)(2,1)S(1)}, bf16[21,4,1,128]{3,1,0,2:T(4,128)(2,1)S(1)}, u32[]{:S(2)}, u32[]{:S(2)}) %collective-permute-start) | collective-permute-done | bytes 21536 | tf_op jit(solution)/shard_map/ppermute | solution.py:21
  26.4 1.0 %pad_maximum_fusion.refs_0_ = bf16[1512,128]{1,0:T(8,128)(2,1)S(1)} fusion(bf16[168,128]{1,0:T(8,128)(2,1)S(1)} %reshape.10, bf16[1344,128]{1,0:T(8,128)(2,1)} %bitcast.9), kind=kLoop, calls=%fused_computation | loop fusion | flops 774144 | bytes 774144 | tf_op jit(solution)/shard_map/concatenate | solution.py:136
  27.4 3.4 %collective-permute-start.2 = (bf16[1512,128]{1,0:T(8,128)(2,1)S(1)}, bf16[1512,128]{1,0:T(8,128)(2,1)S(1)}, u32[]{:S(2)}, u32[]{:S(2)}) collective-permute-start(bf16[1512,128]{1,0:T(8,128)(2,1)S(1)} %pad_maximum_fusion.refs_0_), channel_id=1, source_target_pairs={{0,2},{1,3},{2,0},{3,1},{4,6},{5,7},{6,4},{7,5},{8,10},{9,11},{10,... | collective-permute-start | bytes 1161224 | tf_op jit(solution)/shard_map/ppermute | solution.py:146
  30.8 0.1 constant_dynamic-slice_fusion.3
  31.0 1.9 %collective-permute-start.4 = (bf16[1512,128]{1,0:T(8,128)(2,1)S(1)}, bf16[1512,128]{1,0:T(8,128)(2,1)S(1)}, u32[]{:S(2)}, u32[]{:S(2)}) collective-permute-start(bf16[1512,128]{1,0:T(8,128)(2,1)S(1)} %pad_maximum_fusion.refs_0_), channel_id=1, source_target_pairs={{0,1},{1,0},{2,3},{3,2},{4,5},{5,4},{6,7},{7,6},{8,9},{9,8},{10,11... | collective-permute-start | bytes 1161224 | tf_op jit(solution)/shard_map/ppermute | solution.py:145
  32.9 5.7 %collective-permute-done.2.refs_0_ = bf16[1512,128]{1,0:T(8,128)(2,1)S(1)} collective-permute-done((bf16[1512,128]{1,0:T(8,128)(2,1)S(1)}, bf16[1512,128]{1,0:T(8,128)(2,1)S(1)}, u32[]{:S(2)}, u32[]{:S(2)}) %collective-permute-start.2) | collective-permute-done | bytes 387104 | tf_op jit(solution)/shard_map/ppermute | solution.py:146
  38.6 1.9 %collective-permute-start.3 = (bf16[1512,128]{1,0:T(8,128)(2,1)S(1)}, bf16[1512,128]{1,0:T(8,128)(2,1)S(1)}, u32[]{:S(2)}, u32[]{:S(2)}) collective-permute-start(bf16[1512,128]{1,0:T(8,128)(2,1)S(1)} %collective-permute-done.2.refs_0_), channel_id=1, source_target_pairs={{0,1},{1,0},{2,3},{3,2},{4,5},{5,4},{6,7},{7,6},{8,9},{9,8},{10,11... | collective-permute-start | bytes 1161224 | tf_op jit(solution)/shard_map/ppermute | solution.py:147
  40.5 0.1 fusion.6
  40.6 0.0 copy-start
  40.6 0.0 copy-start.1
  40.6 0.0 copy-start.2
  40.6 0.0 copy-start.3
  40.7 0.0 copy-start.4
  40.7 0.1 copy.14.refs_8_
  40.8 0.1 fusion.8
  40.9 0.1 pad_maximum_fusion.1
  41.0 0.0 collective-permute-done.4.refs_1_
  41.0 1.2 %shard_map.82.refs_2_ = bf16[16,48,768]{2,1,0:T(8,128)(2,1)S(1)} custom-call(bf16[1512,128]{1,0:T(8,128)(2,1)S(1)} %pad_maximum_fusion.refs_0_, bf16[1512,128]{1,0:T(8,128)(2,1)S(1)} %collective-permute-done.4.refs_1_), custom_call_target="tpu_custom_call" | custom-call | flops 7077888 | bytes 1953792 | tf_op jit(solution)/shard_map/pallas_call | solution.py:177
  42.2 0.0 collective-permute-done.3.refs_1_
  42.2 3.1 %shard_map.83 = bf16[21,4,16,128]{3,2,1,0:T(8,128)(2,1)} custom-call(bf16[1512,128]{1,0:T(8,128)(2,1)S(1)} %collective-permute-done.2.refs_0_, bf16[1512,128]{1,0:T(8,128)(2,1)S(1)} %collective-permute-done.3.refs_1_, bf16[16,48,768]{2,1,0:T(8,128)(2,1)S(1)} %shard_map.82.refs_2_, bf16[168,96]{1,0:T(8,128)(2,1)S(1)} %bitcast.8, f32[7,16,128]{2,1,0:T(8,128)S(1)} %copy-done, ...), custom_call_target="tpu_custom_call" | custom-call | flops 396361728 | bytes 2297856 | tf_op jit(solution)/shard_map/pallas_call | solution.py:190
  (15 shorter events, 0.1 us)
Async XLA Ops:
  0.0 30.8 %copy-start.5 = (bf16[7,84,84]{2,1,0:T(8,128)(2,1)S(1)}, bf16[7,84,84]{2,1,0:T(8,128)(2,1)}, u32[]{:S(2)}) copy-start(bf16[7,84,84]{2,1,0:T(8,128)(2,1)} %param.9) | copy-start | bytes 296356
  0.0 40.6 %copy-start.6 = (f32[7,3]{0,1:T(4,128)S(1)}, f32[7,3]{0,1:T(4,128)}, u32[]{:S(2)}) copy-start(f32[7,3]{0,1:T(4,128)} %param.14) | copy-start | bytes 256
  1.1 16.1 %collective-permute-start.1 = (bf16[21,4,1,128]{3,2,1,0:T(2,128)(2,1)S(1)}, bf16[21,4,1,128]{3,2,1,0:T(2,128)(2,1)S(1)}, u32[]{:S(2)}, u32[]{:S(2)}) collective-permute-start(bf16[21,4,1,128]{3,2,1,0:T(2,128)(2,1)S(1)} %get-tuple-element.6), channel_id=1, source_target_pairs={{4,0},{8,4},{12,8},{16,12},{20,16},{24,20},{28,24},{32,28},{36,32}... | collective-permute-start | bytes 64520 | tf_op jit(solution)/shard_map/ppermute | solution.py:22
  15.2 11.0 %collective-permute-start = (bf16[21,4,1,128]{3,1,0,2:T(4,128)(2,1)S(1)}, bf16[21,4,1,128]{3,1,0,2:T(4,128)(2,1)S(1)}, u32[]{:S(2)}, u32[]{:S(2)}) collective-permute-start(bf16[21,4,1,128]{3,1,0,2:T(4,128)(2,1)S(1)} %copy.16), channel_id=1, source_target_pairs={{0,4},{4,8},{8,12},{12,16},{16,20},{20,24},{24,28},{28,32},{32,36}... | collective-permute-start | bytes 64520 | tf_op jit(solution)/shard_map/ppermute | solution.py:21
  27.4 11.2 %collective-permute-start.2 = (bf16[1512,128]{1,0:T(8,128)(2,1)S(1)}, bf16[1512,128]{1,0:T(8,128)(2,1)S(1)}, u32[]{:S(2)}, u32[]{:S(2)}) collective-permute-start(bf16[1512,128]{1,0:T(8,128)(2,1)S(1)} %pad_maximum_fusion.refs_0_), channel_id=1, source_target_pairs={{0,2},{1,3},{2,0},{3,1},{4,6},{5,7},{6,4},{7,5},{8,10},{9,11},{10,... | collective-permute-start | bytes 1161224 | tf_op jit(solution)/shard_map/ppermute | solution.py:146
  31.0 10.0 %collective-permute-start.4 = (bf16[1512,128]{1,0:T(8,128)(2,1)S(1)}, bf16[1512,128]{1,0:T(8,128)(2,1)S(1)}, u32[]{:S(2)}, u32[]{:S(2)}) collective-permute-start(bf16[1512,128]{1,0:T(8,128)(2,1)S(1)} %pad_maximum_fusion.refs_0_), channel_id=1, source_target_pairs={{0,1},{1,0},{2,3},{3,2},{4,5},{5,4},{6,7},{7,6},{8,9},{9,8},{10,11... | collective-permute-start | bytes 1161224 | tf_op jit(solution)/shard_map/ppermute | solution.py:145
  38.6 3.6 %collective-permute-start.3 = (bf16[1512,128]{1,0:T(8,128)(2,1)S(1)}, bf16[1512,128]{1,0:T(8,128)(2,1)S(1)}, u32[]{:S(2)}, u32[]{:S(2)}) collective-permute-start(bf16[1512,128]{1,0:T(8,128)(2,1)S(1)} %collective-permute-done.2.refs_0_), channel_id=1, source_target_pairs={{0,1},{1,0},{2,3},{3,2},{4,5},{5,4},{6,7},{7,6},{8,9},{9,8},{10,11... | collective-permute-start | bytes 1161224 | tf_op jit(solution)/shard_map/ppermute | solution.py:147
  40.6 1.6 %copy-start = (f32[7,16,128]{2,1,0:T(8,128)S(1)}, f32[7,16,128]{2,1,0:T(8,128)}, u32[]{:S(2)}) copy-start(f32[7,16,128]{2,1,0:T(8,128)} %refs_4_.1) | copy-start | bytes 172036
  40.6 1.6 %copy-start.1 = (s32[16,128]{1,0:T(8,128)S(1)}, s32[16,128]{1,0:T(8,128)}, u32[]{:S(2)}) copy-start(s32[16,128]{1,0:T(8,128)} %refs_5_.1) | copy-start | bytes 24580
  40.6 1.6 %copy-start.2 = (s32[16,128]{1,0:T(8,128)S(1)}, s32[16,128]{1,0:T(8,128)}, u32[]{:S(2)}) copy-start(s32[16,128]{1,0:T(8,128)} %refs_6_.1) | copy-start | bytes 24580
  40.6 1.6 %copy-start.3 = (f32[7,8]{1,0:T(8,128)S(1)}, f32[7,8]{1,0:T(8,128)}, u32[]{:S(2)}) copy-start(f32[7,8]{1,0:T(8,128)} %refs_7_.1) | copy-start | bytes 676
  40.7 1.6 %copy-start.4 = (f32[7,8]{1,0:T(8,128)S(1)}, f32[7,8]{1,0:T(8,128)}, u32[]{:S(2)}) copy-start(f32[7,8]{1,0:T(8,128)} %refs_9_.1) | copy-start | bytes 676

commit v5 on v4

--- a/solution.py
+++ b/solution.py
@@ -23,14 +23,19 @@
     return above, below
 
 
-def kernel(nblock, final, nfield, rows, width, terms, nmat, nchar, *refs):
+def kernel(nblock, prev, final, partial, nfield, rows, width, terms, nmat, nchar, *refs):
     blocks = refs[:nblock]
+    refs = refs[nblock:]
+    if prev:
+        prev_ref, refs = refs[0], refs[1:]
     if final:
-        prev_ref, cp_ref, kl_ref, mat_ref, chr_ref, mt_ref, ct_ref, et_ref = refs[nblock:nblock + 8]
-        out_ref, fs, hs, os, cs, es = refs[nblock + 8:]
-        nloc = out_ref.shape[0]
+        cp_ref, kl_ref, mat_ref, chr_ref, mt_ref, ct_ref, et_ref = refs[:7]
+        refs = refs[7:]
+        if partial:
+            part_ref, refs = refs[0], refs[1:]
+        out_ref, fs, hs, os, cs, es = refs
     else:
-        out_ref, fs, hs = refs[nblock:]
+        out_ref, fs, hs = refs
     nloc = blocks[0].shape[0] // (nfield * (rows + 2))
     nmode = nblock * nloc
     span = fs.shape[0] // JS
@@ -99,7 +104,9 @@
         return
 
     def step(x, carry):
-        operand = jnp.concatenate([prev_ref[x], derive(x)], axis=0)
+        operand = derive(x)
+        if prev:
+            operand = jnp.concatenate([prev_ref[x], operand], axis=0)
         mixed = jnp.dot(cp_ref[...], operand, preferred_element_type=jnp.float32)
         cvals = [jnp.broadcast_to(cs[k, pl.ds(x, 1), :], (PAD_I, width)) for k in range(terms)]
         evals = [jnp.broadcast_to(es[k, pl.ds(x, 1), :], (PAD_I, width)) for k in range(terms)]
@@ -121,7 +128,10 @@
     lax.fori_loop(0, rows, step, 0, unroll=16)
 
     for i in range(out_ref.shape[0]):
-        out_ref[i] = os[pl.ds(i * OS, core), :].reshape(nfield, rows, width).astype(out_ref.dtype)
+        value = os[pl.ds(i * OS, core), :].reshape(nfield, rows, width)
+        if partial:
+            value = value + part_ref[i]
+        out_ref[i] = value.astype(out_ref.dtype)
 
 
 def body(
@@ -129,7 +139,6 @@
 ):
     local_modes, nfield, rows, width = fields.shape
     terms = coupling.shape[0]
-    total_modes = coupling.shape[1]
     groups = lax.axis_size("modes")
     assert groups == 4
     above, below = edge_rows(fields, "cells", 2)
@@ -158,52 +167,72 @@
     weights = jnp.pad(weights, ((0, 0), (0, PAD_I - local_modes), (0, 0)))
     vmem = pl.BlockSpec(memory_space=pltpu.VMEM)
     smem = pl.BlockSpec(memory_space=pltpu.SMEM)
-    half = groups // 2
-    span = -(-half * local_modes // 16) * 16
     tables = (kl_field, material, char_state, material_table, char_table, expansion_table)
-    gap = span - half * local_modes
-    weights = weights.reshape(terms, PAD_I, total_modes)
-    zeros = jnp.zeros((terms, PAD_I, gap), weights.dtype)
-    cols = jnp.concatenate(
-        [weights[:, :, : half * local_modes], zeros, weights[:, :, half * local_modes:], zeros], axis=2
-    ).reshape(terms * PAD_I, 2 * span)
     comps = nfield + 2
-    scratch = [
-        pltpu.VMEM((span * JS, width), jnp.float32),
-        pltpu.VMEM((2 * local_modes * nfield, width), jnp.float32),
+    params = pltpu.CompilerParams(vmem_limit_bytes=48 * 1024 * 1024)
+    nmat, nchar = material_table.shape[1], char_table.shape[1]
+
+    def padded(count):
+        return -(-count * local_modes // 16) * 16
+
+    def columns(groups_of_blocks):
+        pieces = []
+        for lo, hi in groups_of_blocks:
+            pieces.append(weights[:, :, lo * local_modes:hi * local_modes])
+            gap = padded(hi - lo) - (hi - lo) * local_modes
+            if gap:
+                pieces.append(jnp.zeros((terms, PAD_I, gap), weights.dtype))
+        cat = jnp.concatenate(pieces, axis=2)
+        return cat.reshape(terms * PAD_I, cat.shape[2])
+
+    def scratch(count):
+        return [
+            pltpu.VMEM((padded(count) * JS, width), jnp.float32),
+            pltpu.VMEM((2 * local_modes * nfield, width), jnp.float32),
+        ]
+
+    mix_scratch = [
+        pltpu.VMEM((PAD_I * OS, width), jnp.float32),
+        pltpu.VMEM((terms, rows, width), jnp.float32),
+        pltpu.VMEM((terms, rows, width), jnp.float32),
     ]
-    params = pltpu.CompilerParams(vmem_limit_bytes=48 * 1024 * 1024)
-
+
+    def mix_cost(span):
+        return pl.CostEstimate(
+            flops=2 * terms * PAD_I * span * comps * rows * width, transcendentals=0,
+            bytes_accessed=span * comps * rows * width * 2 + fields.size * 8,
+        )
+
+    partial = pl.pallas_call(
+        functools.partial(kernel, 2, False, True, False, nfield, rows, width, terms, nmat, nchar),
+        out_shape=jax.ShapeDtypeStruct(fields.shape, jnp.float32),
+        in_specs=[vmem] * 6 + [smem] * 3,
+        out_specs=vmem,
+        scratch_shapes=scratch(2) + mix_scratch,
+        compiler_params=params,
+        cost_estimate=mix_cost(padded(2)),
+    )(pack, partner, columns([(0, 2)]), *tables)
     ops = pl.pallas_call(
-        functools.partial(kernel, half, False, nfield, rows, width, terms,
-                          material_table.shape[1], char_table.shape[1]),
-        out_shape=jax.ShapeDtypeStruct((rows, span, comps * width), jnp.bfloat16),
-        in_specs=[vmem] * half,
+        functools.partial(kernel, 1, False, False, False, nfield, rows, width, terms, nmat, nchar),
+        out_shape=jax.ShapeDtypeStruct((rows, padded(1), comps * width), jnp.bfloat16),
+        in_specs=[vmem],
         out_specs=vmem,
-        scratch_shapes=scratch,
+        scratch_shapes=scratch(1),
         compiler_params=params,
         cost_estimate=pl.CostEstimate(
-            flops=12 * span * comps * rows * width, transcendentals=0,
-            bytes_accessed=half * pack.size * 2 + rows * span * comps * width * 2,
+            flops=12 * padded(1) * comps * rows * width, transcendentals=0,
+            bytes_accessed=pack.size * 2 + rows * padded(1) * comps * width * 2,
         ),
-    )(pack, partner)
+    )(counter)
     return pl.pallas_call(
-        functools.partial(kernel, half, True, nfield, rows, width, terms,
-                          material_table.shape[1], char_table.shape[1]),
+        functools.partial(kernel, 1, True, True, True, nfield, rows, width, terms, nmat, nchar),
         out_shape=jax.ShapeDtypeStruct(fields.shape, fields.dtype),
-        in_specs=[vmem] * (half + 5) + [smem] * 3,
+        in_specs=[vmem] * 6 + [smem] * 3 + [vmem],
         out_specs=vmem,
-        scratch_shapes=scratch + [
-            pltpu.VMEM((PAD_I * OS, width), jnp.float32),
-            pltpu.VMEM((terms, rows, width), jnp.float32),
-            pltpu.VMEM((terms, rows, width), jnp.float32),
-        ],
+        scratch_shapes=scratch(1) + mix_scratch,
         compiler_params=params,
-        cost_estimate=pl.CostEstimate(
-            flops=2 * terms * PAD_I * 2 * span * comps * rows * width, transcendentals=0,
-            bytes_accessed=half * pack.size * 2 + rows * span * comps * width * 2 + fields.size * 2,
-        ),
-    )(counter, diagonal, ops, cols, *tables)
+        cost_estimate=mix_cost(2 * padded(1)),
+    )(diagonal, ops, columns([(2, 3), (3, 4)]), *tables, partial)
 
 
 def solution(mesh):

time: 46.3 us -> 47.8 us (1.032)
  Pallas kernels: 4.28 us -> 6.21 us
  other arithmetic: 1.26 us -> 0.3 us
  local copies, waits for them, and re-layouts: 1.53 us -> 2.09 us
    pallas_call x2 -> x3, Pallas kernels: 4.28 us -> 6.21 us  [the longest x1 3.01 us: body(): pl.pallas_call(functools.partial(kernel, 1, True, True, True, nfield, row...]
    concatenate x1, other arithmetic: 1.01 us -> 0.03 us  [body(): jnp.concatenate([fields.reshape(local_modes * nfield * rows, width), jnp....]
    unnamed x17 -> x21, local copies, waits for them, and re-layouts: 0.15 us -> 0.7 us
  transfers between devices with their start and end apart: 5 -> 5, of which waited for: 2 -> 2; matrix products, arithmetic and copies ran while one was open for 1% -> 1% of each run, Pallas kernels for 3% -> 7%
where the time goes in v5:
time: 47.8 us; the launch traced here: 46.9 us
  starting transfers between devices  23.4 us (49%)
  waiting for transfers between devices  14.6 us (31%)
  Pallas kernels  6.21 us (13%)
  local copies, waits for them, and re-layouts  2.09 us (4%)
    ppermute x1, starting transfers between devices, edge_rows(): lax.ppermute(head, axis, [((i + 1) % count, i) for i in range(ends)])  14.1 us
    ppermute x1, waiting for transfers between devices, edge_rows(): lax.ppermute(tail, axis, [(i, (i + 1) % count) for i in range(ends)])  9.07 us
    ppermute x1, waiting for transfers between devices, body(): counter = lax.ppermute(pack, 'modes', [(i, i ^ 2) for i in range(groups)])  5.55 us
    ppermute x1, starting transfers between devices, body(): counter = lax.ppermute(pack, 'modes', [(i, i ^ 2) for i in range(groups)])  3.51 us
    pallas_call x1, Pallas kernels, body(): pl.pallas_call(functools.partial(kernel, 1, True, True, True, nfield, row...  3.01 us
    pallas_call x1, Pallas kernels, body(): pl.pallas_call(functools.partial(kernel, 2, False, True, False, nfield, r...  2.41 us
    ppermute x1, starting transfers between devices, edge_rows(): lax.ppermute(tail, axis, [(i, (i + 1) % count) for i in range(ends)])  1.92 us
    ppermute x1, starting transfers between devices, body(): partner = lax.ppermute(pack, 'modes', [(i, i ^ 1) for i in range(groups)])  1.92 us
  transfers between devices with their start and end apart: 5, of which 2 were waited for; matrix products, arithmetic and copies ran while one was open for 1% of the time, Pallas kernels for 7%

profile of v5, /device:TPU:6, one launch (start us, length us, event | category | flops | bytes accessed | tf_op | source)
XLA Modules:
  0.0 46.9 jit_solution(6954447359137903912)
XLA Ops:
  0.0 1.1 %fusion.7 = (bf16[21,4,1,128]{3,2,1,0:T(2,128)(2,1)S(1)}, bf16[21,4,1,128]{3,2,1,0:T(2,128)(2,1)S(1)}) fusion(bf16[21,4,16,128]{3,2,1,0:T(8,128)(2,1)} %param.8), kind=kLoop, calls=%fused_computation.17 | loop fusion | bytes 86016 | tf_op jit(solution)/shard_map/slice | solution.py:20
  1.1 14.1 %collective-permute-start.1 = (bf16[21,4,1,128]{3,2,1,0:T(2,128)(2,1)S(1)}, bf16[21,4,1,128]{3,2,1,0:T(2,128)(2,1)S(1)}, u32[]{:S(2)}, u32[]{:S(2)}) collective-permute-start(bf16[21,4,1,128]{3,2,1,0:T(2,128)(2,1)S(1)} %get-tuple-element.6), channel_id=1, source_target_pairs={{4,0},{8,4},{12,8},{16,12},{20,16},{24,20},{28,24},{32,28},{36,32}... | collective-permute-start | bytes 64520 | tf_op jit(solution)/shard_map/ppermute | solution.py:22
  15.3 1.9 %collective-permute-start = (bf16[21,4,1,128]{3,1,0,2:T(4,128)(2,1)S(1)}, bf16[21,4,1,128]{3,1,0,2:T(4,128)(2,1)S(1)}, u32[]{:S(2)}, u32[]{:S(2)}) collective-permute-start(bf16[21,4,1,128]{3,1,0,2:T(4,128)(2,1)S(1)} %copy.18), channel_id=1, source_target_pairs={{0,4},{4,8},{8,12},{12,16},{16,20},{20,24},{24,28},{28,32},{32,36}... | collective-permute-start | bytes 64520 | tf_op jit(solution)/shard_map/ppermute | solution.py:21
  17.2 9.1 %collective-permute-done = bf16[21,4,1,128]{3,1,0,2:T(4,128)(2,1)S(1)} collective-permute-done((bf16[21,4,1,128]{3,1,0,2:T(4,128)(2,1)S(1)}, bf16[21,4,1,128]{3,1,0,2:T(4,128)(2,1)S(1)}, u32[]{:S(2)}, u32[]{:S(2)}) %collective-permute-start) | collective-permute-done | bytes 21536 | tf_op jit(solution)/shard_map/ppermute | solution.py:21
  26.4 0.0 copy-start.6
  26.4 3.5 %collective-permute-start.2 = (bf16[1512,128]{1,0:T(8,128)(2,1)S(1)}, bf16[1512,128]{1,0:T(8,128)(2,1)S(1)}, u32[]{:S(2)}, u32[]{:S(2)}) collective-permute-start(bf16[1512,128]{1,0:T(8,128)(2,1)S(1)} %pad_maximum_fusion.refs_0_), channel_id=1, source_target_pairs={{0,2},{1,3},{2,0},{3,1},{4,6},{5,7},{6,4},{7,5},{8,10},{9,11},{10,... | collective-permute-start | bytes 1161224 | tf_op jit(solution)/shard_map/ppermute | solution.py:155
  30.0 0.1 constant_dynamic-slice_fusion.3
  30.1 0.1 fusion.6
  30.3 0.0 copy-start.7
  30.3 1.9 %collective-permute-start.4 = (bf16[1512,128]{1,0:T(8,128)(2,1)S(1)}, bf16[1512,128]{1,0:T(8,128)(2,1)S(1)}, u32[]{:S(2)}, u32[]{:S(2)}) collective-permute-start(bf16[1512,128]{1,0:T(8,128)(2,1)S(1)} %pad_maximum_fusion.refs_0_), channel_id=1, source_target_pairs={{0,1},{1,0},{2,3},{3,2},{4,5},{5,4},{6,7},{7,6},{8,9},{9,8},{10,11... | collective-permute-start | bytes 1161224 | tf_op jit(solution)/shard_map/ppermute | solution.py:154
  32.2 5.6 %collective-permute-done.2.refs_0_ = bf16[1512,128]{1,0:T(8,128)(2,1)S(1)} collective-permute-done((bf16[1512,128]{1,0:T(8,128)(2,1)S(1)}, bf16[1512,128]{1,0:T(8,128)(2,1)S(1)}, u32[]{:S(2)}, u32[]{:S(2)}) %collective-permute-start.2) | collective-permute-done | bytes 387104 | tf_op jit(solution)/shard_map/ppermute | solution.py:155
  37.8 1.9 %collective-permute-start.3 = (bf16[1512,128]{1,0:T(8,128)(2,1)S(1)}, bf16[1512,128]{1,0:T(8,128)(2,1)S(1)}, u32[]{:S(2)}, u32[]{:S(2)}) collective-permute-start(bf16[1512,128]{1,0:T(8,128)(2,1)S(1)} %collective-permute-done.2.refs_0_), channel_id=1, source_target_pairs={{0,1},{1,0},{2,3},{3,2},{4,5},{5,4},{6,7},{7,6},{8,9},{9,8},{10,11... | collective-permute-start | bytes 1161224 | tf_op jit(solution)/shard_map/ppermute | solution.py:156
  39.7 0.1 fusion.8
  39.8 0.1 copy.16.refs_7_
  39.9 0.1 pad_maximum_fusion.1
  40.0 0.5 %copy-done.8 = pred[48]{0:T(512)(128)(4,1)S(1)} copy-done((pred[48]{0:T(512)(128)(4,1)S(1)}, pred[48]{0:T(512)(128)(4,1)}, u32[]{:S(2)}) %copy-start.8) | copy-done | bytes 72
  40.6 0.0 copy-start
  40.6 0.0 copy-start.1
  40.6 0.0 copy-start.2
  40.6 0.0 copy-start.3
  40.6 0.0 copy-start.4
  40.6 0.8 %shard_map.82.refs_1_ = bf16[16,32,768]{2,1,0:T(8,128)(2,1)S(1)} custom-call(bf16[1512,128]{1,0:T(8,128)(2,1)S(1)} %collective-permute-done.2.refs_0_), custom_call_target="tpu_custom_call" | custom-call | flops 4718592 | bytes 1173504 | tf_op jit(solution)/shard_map/pallas_call | solution.py:215
  41.5 2.4 %shard_map.83.refs_9_ = f32[21,4,16,128]{3,2,1,0:T(8,128)S(1)} custom-call(bf16[1512,128]{1,0:T(8,128)(2,1)S(1)} %pad_maximum_fusion.refs_0_, bf16[1512,128]{1,0:T(8,128)(2,1)S(1)} %collective-permute-done.4.refs_1_, bf16[168,48]{1,0:T(8,128)(2,1)S(1)} %bitcast.10, f32[7,16,128]{2,1,0:T(8,128)S(1)} %copy-done, s32[16,128]{1,0:T(8,128)S(1)} %copy-done.1, ...), custom_call_target="tpu_custom_call" | custom-call | flops 198180864 | bytes 2555904 | tf_op jit(solution)/shard_map/pallas_call | solution.py:206
  43.9 3.0 %shard_map.84 = bf16[21,4,16,128]{3,2,1,0:T(8,128)(2,1)} custom-call(bf16[1512,128]{1,0:T(8,128)(2,1)S(1)} %collective-permute-done.3.refs_0_, bf16[16,32,768]{2,1,0:T(8,128)(2,1)S(1)} %shard_map.82.refs_1_, bf16[168,64]{1,0:T(8,128)(2,1)S(1)} %bitcast.9, f32[7,16,128]{2,1,0:T(8,128)S(1)} %copy-done, s32[16,128]{1,0:T(8,128)S(1)} %copy-done.1, ...), custom_call_target="tpu_custom_call" | custom-call | flops 264241152 | bytes 2949120 | tf_op jit(solution)/shard_map/pallas_call | solution.py:227
  (21 shorter events, 0.2 us)
Async XLA Ops:
  0.0 26.4 %copy-start.5 = (bf16[21,4,16,128]{3,2,1,0:T(8,128)(2,1)S(1)}, bf16[21,4,16,128]{3,2,1,0:T(8,128)(2,1)}, u32[]{:S(2)}) copy-start(bf16[21,4,16,128]{3,2,1,0:T(8,128)(2,1)} %param.8) | copy-start | bytes 1032196
  1.1 16.1 %collective-permute-start.1 = (bf16[21,4,1,128]{3,2,1,0:T(2,128)(2,1)S(1)}, bf16[21,4,1,128]{3,2,1,0:T(2,128)(2,1)S(1)}, u32[]{:S(2)}, u32[]{:S(2)}) collective-permute-start(bf16[21,4,1,128]{3,2,1,0:T(2,128)(2,1)S(1)} %get-tuple-element.6), channel_id=1, source_target_pairs={{4,0},{8,4},{12,8},{16,12},{20,16},{24,20},{28,24},{32,28},{36,32}... | collective-permute-start | bytes 64520 | tf_op jit(solution)/shard_map/ppermute | solution.py:22
  15.3 11.0 %collective-permute-start = (bf16[21,4,1,128]{3,1,0,2:T(4,128)(2,1)S(1)}, bf16[21,4,1,128]{3,1,0,2:T(4,128)(2,1)S(1)}, u32[]{:S(2)}, u32[]{:S(2)}) collective-permute-start(bf16[21,4,1,128]{3,1,0,2:T(4,128)(2,1)S(1)} %copy.18), channel_id=1, source_target_pairs={{0,4},{4,8},{8,12},{12,16},{16,20},{20,24},{24,28},{28,32},{32,36}... | collective-permute-start | bytes 64520 | tf_op jit(solution)/shard_map/ppermute | solution.py:21
  26.4 3.6 %copy-start.6 = (bf16[7,84,84]{2,1,0:T(8,128)(2,1)S(1)}, bf16[7,84,84]{2,1,0:T(8,128)(2,1)}, u32[]{:S(2)}) copy-start(bf16[7,84,84]{2,1,0:T(8,128)(2,1)} %param.9) | copy-start | bytes 296356
  26.4 11.3 %collective-permute-start.2 = (bf16[1512,128]{1,0:T(8,128)(2,1)S(1)}, bf16[1512,128]{1,0:T(8,128)(2,1)S(1)}, u32[]{:S(2)}, u32[]{:S(2)}) collective-permute-start(bf16[1512,128]{1,0:T(8,128)(2,1)S(1)} %pad_maximum_fusion.refs_0_), channel_id=1, source_target_pairs={{0,2},{1,3},{2,0},{3,1},{4,6},{5,7},{6,4},{7,5},{8,10},{9,11},{10,... | collective-permute-start | bytes 1161224 | tf_op jit(solution)/shard_map/ppermute | solution.py:155
  30.3 9.5 %copy-start.7 = (f32[7,3]{0,1:T(4,128)S(1)}, f32[7,3]{0,1:T(4,128)}, u32[]{:S(2)}) copy-start(f32[7,3]{0,1:T(4,128)} %param.14) | copy-start | bytes 256
  30.3 11.1 %collective-permute-start.4 = (bf16[1512,128]{1,0:T(8,128)(2,1)S(1)}, bf16[1512,128]{1,0:T(8,128)(2,1)S(1)}, u32[]{:S(2)}, u32[]{:S(2)}) collective-permute-start(bf16[1512,128]{1,0:T(8,128)(2,1)S(1)} %pad_maximum_fusion.refs_0_), channel_id=1, source_target_pairs={{0,1},{1,0},{2,3},{3,2},{4,5},{5,4},{6,7},{7,6},{8,9},{9,8},{10,11... | collective-permute-start | bytes 1161224 | tf_op jit(solution)/shard_map/ppermute | solution.py:154
  37.8 6.1 %collective-permute-start.3 = (bf16[1512,128]{1,0:T(8,128)(2,1)S(1)}, bf16[1512,128]{1,0:T(8,128)(2,1)S(1)}, u32[]{:S(2)}, u32[]{:S(2)}) collective-permute-start(bf16[1512,128]{1,0:T(8,128)(2,1)S(1)} %collective-permute-done.2.refs_0_), channel_id=1, source_target_pairs={{0,1},{1,0},{2,3},{3,2},{4,5},{5,4},{6,7},{7,6},{8,9},{9,8},{10,11... | collective-permute-start | bytes 1161224 | tf_op jit(solution)/shard_map/ppermute | solution.py:156
  39.9 0.7 %copy-start.8 = (pred[48]{0:T(512)(128)(4,1)S(1)}, pred[48]{0:T(512)(128)(4,1)}, u32[]{:S(2)}) copy-start(pred[48]{0:T(512)(128)(4,1)} %constant.82.clone.1) | copy-start | bytes 148
  40.6 0.9 %copy-start = (f32[7,16,128]{2,1,0:T(8,128)S(1)}, f32[7,16,128]{2,1,0:T(8,128)}, u32[]{:S(2)}) copy-start(f32[7,16,128]{2,1,0:T(8,128)} %refs_3_.3) | copy-start | bytes 172036
  40.6 0.9 %copy-start.1 = (s32[16,128]{1,0:T(8,128)S(1)}, s32[16,128]{1,0:T(8,128)}, u32[]{:S(2)}) copy-start(s32[16,128]{1,0:T(8,128)} %refs_4_.3) | copy-start | bytes 24580
  40.6 0.9 %copy-start.2 = (s32[16,128]{1,0:T(8,128)S(1)}, s32[16,128]{1,0:T(8,128)}, u32[]{:S(2)}) copy-start(s32[16,128]{1,0:T(8,128)} %refs_5_.3) | copy-start | bytes 24580
  40.6 0.9 %copy-start.3 = (f32[7,8]{1,0:T(8,128)S(1)}, f32[7,8]{1,0:T(8,128)}, u32[]{:S(2)}) copy-start(f32[7,8]{1,0:T(8,128)} %refs_6_.3) | copy-start | bytes 676
  40.6 0.9 %copy-start.4 = (f32[7,8]{1,0:T(8,128)S(1)}, f32[7,8]{1,0:T(8,128)}, u32[]{:S(2)}) copy-start(f32[7,8]{1,0:T(8,128)} %refs_8_.3) | copy-start | bytes 676

commit v6 on v5

--- a/solution.py
+++ b/solution.py
@@ -24,8 +24,8 @@
 
 
 def kernel(nblock, prev, final, partial, nfield, rows, width, terms, nmat, nchar, *refs):
-    blocks = refs[:nblock]
-    refs = refs[nblock:]
+    blocks = [(refs[2 * b], refs[2 * b + 1]) for b in range(nblock)]
+    refs = refs[2 * nblock:]
     if prev:
         prev_ref, refs = refs[0], refs[1:]
     if final:
@@ -36,11 +36,10 @@
         out_ref, fs, hs, os, cs, es = refs
     else:
         out_ref, fs, hs = refs
-    nloc = blocks[0].shape[0] // (nfield * (rows + 2))
+    nloc = blocks[0][0].shape[0] // (nfield * rows)
     nmode = nblock * nloc
     span = fs.shape[0] // JS
     core = nfield * rows
-    per = nloc * nfield
 
     if final:
         mat = mat_ref[...]
@@ -59,11 +58,11 @@
             cs[k] = kl * mv * cv
             es[k] = kl * ev
 
-    for d, blk in enumerate(blocks):
+    for d, (blk, hal) in enumerate(blocks):
         for jl in range(nloc):
             j = d * nloc + jl
             fs[pl.ds(j * JS, core), :] = blk[pl.ds(jl * core, core), :].astype(jnp.float32)
-        hs[...] = blk[pl.ds(nloc * core, 2 * per), :].astype(jnp.float32)
+        hs[...] = hal[...].astype(jnp.float32)
         for side in range(2 * nfield):
             fs[pl.ds(d * nloc * JS + core + side, nloc, stride=JS), :] = hs[pl.ds(side * nloc, nloc), :]
     if span > nmode:
@@ -141,19 +140,20 @@
     terms = coupling.shape[0]
     groups = lax.axis_size("modes")
     assert groups == 4
+    cells = fields.reshape(local_modes * nfield * rows, width)
+    counter = lax.ppermute(cells, "modes", [(i, i ^ 2) for i in range(groups)])
+    partner = lax.ppermute(cells, "modes", [(i, i ^ 1) for i in range(groups)])
     above, below = edge_rows(fields, "cells", 2)
-    pack = jnp.concatenate(
-        [
-            fields.reshape(local_modes * nfield * rows, width),
-            jnp.stack([above[:, :, 0], below[:, :, 0]], axis=1)
-            .transpose(2, 1, 0, 3)
-            .reshape(2 * nfield * local_modes, width),
-        ],
-        axis=0,
-    )
-    partner = lax.ppermute(pack, "modes", [(i, i ^ 1) for i in range(groups)])
-    counter = lax.ppermute(pack, "modes", [(i, i ^ 2) for i in range(groups)])
-    diagonal = lax.ppermute(counter, "modes", [(i, i ^ 1) for i in range(groups)])
+    halo = (
+        jnp.stack([above[:, :, 0], below[:, :, 0]], axis=1)
+        .transpose(2, 1, 0, 3)
+        .reshape(2 * nfield * local_modes, width)
+    )
+    counter_halo = lax.ppermute(halo, "modes", [(i, i ^ 2) for i in range(groups)])
+    partner_halo = lax.ppermute(halo, "modes", [(i, i ^ 1) for i in range(groups)])
+    diagonal, diagonal_halo = lax.ppermute(
+        (counter, counter_halo), "modes", [(i, i ^ 1) for i in range(groups)]
+    )
     me = lax.axis_index("modes")
     first_mode = me * local_modes
     weights = lax.dynamic_slice_in_dim(coupling, first_mode, local_modes, 1)
@@ -206,33 +206,33 @@
     partial = pl.pallas_call(
         functools.partial(kernel, 2, False, True, False, nfield, rows, width, terms, nmat, nchar),
         out_shape=jax.ShapeDtypeStruct(fields.shape, jnp.float32),
-        in_specs=[vmem] * 6 + [smem] * 3,
+        in_specs=[vmem] * 8 + [smem] * 3,
         out_specs=vmem,
         scratch_shapes=scratch(2) + mix_scratch,
         compiler_params=params,
         cost_estimate=mix_cost(padded(2)),
-    )(pack, partner, columns([(0, 2)]), *tables)
+    )(cells, halo, partner, partner_halo, columns([(0, 2)]), *tables)
     ops = pl.pallas_call(
         functools.partial(kernel, 1, False, False, False, nfield, rows, width, terms, nmat, nchar),
         out_shape=jax.ShapeDtypeStruct((rows, padded(1), comps * width), jnp.bfloat16),
-        in_specs=[vmem],
+        in_specs=[vmem] * 2,
         out_specs=vmem,
         scratch_shapes=scratch(1),
         compiler_params=params,
         cost_estimate=pl.CostEstimate(
             flops=12 * padded(1) * comps * rows * width, transcendentals=0,
-            bytes_accessed=pack.size * 2 + rows * padded(1) * comps * width * 2,
+            bytes_accessed=fields.size * 2 + rows * padded(1) * comps * width * 2,
         ),
-    )(counter)
+    )(counter, counter_halo)
     return pl.pallas_call(
         functools.partial(kernel, 1, True, True, True, nfield, rows, width, terms, nmat, nchar),
         out_shape=jax.ShapeDtypeStruct(fields.shape, fields.dtype),
-        in_specs=[vmem] * 6 + [smem] * 3 + [vmem],
+        in_specs=[vmem] * 7 + [smem] * 3 + [vmem],
         out_specs=vmem,
         scratch_shapes=scratch(1) + mix_scratch,
         compiler_params=params,
         cost_estimate=mix_cost(2 * padded(1)),
-    )(diagonal, ops, columns([(2, 3), (3, 4)]), *tables, partial)
+    )(diagonal, diagonal_halo, ops, columns([(2, 3), (3, 4)]), *tables, partial)
 
 
 def solution(mesh):

time: 47.8 us -> 48.7 us (1.019)
  the two profiles are of different devices: /device:TPU:6 before, /device:TPU:7 now
where the time goes in v6:
time: 48.7 us; the launch traced here: 48.4 us
  starting transfers between devices  32 us (66%)
  waiting for transfers between devices  7.42 us (15%)
  Pallas kernels  6.22 us (13%)
  local copies, waits for them, and re-layouts  2.19 us (4%)
    ppermute x1, starting transfers between devices, edge_rows(): lax.ppermute(head, axis, [((i + 1) % count, i) for i in range(ends)])  12.9 us
    ppermute x1, waiting for transfers between devices, edge_rows(): lax.ppermute(tail, axis, [(i, (i + 1) % count) for i in range(ends)])  7.4 us
    ppermute x2, starting transfers between devices, body(): lax.ppermute((counter, counter_halo), 'modes', [(i, i ^ 1) for i in range...  6.42 us
    ppermute x1, starting transfers between devices, body(): counter = lax.ppermute(cells, 'modes', [(i, i ^ 2) for i in range(groups)])  4 us
    pallas_call x1, Pallas kernels, body(): pl.pallas_call(functools.partial(kernel, 1, True, True, True, nfield, row...  3.01 us
    ppermute x1, starting transfers between devices, body(): partner = lax.ppermute(cells, 'modes', [(i, i ^ 1) for i in range(groups)])  2.71 us
    pallas_call x1, Pallas kernels, body(): pl.pallas_call(functools.partial(kernel, 2, False, True, False, nfield, r...  2.42 us
    ppermute x1, starting transfers between devices, body(): lax.ppermute(halo, 'modes', [(i, i ^ 2) for i in range(groups)])  2.08 us
  transfers between devices with their start and end apart: 8, of which 1 were waited for; matrix products, arithmetic and copies ran while one was open for 4% of the time, Pallas kernels for 7%

profile of v6, /device:TPU:7, one launch (start us, length us, event | category | flops | bytes accessed | tf_op | source)
XLA Modules:
  0.0 48.4 jit_solution(11555897767204577352)
XLA Ops:
  0.0 2.7 %collective-permute-start.6 = (bf16[1344,128]{1,0:T(8,128)(2,1)}, bf16[1344,128]{1,0:T(8,128)(2,1)S(1)}, u32[]{:S(2)}, u32[]{:S(2)}) collective-permute-start(bf16[1344,128]{1,0:T(8,128)(2,1)} %bitcast.9), channel_id=1, source_target_pairs={{0,1},{1,0},{2,3},{3,2},{4,5},{5,4},{6,7},{7,6},{8,9},{9,8},{10,11... | collective-permute-start | bytes 1032200 | tf_op jit(solution)/shard_map/ppermute | solution.py:145
  2.7 4.0 %collective-permute-start = (bf16[1344,128]{1,0:T(8,128)(2,1)}, bf16[1344,128]{1,0:T(8,128)(2,1)S(1)}, u32[]{:S(2)}, u32[]{:S(2)}) collective-permute-start(bf16[1344,128]{1,0:T(8,128)(2,1)} %bitcast.10), channel_id=1, source_target_pairs={{0,2},{1,3},{2,0},{3,1},{4,6},{5,7},{6,4},{7,5},{8,10},{9,11},{10,... | collective-permute-start | bytes 1032200 | tf_op jit(solution)/shard_map/ppermute | solution.py:144
  6.7 1.1 %fusion.7 = (bf16[21,4,1,128]{3,2,1,0:T(2,128)(2,1)S(1)}, bf16[21,4,1,128]{3,2,1,0:T(2,128)(2,1)S(1)}) fusion(bf16[21,4,16,128]{3,2,1,0:T(8,128)(2,1)} %param.8), kind=kLoop, calls=%fused_computation.16 | loop fusion | bytes 86016 | tf_op jit(solution)/shard_map/slice | solution.py:20
  7.8 12.9 %collective-permute-start.3 = (bf16[21,4,1,128]{3,2,1,0:T(2,128)(2,1)S(1)}, bf16[21,4,1,128]{3,2,1,0:T(2,128)(2,1)S(1)}, u32[]{:S(2)}, u32[]{:S(2)}) collective-permute-start(bf16[21,4,1,128]{3,2,1,0:T(2,128)(2,1)S(1)} %get-tuple-element.6), channel_id=1, source_target_pairs={{4,0},{8,4},{12,8},{16,12},{20,16},{24,20},{28,24},{32,28},{36,32}... | collective-permute-start | bytes 64520 | tf_op jit(solution)/shard_map/ppermute | solution.py:22
  20.8 1.9 %collective-permute-start.2 = (bf16[21,4,1,128]{3,1,0,2:T(4,128)(2,1)S(1)}, bf16[21,4,1,128]{3,1,0,2:T(4,128)(2,1)S(1)}, u32[]{:S(2)}, u32[]{:S(2)}) collective-permute-start(bf16[21,4,1,128]{3,1,0,2:T(4,128)(2,1)S(1)} %copy.18), channel_id=1, source_target_pairs={{0,4},{4,8},{8,12},{12,16},{16,20},{20,24},{24,28},{28,32},{32,36}... | collective-permute-start | bytes 64520 | tf_op jit(solution)/shard_map/ppermute | solution.py:21
  22.7 0.1 constant_dynamic-slice_fusion.3
  22.9 0.1 fusion.6
  23.0 0.1 fusion.8
  23.1 7.4 %collective-permute-done.2 = bf16[21,4,1,128]{3,1,0,2:T(4,128)(2,1)S(1)} collective-permute-done((bf16[21,4,1,128]{3,1,0,2:T(4,128)(2,1)S(1)}, bf16[21,4,1,128]{3,1,0,2:T(4,128)(2,1)S(1)}, u32[]{:S(2)}, u32[]{:S(2)}) %collective-permute-start.2) | collective-permute-done | bytes 21536 | tf_op jit(solution)/shard_map/ppermute | solution.py:21
  30.6 0.0 copy-start.8
  30.6 2.1 %collective-permute-start.4 = (bf16[168,128]{1,0:T(8,128)(2,1)S(1)}, bf16[168,128]{1,0:T(8,128)(2,1)S(1)}, u32[]{:S(2)}, u32[]{:S(2)}) collective-permute-start(bf16[168,128]{1,0:T(8,128)(2,1)S(1)} %reshape.13.refs_1_), channel_id=1, source_target_pairs={{0,2},{1,3},{2,0},{3,1},{4,6},{5,7},{6,4},{7,5},{8,10},{9,11},{10,... | collective-permute-start | bytes 129032 | tf_op jit(solution)/shard_map/ppermute | solution.py:152
  32.7 4.0 %collective-permute-start.1 = (bf16[1344,128]{1,0:T(8,128)(2,1)S(1)}, bf16[1344,128]{1,0:T(8,128)(2,1)S(1)}, u32[]{:S(2)}, u32[]{:S(2)}) collective-permute-start(bf16[1344,128]{1,0:T(8,128)(2,1)S(1)} %collective-permute-done.refs_0_), channel_id=1, source_target_pairs={{0,1},{1,0},{2,3},{3,2},{4,5},{5,4},{6,7},{7,6},{8,9},{9,8},{10,11... | collective-permute-start | bytes 1032200 | tf_op jit(solution)/shard_map/ppermute | solution.py:154
  36.8 1.9 %collective-permute-start.7 = (bf16[168,128]{1,0:T(8,128)(2,1)S(1)}, bf16[168,128]{1,0:T(8,128)(2,1)S(1)}, u32[]{:S(2)}, u32[]{:S(2)}) collective-permute-start(bf16[168,128]{1,0:T(8,128)(2,1)S(1)} %reshape.13.refs_1_), channel_id=1, source_target_pairs={{0,1},{1,0},{2,3},{3,2},{4,5},{5,4},{6,7},{7,6},{8,9},{9,8},{10,11... | collective-permute-start | bytes 129032 | tf_op jit(solution)/shard_map/ppermute | solution.py:153
  38.7 2.4 %collective-permute-start.5 = (bf16[168,128]{1,0:T(8,128)(2,1)S(1)}, bf16[168,128]{1,0:T(8,128)(2,1)S(1)}, u32[]{:S(2)}, u32[]{:S(2)}) collective-permute-start(bf16[168,128]{1,0:T(8,128)(2,1)S(1)} %collective-permute-done.4.refs_1_), channel_id=1, source_target_pairs={{0,1},{1,0},{2,3},{3,2},{4,5},{5,4},{6,7},{7,6},{8,9},{9,8},{10,11... | collective-permute-start | bytes 129032 | tf_op jit(solution)/shard_map/ppermute | solution.py:154
  41.1 0.0 copy-start.7
  41.2 0.1 pad_maximum_fusion
  41.3 0.6 %copy-done.7 = f32[7,3]{0,1:T(4,128)S(1)} copy-done((f32[7,3]{0,1:T(4,128)S(1)}, f32[7,3]{0,1:T(4,128)}, u32[]{:S(2)}) %copy-start.7) | copy-done | bytes 108
  41.8 0.1 copy.16.refs_9_.refs_8_
  41.9 0.0 copy-start.4
  41.9 0.0 copy-start.5
  42.0 0.8 %shard_map.82.refs_2_ = bf16[16,32,768]{2,1,0:T(8,128)(2,1)S(1)} custom-call(bf16[1344,128]{1,0:T(8,128)(2,1)S(1)} %collective-permute-done.refs_0_, bf16[168,128]{1,0:T(8,128)(2,1)S(1)} %collective-permute-done.4.refs_1_), custom_call_target="tpu_custom_call" | custom-call | flops 4718592 | bytes 1130496 | tf_op jit(solution)/shard_map/pallas_call | solution.py:215
  42.8 0.1 copy-done
  42.9 2.4 %shard_map.83.refs_10_ = f32[21,4,16,128]{3,2,1,0:T(8,128)S(1)} custom-call(bf16[1344,128]{1,0:T(8,128)(2,1)S(1)} %bitcast.11, bf16[168,128]{1,0:T(8,128)(2,1)S(1)} %reshape.13.refs_1_, bf16[1344,128]{1,0:T(8,128)(2,1)S(1)} %collective-permute-done.6.refs_2_, bf16[168,128]{1,0:T(8,128)(2,1)S(1)} %collective-permute-done.7.refs_3_, ...), custom_call_target="tpu_custom_call" | custom-call | flops 198180864 | bytes 2555904 | tf_op jit(solution)/shard_map/pallas_call | solution.py:206
  45.4 3.0 %shard_map.84 = bf16[21,4,16,128]{3,2,1,0:T(8,128)(2,1)} custom-call(bf16[1344,128]{1,0:T(8,128)(2,1)S(1)} %collective-permute-done.1.refs_0_, bf16[168,128]{1,0:T(8,128)(2,1)S(1)} %collective-permute-done.5.refs_1_, bf16[16,32,768]{2,1,0:T(8,128)(2,1)S(1)} %shard_map.82.refs_2_, bf16[168,64]{1,0:T(8,128)(2,1)S(1)} %bitcast.12, f32[7,16,128]{2,1,0:T(8,128)S(1)} %copy-done.1, ...), custom_call_target="tpu_custom_call" | custom-call | flops 264241152 | bytes 2949120 | tf_op jit(solution)/shard_map/pallas_call | solution.py:227
  (26 shorter events, 0.2 us)
Async XLA Ops:
  0.0 22.7 %copy-start.6 = (bf16[7,84,84]{2,1,0:T(8,128)(2,1)S(1)}, bf16[7,84,84]{2,1,0:T(8,128)(2,1)}, u32[]{:S(2)}) copy-start(bf16[7,84,84]{2,1,0:T(8,128)(2,1)} %param.9) | copy-start | bytes 296356
  0.0 42.8 %collective-permute-start.6 = (bf16[1344,128]{1,0:T(8,128)(2,1)}, bf16[1344,128]{1,0:T(8,128)(2,1)S(1)}, u32[]{:S(2)}, u32[]{:S(2)}) collective-permute-start(bf16[1344,128]{1,0:T(8,128)(2,1)} %bitcast.9), channel_id=1, source_target_pairs={{0,1},{1,0},{2,3},{3,2},{4,5},{5,4},{6,7},{7,6},{8,9},{9,8},{10,11... | collective-permute-start | bytes 1032200 | tf_op jit(solution)/shard_map/ppermute | solution.py:145
  2.7 30.0 %collective-permute-start = (bf16[1344,128]{1,0:T(8,128)(2,1)}, bf16[1344,128]{1,0:T(8,128)(2,1)S(1)}, u32[]{:S(2)}, u32[]{:S(2)}) collective-permute-start(bf16[1344,128]{1,0:T(8,128)(2,1)} %bitcast.10), channel_id=1, source_target_pairs={{0,2},{1,3},{2,0},{3,1},{4,6},{5,7},{6,4},{7,5},{8,10},{9,11},{10,... | collective-permute-start | bytes 1032200 | tf_op jit(solution)/shard_map/ppermute | solution.py:144
  7.8 15.3 %collective-permute-start.3 = (bf16[21,4,1,128]{3,2,1,0:T(2,128)(2,1)S(1)}, bf16[21,4,1,128]{3,2,1,0:T(2,128)(2,1)S(1)}, u32[]{:S(2)}, u32[]{:S(2)}) collective-permute-start(bf16[21,4,1,128]{3,2,1,0:T(2,128)(2,1)S(1)} %get-tuple-element.6), channel_id=1, source_target_pairs={{4,0},{8,4},{12,8},{16,12},{20,16},{24,20},{28,24},{32,28},{36,32}... | collective-permute-start | bytes 64520 | tf_op jit(solution)/shard_map/ppermute | solution.py:22
  20.8 9.8 %collective-permute-start.2 = (bf16[21,4,1,128]{3,1,0,2:T(4,128)(2,1)S(1)}, bf16[21,4,1,128]{3,1,0,2:T(4,128)(2,1)S(1)}, u32[]{:S(2)}, u32[]{:S(2)}) collective-permute-start(bf16[21,4,1,128]{3,1,0,2:T(4,128)(2,1)S(1)} %copy.18), channel_id=1, source_target_pairs={{0,4},{4,8},{8,12},{12,16},{16,20},{20,24},{24,28},{28,32},{32,36}... | collective-permute-start | bytes 64520 | tf_op jit(solution)/shard_map/ppermute | solution.py:21
  30.6 6.2 %copy-start.8 = (pred[48]{0:T(512)(128)(4,1)S(1)}, pred[48]{0:T(512)(128)(4,1)}, u32[]{:S(2)}) copy-start(pred[48]{0:T(512)(128)(4,1)} %constant.82.clone.1) | copy-start | bytes 148
  30.6 8.1 %collective-permute-start.4 = (bf16[168,128]{1,0:T(8,128)(2,1)S(1)}, bf16[168,128]{1,0:T(8,128)(2,1)S(1)}, u32[]{:S(2)}, u32[]{:S(2)}) collective-permute-start(bf16[168,128]{1,0:T(8,128)(2,1)S(1)} %reshape.13.refs_1_), channel_id=1, source_target_pairs={{0,2},{1,3},{2,0},{3,1},{4,6},{5,7},{6,4},{7,5},{8,10},{9,11},{10,... | collective-permute-start | bytes 129032 | tf_op jit(solution)/shard_map/ppermute | solution.py:152
  32.7 12.6 %collective-permute-start.1 = (bf16[1344,128]{1,0:T(8,128)(2,1)S(1)}, bf16[1344,128]{1,0:T(8,128)(2,1)S(1)}, u32[]{:S(2)}, u32[]{:S(2)}) collective-permute-start(bf16[1344,128]{1,0:T(8,128)(2,1)S(1)} %collective-permute-done.refs_0_), channel_id=1, source_target_pairs={{0,1},{1,0},{2,3},{3,2},{4,5},{5,4},{6,7},{7,6},{8,9},{9,8},{10,11... | collective-permute-start | bytes 1032200 | tf_op jit(solution)/shard_map/ppermute | solution.py:154
  36.8 6.0 %collective-permute-start.7 = (bf16[168,128]{1,0:T(8,128)(2,1)S(1)}, bf16[168,128]{1,0:T(8,128)(2,1)S(1)}, u32[]{:S(2)}, u32[]{:S(2)}) collective-permute-start(bf16[168,128]{1,0:T(8,128)(2,1)S(1)} %reshape.13.refs_1_), channel_id=1, source_target_pairs={{0,1},{1,0},{2,3},{3,2},{4,5},{5,4},{6,7},{7,6},{8,9},{9,8},{10,11... | collective-permute-start | bytes 129032 | tf_op jit(solution)/shard_map/ppermute | solution.py:153
  38.7 6.6 %collective-permute-start.5 = (bf16[168,128]{1,0:T(8,128)(2,1)S(1)}, bf16[168,128]{1,0:T(8,128)(2,1)S(1)}, u32[]{:S(2)}, u32[]{:S(2)}) collective-permute-start(bf16[168,128]{1,0:T(8,128)(2,1)S(1)} %collective-permute-done.4.refs_1_), channel_id=1, source_target_pairs={{0,1},{1,0},{2,3},{3,2},{4,5},{5,4},{6,7},{7,6},{8,9},{9,8},{10,11... | collective-permute-start | bytes 129032 | tf_op jit(solution)/shard_map/ppermute | solution.py:154
  41.1 0.7 %copy-start.7 = (f32[7,3]{0,1:T(4,128)S(1)}, f32[7,3]{0,1:T(4,128)}, u32[]{:S(2)}) copy-start(f32[7,3]{0,1:T(4,128)} %param.14) | copy-start | bytes 256
  41.9 1.0 %copy-start = (bf16[21,4,16,128]{3,2,1,0:T(8,128)(2,1)S(1)}, bf16[21,4,16,128]{3,2,1,0:T(8,128)(2,1)}, u32[]{:S(2)}) copy-start(bf16[21,4,16,128]{3,2,1,0:T(8,128)(2,1)} %param.8) | copy-start | bytes 1032196
  41.9 1.0 %copy-start.1 = (f32[7,16,128]{2,1,0:T(8,128)S(1)}, f32[7,16,128]{2,1,0:T(8,128)}, u32[]{:S(2)}) copy-start(f32[7,16,128]{2,1,0:T(8,128)} %refs_4_.1) | copy-start | bytes 172036
  41.9 1.0 %copy-start.2 = (s32[16,128]{1,0:T(8,128)S(1)}, s32[16,128]{1,0:T(8,128)}, u32[]{:S(2)}) copy-start(s32[16,128]{1,0:T(8,128)} %refs_5_.3) | copy-start | bytes 24580
  41.9 1.0 %copy-start.3 = (s32[16,128]{1,0:T(8,128)S(1)}, s32[16,128]{1,0:T(8,128)}, u32[]{:S(2)}) copy-start(s32[16,128]{1,0:T(8,128)} %refs_6_.3) | copy-start | bytes 24580
  41.9 1.0 %copy-start.4 = (f32[7,8]{1,0:T(8,128)S(1)}, f32[7,8]{1,0:T(8,128)}, u32[]{:S(2)}) copy-start(f32[7,8]{1,0:T(8,128)} %refs_7_.3) | copy-start | bytes 676
  41.9 1.0 %copy-start.5 = (f32[7,8]{1,0:T(8,128)S(1)}, f32[7,8]{1,0:T(8,128)}, u32[]{:S(2)}) copy-start(f32[7,8]{1,0:T(8,128)} %refs_9_.2) | copy-start | bytes 676

commit v7 on v5

--- a/solution.py
+++ b/solution.py
@@ -10,14 +10,33 @@
 
 PAD_I = 24
 JS = 73
+EDGE = 96
 OS = 65
 
 
-def edge_rows(cells, axis, dim):
+def edges_kernel(rows, count, x_ref, head_ref, tail_ref, xs):
+    xs[...] = x_ref[...].astype(jnp.float32)
+    spare = head_ref.shape[0] - count
+    gap = jnp.zeros((spare, head_ref.shape[1]), jnp.float32)
+    head = xs[pl.ds(0, count, stride=rows), :]
+    tail = xs[pl.ds(rows - 1, count, stride=rows), :]
+    head_ref[...] = jnp.concatenate([head, gap], axis=0).astype(head_ref.dtype)
+    tail_ref[...] = jnp.concatenate([tail, gap], axis=0).astype(tail_ref.dtype)
+
+
+def edge_rows(cells, axis):
     count = lax.axis_size(axis)
     ends = count - 1
-    head = lax.slice_in_dim(cells, 0, 1, axis=dim)
-    tail = lax.slice_in_dim(cells, cells.shape[dim] - 1, cells.shape[dim], axis=dim)
+    local_modes, nfield, rows, width = cells.shape
+    blocks = local_modes * nfield
+    vmem = pl.BlockSpec(memory_space=pltpu.VMEM)
+    head, tail = pl.pallas_call(
+        functools.partial(edges_kernel, rows, blocks),
+        out_shape=(jax.ShapeDtypeStruct((EDGE, width), cells.dtype),) * 2,
+        in_specs=[vmem],
+        out_specs=(vmem, vmem),
+        scratch_shapes=[pltpu.VMEM((blocks * rows, width), jnp.float32)],
+    )(cells.reshape(blocks * rows, width))
     above = lax.ppermute(tail, axis, [(i, (i + 1) % count) for i in range(ends)])
     below = lax.ppermute(head, axis, [((i + 1) % count, i) for i in range(ends)])
     return above, below
@@ -36,11 +55,10 @@
         out_ref, fs, hs, os, cs, es = refs
     else:
         out_ref, fs, hs = refs
-    nloc = blocks[0].shape[0] // (nfield * (rows + 2))
+    nloc = (blocks[0].shape[0] - 2 * EDGE) // (nfield * rows)
     nmode = nblock * nloc
     span = fs.shape[0] // JS
     core = nfield * rows
-    per = nloc * nfield
 
     if final:
         mat = mat_ref[...]
@@ -63,9 +81,12 @@
         for jl in range(nloc):
             j = d * nloc + jl
             fs[pl.ds(j * JS, core), :] = blk[pl.ds(jl * core, core), :].astype(jnp.float32)
-        hs[...] = blk[pl.ds(nloc * core, 2 * per), :].astype(jnp.float32)
-        for side in range(2 * nfield):
-            fs[pl.ds(d * nloc * JS + core + side, nloc, stride=JS), :] = hs[pl.ds(side * nloc, nloc), :]
+        hs[...] = blk[pl.ds(nloc * core, 2 * EDGE), :].astype(jnp.float32)
+        for side in range(2):
+            for f in range(nfield):
+                fs[pl.ds(d * nloc * JS + core + 2 * f + side, nloc, stride=JS), :] = hs[
+                    pl.ds(side * EDGE + f, nloc, stride=nfield), :
+                ]
     if span > nmode:
         fs[pl.ds(nmode * JS, (span - nmode) * JS), :] = jnp.zeros(((span - nmode) * JS, width), jnp.float32)
 
@@ -141,13 +162,12 @@
     terms = coupling.shape[0]
     groups = lax.axis_size("modes")
     assert groups == 4
-    above, below = edge_rows(fields, "cells", 2)
+    above, below = edge_rows(fields, "cells")
     pack = jnp.concatenate(
         [
             fields.reshape(local_modes * nfield * rows, width),
-            jnp.stack([above[:, :, 0], below[:, :, 0]], axis=1)
-            .transpose(2, 1, 0, 3)
-            .reshape(2 * nfield * local_modes, width),
+            above,
+            below,
         ],
         axis=0,
     )
@@ -188,7 +208,7 @@
     def scratch(count):
         return [
             pltpu.VMEM((padded(count) * JS, width), jnp.float32),
-            pltpu.VMEM((2 * local_modes * nfield, width), jnp.float32),
+            pltpu.VMEM((2 * EDGE, width), jnp.float32),
         ]
 
     mix_scratch = [

time: 47.8 us -> 41.6 us (0.87)
  the two profiles are of different devices: /device:TPU:6 before, /device:TPU:7 now
where the time goes in v7:
time: 41.6 us; the launch traced here: 41.3 us
  starting transfers between devices  27 us (65%)
  Pallas kernels  7.92 us (19%)
  waiting for transfers between devices  5.02 us (12%)
  local copies, waits for them, and re-layouts  0.91 us (2%)
    ppermute x1, starting transfers between devices, edge_rows(): lax.ppermute(head, axis, [((i + 1) % count, i) for i in range(ends)])  12.5 us
    ppermute x1, starting transfers between devices, body(): lax.ppermute(counter, 'modes', [(i, i ^ 1) for i in range(groups)])  4.28 us
    ppermute x1, waiting for transfers between devices, body(): counter = lax.ppermute(pack, 'modes', [(i, i ^ 2) for i in range(groups)])  3.89 us
    ppermute x1, starting transfers between devices, body(): partner = lax.ppermute(pack, 'modes', [(i, i ^ 1) for i in range(groups)])  3.72 us
    ppermute x1, starting transfers between devices, body(): counter = lax.ppermute(pack, 'modes', [(i, i ^ 2) for i in range(groups)])  3.23 us
    ppermute x1, starting transfers between devices, edge_rows(): lax.ppermute(tail, axis, [(i, (i + 1) % count) for i in range(ends)])  3.19 us
    pallas_call x1, Pallas kernels, body(): pl.pallas_call(functools.partial(kernel, 1, True, True, True, nfield, row...  2.99 us
    pallas_call x1, Pallas kernels, body(): pl.pallas_call(functools.partial(kernel, 2, False, True, False, nfield, r...  2.4 us
  transfers between devices with their start and end apart: 5, of which 2 were waited for; matrix products, arithmetic and copies ran while one was open for 1% of the time, Pallas kernels for 8%

profile of v7, /device:TPU:7, one launch (start us, length us, event | category | flops | bytes accessed | tf_op | source)
XLA Modules:
  0.0 41.3 jit_solution(5032680876222854313)
XLA Ops:
  0.0 1.7 %shard_map.82 = (bf16[96,128]{1,0:T(8,128)(2,1)}, bf16[96,128]{1,0:T(8,128)(2,1)}) custom-call(bf16[1344,128]{1,0:T(8,128)(2,1)} %bitcast.5), custom_call_target="tpu_custom_call" | custom-call | tf_op jit(solution)/shard_map/pallas_call | solution.py:33
  1.7 3.2 %collective-permute-start = (bf16[96,128]{1,0:T(8,128)(2,1)}, bf16[96,128]{1,0:T(8,128)(2,1)S(1)}, u32[]{:S(2)}, u32[]{:S(2)}) collective-permute-start(bf16[96,128]{1,0:T(8,128)(2,1)} %get-tuple-element.7), channel_id=1, source_target_pairs={{0,4},{4,8},{8,12},{12,16},{16,20},{20,24},{24,28},{28,32},{32,36}... | collective-permute-start | bytes 73736 | tf_op jit(solution)/shard_map/ppermute | solution.py:40
  4.9 12.5 %collective-permute-start.1 = (bf16[96,128]{1,0:T(8,128)(2,1)}, bf16[96,128]{1,0:T(8,128)(2,1)S(1)}, u32[]{:S(2)}, u32[]{:S(2)}) collective-permute-start(bf16[96,128]{1,0:T(8,128)(2,1)} %get-tuple-element.8), channel_id=1, source_target_pairs={{4,0},{8,4},{12,8},{16,12},{20,16},{24,20},{28,24},{32,28},{36,32}... | collective-permute-start | bytes 73736 | tf_op jit(solution)/shard_map/ppermute | solution.py:41
  17.5 0.0 collective-permute-done
  17.5 1.1 %collective-permute-done.1 = bf16[96,128]{1,0:T(8,128)(2,1)S(1)} collective-permute-done((bf16[96,128]{1,0:T(8,128)(2,1)}, bf16[96,128]{1,0:T(8,128)(2,1)S(1)}, u32[]{:S(2)}, u32[]{:S(2)}) %collective-permute-start.1) | collective-permute-done | bytes 24608 | tf_op jit(solution)/shard_map/ppermute | solution.py:41
  18.7 3.2 %collective-permute-start.2 = (bf16[1536,128]{1,0:T(8,128)(2,1)S(1)}, bf16[1536,128]{1,0:T(8,128)(2,1)S(1)}, u32[]{:S(2)}, u32[]{:S(2)}) collective-permute-start(bf16[1536,128]{1,0:T(8,128)(2,1)S(1)} %pad_maximum_fusion.refs_0_), channel_id=1, source_target_pairs={{0,2},{1,3},{2,0},{3,1},{4,6},{5,7},{6,4},{7,5},{8,10},{9,11},{10,... | collective-permute-start | bytes 1179656 | tf_op jit(solution)/shard_map/ppermute | solution.py:175
  21.9 0.1 constant_dynamic-slice_fusion.3
  22.1 0.1 fusion.6
  22.2 0.0 copy-start.7
  22.2 3.7 %collective-permute-start.4 = (bf16[1536,128]{1,0:T(8,128)(2,1)S(1)}, bf16[1536,128]{1,0:T(8,128)(2,1)S(1)}, u32[]{:S(2)}, u32[]{:S(2)}) collective-permute-start(bf16[1536,128]{1,0:T(8,128)(2,1)S(1)} %pad_maximum_fusion.refs_0_), channel_id=1, source_target_pairs={{0,1},{1,0},{2,3},{3,2},{4,5},{5,4},{6,7},{7,6},{8,9},{9,8},{10,11... | collective-permute-start | bytes 1179656 | tf_op jit(solution)/shard_map/ppermute | solution.py:174
  25.9 3.9 %collective-permute-done.2.refs_0_ = bf16[1536,128]{1,0:T(8,128)(2,1)S(1)} collective-permute-done((bf16[1536,128]{1,0:T(8,128)(2,1)S(1)}, bf16[1536,128]{1,0:T(8,128)(2,1)S(1)}, u32[]{:S(2)}, u32[]{:S(2)}) %collective-permute-start.2) | collective-permute-done | bytes 393248 | tf_op jit(solution)/shard_map/ppermute | solution.py:175
  29.8 4.3 %collective-permute-start.3 = (bf16[1536,128]{1,0:T(8,128)(2,1)S(1)}, bf16[1536,128]{1,0:T(8,128)(2,1)S(1)}, u32[]{:S(2)}, u32[]{:S(2)}) collective-permute-start(bf16[1536,128]{1,0:T(8,128)(2,1)S(1)} %collective-permute-done.2.refs_0_), channel_id=1, source_target_pairs={{0,1},{1,0},{2,3},{3,2},{4,5},{5,4},{6,7},{7,6},{8,9},{9,8},{10,11... | collective-permute-start | bytes 1179656 | tf_op jit(solution)/shard_map/ppermute | solution.py:176
  34.1 0.1 fusion.7
  34.2 0.1 copy.10.refs_7_
  34.3 0.1 pad_maximum_fusion.1
  34.4 0.5 %copy-done.8 = pred[48]{0:T(512)(128)(4,1)S(1)} copy-done((pred[48]{0:T(512)(128)(4,1)S(1)}, pred[48]{0:T(512)(128)(4,1)}, u32[]{:S(2)}) %copy-start.8) | copy-done | bytes 72
  35.0 0.0 copy-start
  35.0 0.0 copy-start.1
  35.0 0.0 copy-start.2
  35.0 0.0 copy-start.3
  35.0 0.0 copy-start.4
  35.1 0.8 %shard_map.83.refs_1_ = bf16[16,32,768]{2,1,0:T(8,128)(2,1)S(1)} custom-call(bf16[1536,128]{1,0:T(8,128)(2,1)S(1)} %collective-permute-done.2.refs_0_), custom_call_target="tpu_custom_call" | custom-call | flops 4718592 | bytes 1179648 | tf_op jit(solution)/shard_map/pallas_call | solution.py:235
  35.9 2.4 %shard_map.84.refs_9_ = f32[21,4,16,128]{3,2,1,0:T(8,128)S(1)} custom-call(bf16[1536,128]{1,0:T(8,128)(2,1)S(1)} %pad_maximum_fusion.refs_0_, bf16[1536,128]{1,0:T(8,128)(2,1)S(1)} %collective-permute-done.4.refs_1_, bf16[168,48]{1,0:T(8,128)(2,1)S(1)} %bitcast.3, f32[7,16,128]{2,1,0:T(8,128)S(1)} %copy-done, s32[16,128]{1,0:T(8,128)S(1)} %copy-done.1, ...), custom_call_target="tpu_custom_call" | custom-call | flops 198180864 | bytes 2555904 | tf_op jit(solution)/shard_map/pallas_call | solution.py:226
  38.3 3.0 %shard_map.85 = bf16[21,4,16,128]{3,2,1,0:T(8,128)(2,1)} custom-call(bf16[1536,128]{1,0:T(8,128)(2,1)S(1)} %collective-permute-done.3.refs_0_, bf16[16,32,768]{2,1,0:T(8,128)(2,1)S(1)} %shard_map.83.refs_1_, bf16[168,64]{1,0:T(8,128)(2,1)S(1)} %bitcast.4, f32[7,16,128]{2,1,0:T(8,128)S(1)} %copy-done, s32[16,128]{1,0:T(8,128)S(1)} %copy-done.1, ...), custom_call_target="tpu_custom_call" | custom-call | flops 264241152 | bytes 2949120 | tf_op jit(solution)/shard_map/pallas_call | solution.py:247
  (16 shorter events, 0.1 us)
Async XLA Ops:
  0.0 18.6 %copy-start.5 = (bf16[21,4,16,128]{3,2,1,0:T(8,128)(2,1)S(1)}, bf16[21,4,16,128]{3,2,1,0:T(8,128)(2,1)}, u32[]{:S(2)}) copy-start(bf16[21,4,16,128]{3,2,1,0:T(8,128)(2,1)} %param.8) | copy-start | bytes 1032196
  1.7 15.8 %collective-permute-start = (bf16[96,128]{1,0:T(8,128)(2,1)}, bf16[96,128]{1,0:T(8,128)(2,1)S(1)}, u32[]{:S(2)}, u32[]{:S(2)}) collective-permute-start(bf16[96,128]{1,0:T(8,128)(2,1)} %get-tuple-element.7), channel_id=1, source_target_pairs={{0,4},{4,8},{8,12},{12,16},{16,20},{20,24},{24,28},{28,32},{32,36}... | collective-permute-start | bytes 73736 | tf_op jit(solution)/shard_map/ppermute | solution.py:40
  4.9 13.7 %collective-permute-start.1 = (bf16[96,128]{1,0:T(8,128)(2,1)}, bf16[96,128]{1,0:T(8,128)(2,1)S(1)}, u32[]{:S(2)}, u32[]{:S(2)}) collective-permute-start(bf16[96,128]{1,0:T(8,128)(2,1)} %get-tuple-element.8), channel_id=1, source_target_pairs={{4,0},{8,4},{12,8},{16,12},{20,16},{24,20},{28,24},{32,28},{36,32}... | collective-permute-start | bytes 73736 | tf_op jit(solution)/shard_map/ppermute | solution.py:41
  18.6 3.3 %copy-start.6 = (bf16[7,84,84]{2,1,0:T(8,128)(2,1)S(1)}, bf16[7,84,84]{2,1,0:T(8,128)(2,1)}, u32[]{:S(2)}) copy-start(bf16[7,84,84]{2,1,0:T(8,128)(2,1)} %param.9) | copy-start | bytes 296356
  18.7 11.2 %collective-permute-start.2 = (bf16[1536,128]{1,0:T(8,128)(2,1)S(1)}, bf16[1536,128]{1,0:T(8,128)(2,1)S(1)}, u32[]{:S(2)}, u32[]{:S(2)}) collective-permute-start(bf16[1536,128]{1,0:T(8,128)(2,1)S(1)} %pad_maximum_fusion.refs_0_), channel_id=1, source_target_pairs={{0,2},{1,3},{2,0},{3,1},{4,6},{5,7},{6,4},{7,5},{8,10},{9,11},{10,... | collective-permute-start | bytes 1179656 | tf_op jit(solution)/shard_map/ppermute | solution.py:175
  22.2 12.0 %copy-start.7 = (f32[7,3]{0,1:T(4,128)S(1)}, f32[7,3]{0,1:T(4,128)}, u32[]{:S(2)}) copy-start(f32[7,3]{0,1:T(4,128)} %param.14) | copy-start | bytes 256
  22.2 13.7 %collective-permute-start.4 = (bf16[1536,128]{1,0:T(8,128)(2,1)S(1)}, bf16[1536,128]{1,0:T(8,128)(2,1)S(1)}, u32[]{:S(2)}, u32[]{:S(2)}) collective-permute-start(bf16[1536,128]{1,0:T(8,128)(2,1)S(1)} %pad_maximum_fusion.refs_0_), channel_id=1, source_target_pairs={{0,1},{1,0},{2,3},{3,2},{4,5},{5,4},{6,7},{7,6},{8,9},{9,8},{10,11... | collective-permute-start | bytes 1179656 | tf_op jit(solution)/shard_map/ppermute | solution.py:174
  29.8 8.5 %collective-permute-start.3 = (bf16[1536,128]{1,0:T(8,128)(2,1)S(1)}, bf16[1536,128]{1,0:T(8,128)(2,1)S(1)}, u32[]{:S(2)}, u32[]{:S(2)}) collective-permute-start(bf16[1536,128]{1,0:T(8,128)(2,1)S(1)} %collective-permute-done.2.refs_0_), channel_id=1, source_target_pairs={{0,1},{1,0},{2,3},{3,2},{4,5},{5,4},{6,7},{7,6},{8,9},{9,8},{10,11... | collective-permute-start | bytes 1179656 | tf_op jit(solution)/shard_map/ppermute | solution.py:176
  34.3 0.7 %copy-start.8 = (pred[48]{0:T(512)(128)(4,1)S(1)}, pred[48]{0:T(512)(128)(4,1)}, u32[]{:S(2)}) copy-start(pred[48]{0:T(512)(128)(4,1)} %constant.82.clone.1) | copy-start | bytes 148
  35.0 0.9 %copy-start = (f32[7,16,128]{2,1,0:T(8,128)S(1)}, f32[7,16,128]{2,1,0:T(8,128)}, u32[]{:S(2)}) copy-start(f32[7,16,128]{2,1,0:T(8,128)} %refs_3_.3) | copy-start | bytes 172036
  35.0 0.9 %copy-start.1 = (s32[16,128]{1,0:T(8,128)S(1)}, s32[16,128]{1,0:T(8,128)}, u32[]{:S(2)}) copy-start(s32[16,128]{1,0:T(8,128)} %refs_4_.3) | copy-start | bytes 24580
  35.0 0.9 %copy-start.2 = (s32[16,128]{1,0:T(8,128)S(1)}, s32[16,128]{1,0:T(8,128)}, u32[]{:S(2)}) copy-start(s32[16,128]{1,0:T(8,128)} %refs_5_.3) | copy-start | bytes 24580
  35.0 0.9 %copy-start.3 = (f32[7,8]{1,0:T(8,128)S(1)}, f32[7,8]{1,0:T(8,128)}, u32[]{:S(2)}) copy-start(f32[7,8]{1,0:T(8,128)} %refs_6_.3) | copy-start | bytes 676
  35.0 0.9 %copy-start.4 = (f32[7,8]{1,0:T(8,128)S(1)}, f32[7,8]{1,0:T(8,128)}, u32[]{:S(2)}) copy-start(f32[7,8]{1,0:T(8,128)} %refs_8_.3) | copy-start | bytes 676

commit v8 on v5

--- a/solution.py
+++ b/solution.py
@@ -11,16 +11,6 @@
 PAD_I = 24
 JS = 73
 OS = 65
-
-
-def edge_rows(cells, axis, dim):
-    count = lax.axis_size(axis)
-    ends = count - 1
-    head = lax.slice_in_dim(cells, 0, 1, axis=dim)
-    tail = lax.slice_in_dim(cells, cells.shape[dim] - 1, cells.shape[dim], axis=dim)
-    above = lax.ppermute(tail, axis, [(i, (i + 1) % count) for i in range(ends)])
-    below = lax.ppermute(head, axis, [((i + 1) % count, i) for i in range(ends)])
-    return above, below
 
 
 def kernel(nblock, prev, final, partial, nfield, rows, width, terms, nmat, nchar, *refs):
@@ -33,14 +23,13 @@
         refs = refs[7:]
         if partial:
             part_ref, refs = refs[0], refs[1:]
-        out_ref, fs, hs, os, cs, es = refs
+        out_ref, edge_ref, fs, hs, os, cs, es = refs
     else:
-        out_ref, fs, hs = refs
-    nloc = blocks[0].shape[0] // (nfield * (rows + 2))
+        out_ref, edge_ref, fs, hs = refs
+    nloc = blocks[0].shape[0] // (nfield * rows)
     nmode = nblock * nloc
     span = fs.shape[0] // JS
     core = nfield * rows
-    per = nloc * nfield
 
     if final:
         mat = mat_ref[...]
@@ -63,9 +52,6 @@
         for jl in range(nloc):
             j = d * nloc + jl
             fs[pl.ds(j * JS, core), :] = blk[pl.ds(jl * core, core), :].astype(jnp.float32)
-        hs[...] = blk[pl.ds(nloc * core, 2 * per), :].astype(jnp.float32)
-        for side in range(2 * nfield):
-            fs[pl.ds(d * nloc * JS + core + side, nloc, stride=JS), :] = hs[pl.ds(side * nloc, nloc), :]
     if span > nmode:
         fs[pl.ds(nmode * JS, (span - nmode) * JS), :] = jnp.zeros(((span - nmode) * JS, width), jnp.float32)
 
@@ -76,12 +62,16 @@
     def row(r):
         return fs[pl.ds(r, span, stride=JS), :]
 
+    for e, r in enumerate((0, 1, rows - 2, rows - 1)):
+        for f in range(nfield):
+            edge_ref[e, f] = row(f * rows + r).astype(edge_ref.dtype)
+
     def derive(x):
         comps = []
         grads = None
         for f in range(nfield):
-            up = jnp.where(x == 0, core + 2 * f, f * rows + x - 1)
-            down = jnp.where(x == rows - 1, core + 2 * f + 1, f * rows + x + 1)
+            up = f * rows + x - 1
+            down = f * rows + x + 1
             center = row(f * rows + x)
             above = row(up)
             below = row(down)
@@ -100,7 +90,7 @@
             out_ref[x] = derive(x)
             return carry
 
-        lax.fori_loop(0, rows, keep, 0, unroll=8)
+        lax.fori_loop(1, rows - 1, keep, 0, unroll=7)
         return
 
     def step(x, carry):
@@ -125,13 +115,85 @@
             os[pl.ds(f * rows + x, PAD_I, stride=OS), :] = diffuse
         return carry
 
-    lax.fori_loop(0, rows, step, 0, unroll=16)
+    lax.fori_loop(1, rows - 1, step, 0, unroll=14)
 
     for i in range(out_ref.shape[0]):
         value = os[pl.ds(i * OS, core), :].reshape(nfield, rows, width)
         if partial:
             value = value + part_ref[i]
         out_ref[i] = value.astype(out_ref.dtype)
+
+
+def edge_kernel(nfield, rows, width, terms, nmat, nchar, e1, e2, e3, up_ref, down_ref, cp_ref, kl_ref,
+                mat_ref, chr_ref, mt_ref, ct_ref, et_ref, inner_ref, out_ref):
+    mat = mat_ref[...]
+    chs = chr_ref[...]
+    cond, expand = [], []
+    for k in range(terms):
+        mv = jnp.zeros((rows, width), jnp.float32)
+        ev = jnp.zeros((rows, width), jnp.float32)
+        for m in range(nmat):
+            hit = mat == m
+            mv = jnp.where(hit, mt_ref[k, m], mv)
+            ev = jnp.where(hit, et_ref[k, m], ev)
+        cv = jnp.zeros((rows, width), jnp.float32)
+        for q in range(nchar):
+            cv = jnp.where(chs == q, ct_ref[k, q], cv)
+        kl = kl_ref[k]
+        cond.append(kl * mv * cv)
+        expand.append(kl * ev)
+    pieces = (e1, e2, e3)
+
+    def gather(e, f):
+        return jnp.concatenate([p[e, f] for p in pieces], axis=0).astype(jnp.float32)
+
+    span = sum(p.shape[2] for p in pieces)
+    lane = lax.broadcasted_iota(jnp.int32, (span, width), 1)
+    first = lane == 0
+    last = lane == width - 1
+    results = {}
+    for x, e_mid, e_in, outer in ((0, 0, 1, up_ref), (rows - 1, 3, 2, down_ref)):
+        comps = []
+        grads = None
+        for f in range(nfield):
+            center = gather(e_mid, f)
+            inner = gather(e_in, f)
+            edge = outer[f].astype(jnp.float32)
+            above, below = (edge, inner) if x == 0 else (inner, edge)
+            left = jnp.where(first, 0.0, pltpu.roll(center, 1, 1))
+            right = jnp.where(last, 0.0, pltpu.roll(center, width - 1, 1))
+            lap = 4.0 * center - above - below - left - right
+            comps.append(lap.astype(jnp.bfloat16))
+            if f == 0:
+                gx = 0.5 * (below - above)
+                gy = 0.5 * (right - left)
+                grads = (gx.astype(jnp.bfloat16), gy.astype(jnp.bfloat16))
+        operand = jnp.concatenate(comps + list(grads), axis=1)
+        mixed = jnp.dot(cp_ref[...], operand, preferred_element_type=jnp.float32)
+        cvals = [jnp.broadcast_to(cond[k][x:x + 1, :], (PAD_I, width)) for k in range(terms)]
+        evals = [jnp.broadcast_to(expand[k][x:x + 1, :], (PAD_I, width)) for k in range(terms)]
+        for f in range(nfield):
+            diffuse = None
+            for k in range(terms):
+                part = cvals[k] * mixed[k * PAD_I:(k + 1) * PAD_I, f * width:(f + 1) * width]
+                diffuse = part if diffuse is None else diffuse + part
+            if f in (1, 2):
+                c = nfield + f - 1
+                strain = None
+                for k in range(terms):
+                    part = evals[k] * mixed[k * PAD_I:(k + 1) * PAD_I, c * width:(c + 1) * width]
+                    strain = part if strain is None else strain + part
+                diffuse = diffuse - strain
+            results[(x, f)] = diffuse
+    row = lax.broadcasted_iota(jnp.int32, (rows, width), 0)
+    for i in range(out_ref.shape[0]):
+        for f in range(nfield):
+            value = inner_ref[i, f]
+            value = jnp.where(row == 0, jnp.broadcast_to(results[(0, f)][i:i + 1, :], (rows, width)), value)
+            value = jnp.where(
+                row == rows - 1, jnp.broadcast_to(results[(rows - 1, f)][i:i + 1, :], (rows, width)), value
+            )
+            out_ref[i, f] = value.astype(out_ref.dtype)
 
 
 def body(
@@ -141,18 +203,9 @@
     terms = coupling.shape[0]
     groups = lax.axis_size("modes")
     assert groups == 4
-    above, below = edge_rows(fields, "cells", 2)
-    pack = jnp.concatenate(
-        [
-            fields.reshape(local_modes * nfield * rows, width),
-            jnp.stack([above[:, :, 0], below[:, :, 0]], axis=1)
-            .transpose(2, 1, 0, 3)
-            .reshape(2 * nfield * local_modes, width),
-        ],
-        axis=0,
-    )
-    partner = lax.ppermute(pack, "modes", [(i, i ^ 1) for i in range(groups)])
-    counter = lax.ppermute(pack, "modes", [(i, i ^ 2) for i in range(groups)])
+    cells = fields.reshape(local_modes * nfield * rows, width)
+    counter = lax.ppermute(cells, "modes", [(i, i ^ 2) for i in range(groups)])
+    partner = lax.ppermute(cells, "modes", [(i, i ^ 1) for i in range(groups)])
     diagonal = lax.ppermute(counter, "modes", [(i, i ^ 1) for i in range(groups)])
     me = lax.axis_index("modes")
     first_mode = me * local_modes
@@ -188,8 +241,11 @@
     def scratch(count):
         return [
             pltpu.VMEM((padded(count) * JS, width), jnp.float32),
-            pltpu.VMEM((2 * local_modes * nfield, width), jnp.float32),
+            pltpu.VMEM((8, width), jnp.float32),
         ]
+
+    def edge_shape(count):
+        return jax.ShapeDtypeStruct((4, nfield, padded(count), width), fields.dtype)
 
     mix_scratch = [
         pltpu.VMEM((PAD_I * OS, width), jnp.float32),
@@ -203,36 +259,49 @@
             bytes_accessed=span * comps * rows * width * 2 + fields.size * 8,
         )
 
-    partial = pl.pallas_call(
+    partial, e1 = pl.pallas_call(
         functools.partial(kernel, 2, False, True, False, nfield, rows, width, terms, nmat, nchar),
-        out_shape=jax.ShapeDtypeStruct(fields.shape, jnp.float32),
+        out_shape=(jax.ShapeDtypeStruct(fields.shape, jnp.float32), edge_shape(2)),
         in_specs=[vmem] * 6 + [smem] * 3,
-        out_specs=vmem,
+        out_specs=(vmem, vmem),
         scratch_shapes=scratch(2) + mix_scratch,
         compiler_params=params,
         cost_estimate=mix_cost(padded(2)),
-    )(pack, partner, columns([(0, 2)]), *tables)
-    ops = pl.pallas_call(
+    )(cells, partner, columns([(0, 2)]), *tables)
+    ops, e2 = pl.pallas_call(
         functools.partial(kernel, 1, False, False, False, nfield, rows, width, terms, nmat, nchar),
-        out_shape=jax.ShapeDtypeStruct((rows, padded(1), comps * width), jnp.bfloat16),
+        out_shape=(jax.ShapeDtypeStruct((rows, padded(1), comps * width), jnp.bfloat16), edge_shape(1)),
         in_specs=[vmem],
-        out_specs=vmem,
+        out_specs=(vmem, vmem),
         scratch_shapes=scratch(1),
         compiler_params=params,
         cost_estimate=pl.CostEstimate(
             flops=12 * padded(1) * comps * rows * width, transcendentals=0,
-            bytes_accessed=pack.size * 2 + rows * padded(1) * comps * width * 2,
+            bytes_accessed=cells.size * 2 + rows * padded(1) * comps * width * 2,
         ),
     )(counter)
-    return pl.pallas_call(
+    run = pl.pallas_call(
         functools.partial(kernel, 1, True, True, True, nfield, rows, width, terms, nmat, nchar),
-        out_shape=jax.ShapeDtypeStruct(fields.shape, fields.dtype),
+        out_shape=(jax.ShapeDtypeStruct(fields.shape, jnp.float32), edge_shape(1)),
         in_specs=[vmem] * 6 + [smem] * 3 + [vmem],
-        out_specs=vmem,
+        out_specs=(vmem, vmem),
         scratch_shapes=scratch(1) + mix_scratch,
         compiler_params=params,
         cost_estimate=mix_cost(2 * padded(1)),
-    )(diagonal, ops, columns([(2, 3), (3, 4)]), *tables, partial)
+    )
+    inner, e3 = run(diagonal, ops, columns([(2, 3), (3, 4)]), *tables, partial)
+    head = jnp.concatenate([e1[0], e2[0], e3[0]], axis=1)
+    tail = jnp.concatenate([e1[3], e2[3], e3[3]], axis=1)
+    count = lax.axis_size("cells")
+    above = lax.ppermute(tail, "cells", [(i, i + 1) for i in range(count - 1)])
+    below = lax.ppermute(head, "cells", [(i + 1, i) for i in range(count - 1)])
+    return pl.pallas_call(
+        functools.partial(edge_kernel, nfield, rows, width, terms, nmat, nchar),
+        out_shape=jax.ShapeDtypeStruct(fields.shape, fields.dtype),
+        in_specs=[vmem] * 9 + [smem] * 3 + [vmem],
+        out_specs=vmem,
+        compiler_params=params,
+    )(e1, e2, e3, above, below, columns([(0, 2), (2, 3), (3, 4)]), *tables, inner)
 
 
 def solution(mesh):

time: 47.8 us -> 41.9 us (0.88); the launches traced: 46.9 us -> 41.5 us
  waiting for transfers between devices: 14.6 us -> 7.67 us
  local copies, waits for them, and re-layouts: 2.09 us -> 2.88 us
  Pallas kernels: 6.21 us -> 6.98 us
    ppermute x4, waiting for transfers between devices: 14.6 us -> 7.67 us  [the longest x1 4.13 us: body(): above = lax.ppermute(tail, 'cells', [(i, i + 1) for i in range(count - 1)])]
    slice x1 -> x0, local copies, waits for them, and re-layouts: 1.12 us -> none  [edge_rows(): lax.slice_in_dim(cells, cells.shape[dim] - 1, cells.shape[dim], axis=dim)]
    dynamic_slice x1, local copies, waits for them, and re-layouts: 0.14 us -> 1.23 us  [body(): lax.dynamic_slice_in_dim(weights, (me ^ flip) * local_modes, local_modes, 2)]
    pallas_call x1 -> x2, Pallas kernels: 3.01 us -> 4.06 us  [the longest x1 2.13 us: body(): inner, e3 = run(diagonal, ops, columns([(2, 3), (3, 4)]), *tables, partial)]
    unnamed x21 -> x17, local copies, waits for them, and re-layouts: 0.7 us -> 1.37 us
  transfers between devices with their start and end apart: 5 -> 5, of which waited for: 2 -> 2; matrix products, arithmetic and copies ran while one was open for 1% -> 4% of each run, Pallas kernels for 7% -> 7%
where the time goes in v8:
time: 41.9 us; the launch traced here: 41.5 us
  starting transfers between devices  23.5 us (56%)
  waiting for transfers between devices  7.67 us (18%)
  Pallas kernels  6.98 us (17%)
  local copies, waits for them, and re-layouts  2.88 us (7%)
    ppermute x1, starting transfers between devices, body(): below = lax.ppermute(head, 'cells', [(i + 1, i) for i in range(count - 1)])  11.9 us
    ppermute x1, starting transfers between devices, body(): counter = lax.ppermute(cells, 'modes', [(i, i ^ 2) for i in range(groups)])  4.27 us
    ppermute x1, waiting for transfers between devices, body(): above = lax.ppermute(tail, 'cells', [(i, i + 1) for i in range(count - 1)])  4.13 us
    ppermute x1, waiting for transfers between devices, body(): counter = lax.ppermute(cells, 'modes', [(i, i ^ 2) for i in range(groups)])  3.53 us
    ppermute x1, starting transfers between devices, body(): above = lax.ppermute(tail, 'cells', [(i, i + 1) for i in range(count - 1)])  3.49 us
    pallas_call x1, Pallas kernels, body(): pl.pallas_call(functools.partial(kernel, 2, False, True, False, nfield, r...  2.23 us
    pallas_call x1, Pallas kernels, body(): inner, e3 = run(diagonal, ops, columns([(2, 3), (3, 4)]), *tables, partial)  2.13 us
    pallas_call x1, Pallas kernels, body(): pl.pallas_call(functools.partial(edge_kernel, nfield, rows, width, terms,...  1.93 us
  transfers between devices with their start and end apart: 5, of which 2 were waited for; matrix products, arithmetic and copies ran while one was open for 4% of the time, Pallas kernels for 7%

profile of v8, /device:TPU:6, one launch (start us, length us, event | category | flops | bytes accessed | tf_op | source)
XLA Modules:
  0.0 41.5 jit_solution(2477736877223239158)
XLA Ops:
  0.0 4.3 %collective-permute-start.1 = (bf16[1344,128]{1,0:T(8,128)(2,1)}, bf16[1344,128]{1,0:T(8,128)(2,1)S(1)}, u32[]{:S(2)}, u32[]{:S(2)}) collective-permute-start(bf16[1344,128]{1,0:T(8,128)(2,1)} %bitcast.17), channel_id=1, source_target_pairs={{0,2},{1,3},{2,0},{3,1},{4,6},{5,7},{6,4},{7,5},{8,10},{9,11},{10,... | collective-permute-start | bytes 1032200 | tf_op jit(solution)/shard_map/ppermute | solution.py:207
  4.3 1.9 %collective-permute-start = (bf16[1344,128]{1,0:T(8,128)(2,1)}, bf16[1344,128]{1,0:T(8,128)(2,1)S(1)}, u32[]{:S(2)}, u32[]{:S(2)}) collective-permute-start(bf16[1344,128]{1,0:T(8,128)(2,1)} %bitcast.18), channel_id=1, source_target_pairs={{0,1},{1,0},{2,3},{3,2},{4,5},{5,4},{6,7},{7,6},{8,9},{9,8},{10,11... | collective-permute-start | bytes 1032200 | tf_op jit(solution)/shard_map/ppermute | solution.py:208
  6.2 1.2 %constant_dynamic-slice_fusion.3 = (bf16[7,21,21]{2,1,0:T(8,128)(2,1)S(1)}, bf16[7,21,21]{2,1,0:T(8,128)(2,1)S(1)}, bf16[7,21,21]{2,1,0:T(8,128)(2,1)S(1)}, bf16[7,21,21]{2,1,0:T(8,128)(2,1)S(1)}) fusion(bf16[7,84,84]{2,1,0:T(8,128)(2,1)} %param.9, s32[]{:T(128)S(6)} %select_n.22, s32[]{:T(128)S(6)} %select_n.24, s32[]{:T(128)S(6)} %select_n.28, s32[]{:T(128)S(6)} %select_n.26), kind=kLoop, calls=%fused_computation.21 | loop fusion | bytes 49408 | tf_op jit(solution)/shard_map/dynamic_slice | solution.py:215
  7.5 0.0 copy-start.7
  7.5 0.1 fusion.6
  7.6 0.5 %copy-done.7 = pred[48]{0:T(512)(128)(4,1)S(1)} copy-done((pred[48]{0:T(512)(128)(4,1)S(1)}, pred[48]{0:T(512)(128)(4,1)}, u32[]{:S(2)}) %copy-start.7) | copy-done | bytes 72
  8.1 0.7 %copy-done.6 = f32[7,3]{0,1:T(4,128)S(1)} copy-done((f32[7,3]{0,1:T(4,128)S(1)}, f32[7,3]{0,1:T(4,128)}, u32[]{:S(2)}) %copy-start.6) | copy-done | bytes 108
  8.8 0.1 copy.9.refs_7_.ct_ref
  8.9 0.1 fusion.7
  9.0 3.5 %collective-permute-done.1.refs_0_ = bf16[1344,128]{1,0:T(8,128)(2,1)S(1)} collective-permute-done((bf16[1344,128]{1,0:T(8,128)(2,1)}, bf16[1344,128]{1,0:T(8,128)(2,1)S(1)}, u32[]{:S(2)}, u32[]{:S(2)}) %collective-permute-start.1) | collective-permute-done | bytes 344096 | tf_op jit(solution)/shard_map/ppermute | solution.py:207
  12.5 1.9 %collective-permute-start.2 = (bf16[1344,128]{1,0:T(8,128)(2,1)S(1)}, bf16[1344,128]{1,0:T(8,128)(2,1)S(1)}, u32[]{:S(2)}, u32[]{:S(2)}) collective-permute-start(bf16[1344,128]{1,0:T(8,128)(2,1)S(1)} %collective-permute-done.1.refs_0_), channel_id=1, source_target_pairs={{0,1},{1,0},{2,3},{3,2},{4,5},{5,4},{6,7},{7,6},{8,9},{9,8},{10,11... | collective-permute-start | bytes 1032200 | tf_op jit(solution)/shard_map/ppermute | solution.py:209
  14.5 0.1 pad_maximum_fusion.2
  14.6 0.0 copy-start
  14.6 0.0 copy-start.2
  14.6 0.0 copy-start.5
  14.6 0.7 %shard_map.83 = (bf16[16,32,768]{2,1,0:T(8,128)(2,1)S(1)}, bf16[4,4,32,128]{3,2,1,0:T(8,128)(2,1)S(1)}) custom-call(bf16[1344,128]{1,0:T(8,128)(2,1)S(1)} %collective-permute-done.1.refs_0_), custom_call_target="tpu_custom_call" | custom-call | flops 4718592 | bytes 1130496 | tf_op jit(solution)/shard_map/pallas_call | solution.py:271
  15.4 0.0 copy-done
  15.4 2.2 %shard_map.82 = (f32[21,4,16,128]{3,2,1,0:T(8,128)S(1)}, bf16[4,4,48,128]{3,2,1,0:T(8,128)(2,1)S(1)}) custom-call(bf16[1344,128]{1,0:T(8,128)(2,1)S(1)} %bitcast.19, bf16[1344,128]{1,0:T(8,128)(2,1)S(1)} %collective-permute-done.refs_1_, bf16[168,48]{1,0:T(8,128)(2,1)S(1)} %bitcast.21, f32[7,16,128]{2,1,0:T(8,128)S(1)} %copy-done, s32[16,128]{1,0:T(8,128)S(1)} %copy-done.2, ...), custom_call_target="tpu_custom_call" | custom-call | flops 198180864 | bytes 2555904 | tf_op jit(solution)/shard_map/pallas_call | solution.py:262
  17.7 2.1 %shard_map.84 = (f32[21,4,16,128]{3,2,1,0:T(8,128)S(1)}, bf16[4,4,32,128]{3,2,1,0:T(8,128)(2,1)S(1)}) custom-call(bf16[1344,128]{1,0:T(8,128)(2,1)S(1)} %collective-permute-done.2.refs_0_, bf16[16,32,768]{2,1,0:T(8,128)(2,1)S(1)} %get-tuple-element.13.refs_1_, bf16[168,64]{1,0:T(8,128)(2,1)S(1)} %bitcast.20, f32[7,16,128]{2,1,0:T(8,128)S(1)} %copy-done, ...), custom_call_target="tpu_custom_call" | custom-call | flops 264241152 | bytes 2949120 | tf_op jit(solution)/shard_map/pallas_call | solution.py:292
  19.9 3.5 %collective-permute-start.3 = (bf16[4,112,128]{2,1,0:T(8,128)(2,1)S(1)}, bf16[4,112,128]{2,1,0:T(8,128)(2,1)S(1)}, u32[]{:S(2)}, u32[]{:S(2)}) collective-permute-start(bf16[4,112,128]{2,1,0:T(8,128)(2,1)S(1)} %pad_maximum_fusion), channel_id=1, source_target_pairs={{0,4},{4,8},{8,12},{12,16},{16,20},{20,24},{24,28},{28,32},{32,36}... | collective-permute-start | bytes 344072 | tf_op jit(solution)/shard_map/ppermute | solution.py:296
  23.4 11.9 %collective-permute-start.4 = (bf16[4,112,128]{2,1,0:T(8,128)(2,1)S(1)}, bf16[4,112,128]{2,1,0:T(8,128)(2,1)S(1)}, u32[]{:S(2)}, u32[]{:S(2)}) collective-permute-start(bf16[4,112,128]{2,1,0:T(8,128)(2,1)S(1)} %pad_maximum_fusion.1), channel_id=1, source_target_pairs={{4,0},{8,4},{12,8},{16,12},{20,16},{24,20},{28,24},{32,28},{36,32}... | collective-permute-start | bytes 344072 | tf_op jit(solution)/shard_map/ppermute | solution.py:297
  35.3 0.2 concatenate.23
  35.5 4.1 %collective-permute-done.3.up_ref = bf16[4,112,128]{2,1,0:T(8,128)(2,1)S(1)} collective-permute-done((bf16[4,112,128]{2,1,0:T(8,128)(2,1)S(1)}, bf16[4,112,128]{2,1,0:T(8,128)(2,1)S(1)}, u32[]{:S(2)}, u32[]{:S(2)}) %collective-permute-start.3) | collective-permute-done | bytes 114720 | tf_op jit(solution)/shard_map/ppermute | solution.py:296
  39.6 1.9 %shard_map.85 = bf16[21,4,16,128]{3,2,1,0:T(8,128)(2,1)} custom-call(bf16[4,4,48,128]{3,2,1,0:T(8,128)(2,1)S(1)} %get-tuple-element.11.e1, bf16[4,4,32,128]{3,2,1,0:T(8,128)(2,1)S(1)} %get-tuple-element.12.e2, bf16[4,4,32,128]{3,2,1,0:T(8,128)(2,1)S(1)} %get-tuple-element.15.e3, bf16[4,112,128]{2,1,0:T(8,128)(2,1)S(1)} %collective-permute-done.3.up_ref, ...), custom_call_target="tpu_custom_call" | custom-call | tf_op jit(solution)/shard_map/pallas_call | solution.py:298
  (19 shorter events, 0.1 us)
Async XLA Ops:
  0.0 12.5 %collective-permute-start.1 = (bf16[1344,128]{1,0:T(8,128)(2,1)}, bf16[1344,128]{1,0:T(8,128)(2,1)S(1)}, u32[]{:S(2)}, u32[]{:S(2)}) collective-permute-start(bf16[1344,128]{1,0:T(8,128)(2,1)} %bitcast.17), channel_id=1, source_target_pairs={{0,2},{1,3},{2,0},{3,1},{4,6},{5,7},{6,4},{7,5},{8,10},{9,11},{10,... | collective-permute-start | bytes 1032200 | tf_op jit(solution)/shard_map/ppermute | solution.py:207
  4.3 11.1 %collective-permute-start = (bf16[1344,128]{1,0:T(8,128)(2,1)}, bf16[1344,128]{1,0:T(8,128)(2,1)S(1)}, u32[]{:S(2)}, u32[]{:S(2)}) collective-permute-start(bf16[1344,128]{1,0:T(8,128)(2,1)} %bitcast.18), channel_id=1, source_target_pairs={{0,1},{1,0},{2,3},{3,2},{4,5},{5,4},{6,7},{7,6},{8,9},{9,8},{10,11... | collective-permute-start | bytes 1032200 | tf_op jit(solution)/shard_map/ppermute | solution.py:208
  7.5 0.7 %copy-start.7 = (pred[48]{0:T(512)(128)(4,1)S(1)}, pred[48]{0:T(512)(128)(4,1)}, u32[]{:S(2)}) copy-start(pred[48]{0:T(512)(128)(4,1)} %constant.73.clone.1) | copy-start | bytes 148
  8.1 0.7 %copy-start.6 = (f32[7,3]{0,1:T(4,128)S(1)}, f32[7,3]{0,1:T(4,128)}, u32[]{:S(2)}) copy-start(f32[7,3]{0,1:T(4,128)} %param.14) | copy-start | bytes 256
  8.9 6.4 %copy-start.1 = (bf16[21,4,16,128]{3,2,1,0:T(8,128)(2,1)S(1)}, bf16[21,4,16,128]{3,2,1,0:T(8,128)(2,1)}, u32[]{:S(2)}) copy-start(bf16[21,4,16,128]{3,2,1,0:T(8,128)(2,1)} %param.8) | copy-start | bytes 1032196
  12.5 5.1 %collective-permute-start.2 = (bf16[1344,128]{1,0:T(8,128)(2,1)S(1)}, bf16[1344,128]{1,0:T(8,128)(2,1)S(1)}, u32[]{:S(2)}, u32[]{:S(2)}) collective-permute-start(bf16[1344,128]{1,0:T(8,128)(2,1)S(1)} %collective-permute-done.1.refs_0_), channel_id=1, source_target_pairs={{0,1},{1,0},{2,3},{3,2},{4,5},{5,4},{6,7},{7,6},{8,9},{9,8},{10,11... | collective-permute-start | bytes 1032200 | tf_op jit(solution)/shard_map/ppermute | solution.py:209
  14.6 0.8 %copy-start = (f32[7,16,128]{2,1,0:T(8,128)S(1)}, f32[7,16,128]{2,1,0:T(8,128)}, u32[]{:S(2)}) copy-start(f32[7,16,128]{2,1,0:T(8,128)} %kl_ref.1) | copy-start | bytes 172036
  14.6 0.8 %copy-start.2 = (s32[16,128]{1,0:T(8,128)S(1)}, s32[16,128]{1,0:T(8,128)}, u32[]{:S(2)}) copy-start(s32[16,128]{1,0:T(8,128)} %mat_ref.1) | copy-start | bytes 24580
  14.6 0.8 %copy-start.3 = (s32[16,128]{1,0:T(8,128)S(1)}, s32[16,128]{1,0:T(8,128)}, u32[]{:S(2)}) copy-start(s32[16,128]{1,0:T(8,128)} %chr_ref.1) | copy-start | bytes 24580
  14.6 0.8 %copy-start.4 = (f32[7,8]{1,0:T(8,128)S(1)}, f32[7,8]{1,0:T(8,128)}, u32[]{:S(2)}) copy-start(f32[7,8]{1,0:T(8,128)} %mt_ref.1) | copy-start | bytes 676
  14.6 0.8 %copy-start.5 = (f32[7,8]{1,0:T(8,128)S(1)}, f32[7,8]{1,0:T(8,128)}, u32[]{:S(2)}) copy-start(f32[7,8]{1,0:T(8,128)} %et_ref.1) | copy-start | bytes 676
  19.9 19.7 %collective-permute-start.3 = (bf16[4,112,128]{2,1,0:T(8,128)(2,1)S(1)}, bf16[4,112,128]{2,1,0:T(8,128)(2,1)S(1)}, u32[]{:S(2)}, u32[]{:S(2)}) collective-permute-start(bf16[4,112,128]{2,1,0:T(8,128)(2,1)S(1)} %pad_maximum_fusion), channel_id=1, source_target_pairs={{0,4},{4,8},{8,12},{12,16},{16,20},{20,24},{24,28},{28,32},{32,36}... | collective-permute-start | bytes 344072 | tf_op jit(solution)/shard_map/ppermute | solution.py:296
  23.4 16.2 %collective-permute-start.4 = (bf16[4,112,128]{2,1,0:T(8,128)(2,1)S(1)}, bf16[4,112,128]{2,1,0:T(8,128)(2,1)S(1)}, u32[]{:S(2)}, u32[]{:S(2)}) collective-permute-start(bf16[4,112,128]{2,1,0:T(8,128)(2,1)S(1)} %pad_maximum_fusion.1), channel_id=1, source_target_pairs={{4,0},{8,4},{12,8},{16,12},{20,16},{24,20},{28,24},{32,28},{36,32}... | collective-permute-start | bytes 344072 | tf_op jit(solution)/shard_map/ppermute | solution.py:297

commit v9 on v5

--- a/solution.py
+++ b/solution.py
@@ -23,17 +23,23 @@
     return above, below
 
 
-def kernel(nblock, prev, final, partial, nfield, rows, width, terms, nmat, nchar, *refs):
+def kernel(nblock, prev, final, partial, make, nfield, rows, width, terms, nmat, nchar, *refs):
     blocks = refs[:nblock]
     refs = refs[nblock:]
     if prev:
         prev_ref, refs = refs[0], refs[1:]
-    if final:
+    if final and make:
         cp_ref, kl_ref, mat_ref, chr_ref, mt_ref, ct_ref, et_ref = refs[:7]
         refs = refs[7:]
         if partial:
             part_ref, refs = refs[0], refs[1:]
-        out_ref, fs, hs, os, cs, es = refs
+        out_ref, cs, es, fs, hs, os = refs
+    elif final:
+        cp_ref, cs, es = refs[:3]
+        refs = refs[3:]
+        if partial:
+            part_ref, refs = refs[0], refs[1:]
+        out_ref, fs, hs, os = refs
     else:
         out_ref, fs, hs = refs
     nloc = blocks[0].shape[0] // (nfield * (rows + 2))
@@ -42,7 +48,7 @@
     core = nfield * rows
     per = nloc * nfield
 
-    if final:
+    if final and make:
         mat = mat_ref[...]
         chs = chr_ref[...]
         for k in range(terms):
@@ -191,11 +197,8 @@
             pltpu.VMEM((2 * local_modes * nfield, width), jnp.float32),
         ]
 
-    mix_scratch = [
-        pltpu.VMEM((PAD_I * OS, width), jnp.float32),
-        pltpu.VMEM((terms, rows, width), jnp.float32),
-        pltpu.VMEM((terms, rows, width), jnp.float32),
-    ]
+    mix_scratch = [pltpu.VMEM((PAD_I * OS, width), jnp.float32)]
+    coef = jax.ShapeDtypeStruct((terms, rows, width), jnp.float32)
 
     def mix_cost(span):
         return pl.CostEstimate(
@@ -203,17 +206,17 @@
             bytes_accessed=span * comps * rows * width * 2 + fields.size * 8,
         )
 
-    partial = pl.pallas_call(
-        functools.partial(kernel, 2, False, True, False, nfield, rows, width, terms, nmat, nchar),
-        out_shape=jax.ShapeDtypeStruct(fields.shape, jnp.float32),
+    partial, cond, expand = pl.pallas_call(
+        functools.partial(kernel, 2, False, True, False, True, nfield, rows, width, terms, nmat, nchar),
+        out_shape=(jax.ShapeDtypeStruct(fields.shape, jnp.float32), coef, coef),
         in_specs=[vmem] * 6 + [smem] * 3,
-        out_specs=vmem,
+        out_specs=(vmem, vmem, vmem),
         scratch_shapes=scratch(2) + mix_scratch,
         compiler_params=params,
         cost_estimate=mix_cost(padded(2)),
     )(pack, partner, columns([(0, 2)]), *tables)
     ops = pl.pallas_call(
-        functools.partial(kernel, 1, False, False, False, nfield, rows, width, terms, nmat, nchar),
+        functools.partial(kernel, 1, False, False, False, False, nfield, rows, width, terms, nmat, nchar),
         out_shape=jax.ShapeDtypeStruct((rows, padded(1), comps * width), jnp.bfloat16),
         in_specs=[vmem],
         out_specs=vmem,
@@ -225,14 +228,14 @@
         ),
     )(counter)
     return pl.pallas_call(
-        functools.partial(kernel, 1, True, True, True, nfield, rows, width, terms, nmat, nchar),
+        functools.partial(kernel, 1, True, True, True, False, nfield, rows, width, terms, nmat, nchar),
         out_shape=jax.ShapeDtypeStruct(fields.shape, fields.dtype),
-        in_specs=[vmem] * 6 + [smem] * 3 + [vmem],
+        in_specs=[vmem] * 6,
         out_specs=vmem,
         scratch_shapes=scratch(1) + mix_scratch,
         compiler_params=params,
         cost_estimate=mix_cost(2 * padded(1)),
-    )(diagonal, ops, columns([(2, 3), (3, 4)]), *tables, partial)
+    )(diagonal, ops, columns([(2, 3), (3, 4)]), cond, expand, partial)
 
 
 def solution(mesh):

time: 47.8 us -> 47.1 us (0.985)
  Pallas kernels: 6.21 us -> 5.46 us
    pallas_call x3, Pallas kernels: 6.21 us -> 5.46 us  [the longest x1 2.39 us: body(): pl.pallas_call(functools.partial(kernel, 2, False, True, False, True, nfi...]
where the time goes in v9:
time: 47.1 us; the launch traced here: 46.2 us
  starting transfers between devices  23.4 us (50%)
  waiting for transfers between devices  14.6 us (31%)
  Pallas kernels  5.46 us (12%)
  local copies, waits for them, and re-layouts  2.09 us (4%)
    ppermute x1, starting transfers between devices, edge_rows(): lax.ppermute(head, axis, [((i + 1) % count, i) for i in range(ends)])  14.1 us
    ppermute x1, waiting for transfers between devices, edge_rows(): lax.ppermute(tail, axis, [(i, (i + 1) % count) for i in range(ends)])  9.07 us
    ppermute x1, waiting for transfers between devices, body(): counter = lax.ppermute(pack, 'modes', [(i, i ^ 2) for i in range(groups)])  5.55 us
    ppermute x1, starting transfers between devices, body(): counter = lax.ppermute(pack, 'modes', [(i, i ^ 2) for i in range(groups)])  3.51 us
    pallas_call x1, Pallas kernels, body(): pl.pallas_call(functools.partial(kernel, 2, False, True, False, True, nfi...  2.39 us
    pallas_call x1, Pallas kernels, body(): pl.pallas_call(functools.partial(kernel, 1, True, True, True, False, nfie...  2.27 us
    ppermute x1, starting transfers between devices, edge_rows(): lax.ppermute(tail, axis, [(i, (i + 1) % count) for i in range(ends)])  1.92 us
    ppermute x1, starting transfers between devices, body(): partner = lax.ppermute(pack, 'modes', [(i, i ^ 1) for i in range(groups)])  1.92 us
  transfers between devices with their start and end apart: 5, of which 2 were waited for; matrix products, arithmetic and copies ran while one was open for 1% of the time, Pallas kernels for 7%

profile of v9, /device:TPU:6, one launch (start us, length us, event | category | flops | bytes accessed | tf_op | source)
XLA Modules:
  0.0 46.2 jit_solution(14260475343674895930)
XLA Ops:
  0.0 1.1 %fusion.7 = (bf16[21,4,1,128]{3,2,1,0:T(2,128)(2,1)S(1)}, bf16[21,4,1,128]{3,2,1,0:T(2,128)(2,1)S(1)}) fusion(bf16[21,4,16,128]{3,2,1,0:T(8,128)(2,1)} %param.8), kind=kLoop, calls=%fused_computation.17 | loop fusion | bytes 86016 | tf_op jit(solution)/shard_map/slice | solution.py:20
  1.1 14.1 %collective-permute-start.1 = (bf16[21,4,1,128]{3,2,1,0:T(2,128)(2,1)S(1)}, bf16[21,4,1,128]{3,2,1,0:T(2,128)(2,1)S(1)}, u32[]{:S(2)}, u32[]{:S(2)}) collective-permute-start(bf16[21,4,1,128]{3,2,1,0:T(2,128)(2,1)S(1)} %get-tuple-element.12), channel_id=1, source_target_pairs={{4,0},{8,4},{12,8},{16,12},{20,16},{24,20},{28,24},{32,28},{36,32}... | collective-permute-start | bytes 64520 | tf_op jit(solution)/shard_map/ppermute | solution.py:22
  15.3 1.9 %collective-permute-start = (bf16[21,4,1,128]{3,1,0,2:T(4,128)(2,1)S(1)}, bf16[21,4,1,128]{3,1,0,2:T(4,128)(2,1)S(1)}, u32[]{:S(2)}, u32[]{:S(2)}) collective-permute-start(bf16[21,4,1,128]{3,1,0,2:T(4,128)(2,1)S(1)} %copy.16), channel_id=1, source_target_pairs={{0,4},{4,8},{8,12},{12,16},{16,20},{20,24},{24,28},{28,32},{32,36}... | collective-permute-start | bytes 64520 | tf_op jit(solution)/shard_map/ppermute | solution.py:21
  17.2 9.1 %collective-permute-done = bf16[21,4,1,128]{3,1,0,2:T(4,128)(2,1)S(1)} collective-permute-done((bf16[21,4,1,128]{3,1,0,2:T(4,128)(2,1)S(1)}, bf16[21,4,1,128]{3,1,0,2:T(4,128)(2,1)S(1)}, u32[]{:S(2)}, u32[]{:S(2)}) %collective-permute-start) | collective-permute-done | bytes 21536 | tf_op jit(solution)/shard_map/ppermute | solution.py:21
  26.4 0.0 copy-start.6
  26.4 3.5 %collective-permute-start.2 = (bf16[1512,128]{1,0:T(8,128)(2,1)S(1)}, bf16[1512,128]{1,0:T(8,128)(2,1)S(1)}, u32[]{:S(2)}, u32[]{:S(2)}) collective-permute-start(bf16[1512,128]{1,0:T(8,128)(2,1)S(1)} %pad_maximum_fusion.refs_0_), channel_id=1, source_target_pairs={{0,2},{1,3},{2,0},{3,1},{4,6},{5,7},{6,4},{7,5},{8,10},{9,11},{10,... | collective-permute-start | bytes 1161224 | tf_op jit(solution)/shard_map/ppermute | solution.py:161
  30.0 0.1 constant_dynamic-slice_fusion.3
  30.1 0.1 fusion.6
  30.3 0.0 copy-start.7
  30.3 1.9 %collective-permute-start.4 = (bf16[1512,128]{1,0:T(8,128)(2,1)S(1)}, bf16[1512,128]{1,0:T(8,128)(2,1)S(1)}, u32[]{:S(2)}, u32[]{:S(2)}) collective-permute-start(bf16[1512,128]{1,0:T(8,128)(2,1)S(1)} %pad_maximum_fusion.refs_0_), channel_id=1, source_target_pairs={{0,1},{1,0},{2,3},{3,2},{4,5},{5,4},{6,7},{7,6},{8,9},{9,8},{10,11... | collective-permute-start | bytes 1161224 | tf_op jit(solution)/shard_map/ppermute | solution.py:160
  32.2 5.6 %collective-permute-done.2.refs_0_ = bf16[1512,128]{1,0:T(8,128)(2,1)S(1)} collective-permute-done((bf16[1512,128]{1,0:T(8,128)(2,1)S(1)}, bf16[1512,128]{1,0:T(8,128)(2,1)S(1)}, u32[]{:S(2)}, u32[]{:S(2)}) %collective-permute-start.2) | collective-permute-done | bytes 387104 | tf_op jit(solution)/shard_map/ppermute | solution.py:161
  37.8 1.9 %collective-permute-start.3 = (bf16[1512,128]{1,0:T(8,128)(2,1)S(1)}, bf16[1512,128]{1,0:T(8,128)(2,1)S(1)}, u32[]{:S(2)}, u32[]{:S(2)}) collective-permute-start(bf16[1512,128]{1,0:T(8,128)(2,1)S(1)} %collective-permute-done.2.refs_0_), channel_id=1, source_target_pairs={{0,1},{1,0},{2,3},{3,2},{4,5},{5,4},{6,7},{7,6},{8,9},{9,8},{10,11... | collective-permute-start | bytes 1161224 | tf_op jit(solution)/shard_map/ppermute | solution.py:162
  39.7 0.1 fusion.8
  39.8 0.1 copy.14.refs_7_
  39.9 0.1 pad_maximum_fusion.1
  40.0 0.5 %copy-done.8 = pred[48]{0:T(512)(128)(4,1)S(1)} copy-done((pred[48]{0:T(512)(128)(4,1)S(1)}, pred[48]{0:T(512)(128)(4,1)}, u32[]{:S(2)}) %copy-start.8) | copy-done | bytes 72
  40.6 0.0 copy-start
  40.6 0.0 copy-start.1
  40.6 0.0 copy-start.2
  40.6 0.0 copy-start.3
  40.6 0.0 copy-start.4
  40.6 0.8 %shard_map.82.refs_1_ = bf16[16,32,768]{2,1,0:T(8,128)(2,1)S(1)} custom-call(bf16[1512,128]{1,0:T(8,128)(2,1)S(1)} %collective-permute-done.2.refs_0_), custom_call_target="tpu_custom_call" | custom-call | flops 4718592 | bytes 1173504 | tf_op jit(solution)/shard_map/pallas_call | solution.py:218
  41.5 2.4 %shard_map.83 = (f32[21,4,16,128]{3,2,1,0:T(8,128)S(1)}, f32[7,16,128]{2,1,0:T(8,128)S(1)}, f32[7,16,128]{2,1,0:T(8,128)S(1)}) custom-call(bf16[1512,128]{1,0:T(8,128)(2,1)S(1)} %pad_maximum_fusion.refs_0_, bf16[1512,128]{1,0:T(8,128)(2,1)S(1)} %collective-permute-done.4.refs_1_, bf16[168,48]{1,0:T(8,128)(2,1)S(1)} %bitcast.10, f32[7,16,128]{2,1,0:T(8,128)S(1)} %copy-done, ...), custom_call_target="tpu_custom_call" | custom-call | flops 198180864 | bytes 2555904 | tf_op jit(solution)/shard_map/pallas_call | solution.py:209
  43.9 2.3 %shard_map.84 = bf16[21,4,16,128]{3,2,1,0:T(8,128)(2,1)} custom-call(bf16[1512,128]{1,0:T(8,128)(2,1)S(1)} %collective-permute-done.3.refs_0_, bf16[16,32,768]{2,1,0:T(8,128)(2,1)S(1)} %shard_map.82.refs_1_, bf16[168,64]{1,0:T(8,128)(2,1)S(1)} %bitcast.9, f32[7,16,128]{2,1,0:T(8,128)S(1)} %get-tuple-element.8.refs_3_, ...), custom_call_target="tpu_custom_call" | custom-call | flops 264241152 | bytes 2949120 | tf_op jit(solution)/shard_map/pallas_call | solution.py:230
  (21 shorter events, 0.2 us)
Async XLA Ops:
  0.0 26.4 %copy-start.5 = (bf16[21,4,16,128]{3,2,1,0:T(8,128)(2,1)S(1)}, bf16[21,4,16,128]{3,2,1,0:T(8,128)(2,1)}, u32[]{:S(2)}) copy-start(bf16[21,4,16,128]{3,2,1,0:T(8,128)(2,1)} %param.8) | copy-start | bytes 1032196
  1.1 16.1 %collective-permute-start.1 = (bf16[21,4,1,128]{3,2,1,0:T(2,128)(2,1)S(1)}, bf16[21,4,1,128]{3,2,1,0:T(2,128)(2,1)S(1)}, u32[]{:S(2)}, u32[]{:S(2)}) collective-permute-start(bf16[21,4,1,128]{3,2,1,0:T(2,128)(2,1)S(1)} %get-tuple-element.12), channel_id=1, source_target_pairs={{4,0},{8,4},{12,8},{16,12},{20,16},{24,20},{28,24},{32,28},{36,32}... | collective-permute-start | bytes 64520 | tf_op jit(solution)/shard_map/ppermute | solution.py:22
  15.3 11.0 %collective-permute-start = (bf16[21,4,1,128]{3,1,0,2:T(4,128)(2,1)S(1)}, bf16[21,4,1,128]{3,1,0,2:T(4,128)(2,1)S(1)}, u32[]{:S(2)}, u32[]{:S(2)}) collective-permute-start(bf16[21,4,1,128]{3,1,0,2:T(4,128)(2,1)S(1)} %copy.16), channel_id=1, source_target_pairs={{0,4},{4,8},{8,12},{12,16},{16,20},{20,24},{24,28},{28,32},{32,36}... | collective-permute-start | bytes 64520 | tf_op jit(solution)/shard_map/ppermute | solution.py:21
  26.4 3.6 %copy-start.6 = (bf16[7,84,84]{2,1,0:T(8,128)(2,1)S(1)}, bf16[7,84,84]{2,1,0:T(8,128)(2,1)}, u32[]{:S(2)}) copy-start(bf16[7,84,84]{2,1,0:T(8,128)(2,1)} %param.9) | copy-start | bytes 296356
  26.4 11.3 %collective-permute-start.2 = (bf16[1512,128]{1,0:T(8,128)(2,1)S(1)}, bf16[1512,128]{1,0:T(8,128)(2,1)S(1)}, u32[]{:S(2)}, u32[]{:S(2)}) collective-permute-start(bf16[1512,128]{1,0:T(8,128)(2,1)S(1)} %pad_maximum_fusion.refs_0_), channel_id=1, source_target_pairs={{0,2},{1,3},{2,0},{3,1},{4,6},{5,7},{6,4},{7,5},{8,10},{9,11},{10,... | collective-permute-start | bytes 1161224 | tf_op jit(solution)/shard_map/ppermute | solution.py:161
  30.3 9.5 %copy-start.7 = (f32[7,3]{0,1:T(4,128)S(1)}, f32[7,3]{0,1:T(4,128)}, u32[]{:S(2)}) copy-start(f32[7,3]{0,1:T(4,128)} %param.14) | copy-start | bytes 256
  30.3 11.1 %collective-permute-start.4 = (bf16[1512,128]{1,0:T(8,128)(2,1)S(1)}, bf16[1512,128]{1,0:T(8,128)(2,1)S(1)}, u32[]{:S(2)}, u32[]{:S(2)}) collective-permute-start(bf16[1512,128]{1,0:T(8,128)(2,1)S(1)} %pad_maximum_fusion.refs_0_), channel_id=1, source_target_pairs={{0,1},{1,0},{2,3},{3,2},{4,5},{5,4},{6,7},{7,6},{8,9},{9,8},{10,11... | collective-permute-start | bytes 1161224 | tf_op jit(solution)/shard_map/ppermute | solution.py:160
  37.8 6.1 %collective-permute-start.3 = (bf16[1512,128]{1,0:T(8,128)(2,1)S(1)}, bf16[1512,128]{1,0:T(8,128)(2,1)S(1)}, u32[]{:S(2)}, u32[]{:S(2)}) collective-permute-start(bf16[1512,128]{1,0:T(8,128)(2,1)S(1)} %collective-permute-done.2.refs_0_), channel_id=1, source_target_pairs={{0,1},{1,0},{2,3},{3,2},{4,5},{5,4},{6,7},{7,6},{8,9},{9,8},{10,11... | collective-permute-start | bytes 1161224 | tf_op jit(solution)/shard_map/ppermute | solution.py:162
  39.9 0.7 %copy-start.8 = (pred[48]{0:T(512)(128)(4,1)S(1)}, pred[48]{0:T(512)(128)(4,1)}, u32[]{:S(2)}) copy-start(pred[48]{0:T(512)(128)(4,1)} %constant.82.clone.1) | copy-start | bytes 148
  40.6 0.9 %copy-start = (f32[7,16,128]{2,1,0:T(8,128)S(1)}, f32[7,16,128]{2,1,0:T(8,128)}, u32[]{:S(2)}) copy-start(f32[7,16,128]{2,1,0:T(8,128)} %refs_3_.1) | copy-start | bytes 172036
  40.6 0.9 %copy-start.1 = (s32[16,128]{1,0:T(8,128)S(1)}, s32[16,128]{1,0:T(8,128)}, u32[]{:S(2)}) copy-start(s32[16,128]{1,0:T(8,128)} %refs_4_.1) | copy-start | bytes 24580
  40.6 0.9 %copy-start.2 = (s32[16,128]{1,0:T(8,128)S(1)}, s32[16,128]{1,0:T(8,128)}, u32[]{:S(2)}) copy-start(s32[16,128]{1,0:T(8,128)} %refs_5_.1) | copy-start | bytes 24580
  40.6 0.9 %copy-start.3 = (f32[7,8]{1,0:T(8,128)S(1)}, f32[7,8]{1,0:T(8,128)}, u32[]{:S(2)}) copy-start(f32[7,8]{1,0:T(8,128)} %refs_6_.1) | copy-start | bytes 676
  40.6 0.9 %copy-start.4 = (f32[7,8]{1,0:T(8,128)S(1)}, f32[7,8]{1,0:T(8,128)}, u32[]{:S(2)}) copy-start(f32[7,8]{1,0:T(8,128)} %refs_8_.1) | copy-start | bytes 676

commit v10 on v9

--- a/solution.py
+++ b/solution.py
@@ -178,22 +178,23 @@
     params = pltpu.CompilerParams(vmem_limit_bytes=48 * 1024 * 1024)
     nmat, nchar = material_table.shape[1], char_table.shape[1]
 
-    def padded(count):
-        return -(-count * local_modes // 16) * 16
+    def padded(count, unit=16):
+        return -(-count * local_modes // unit) * unit
 
     def columns(groups_of_blocks):
         pieces = []
-        for lo, hi in groups_of_blocks:
+        for n, (lo, hi) in enumerate(groups_of_blocks):
             pieces.append(weights[:, :, lo * local_modes:hi * local_modes])
-            gap = padded(hi - lo) - (hi - lo) * local_modes
+            unit = 8 if n == len(groups_of_blocks) - 1 and len(groups_of_blocks) > 1 else 16
+            gap = padded(hi - lo, unit) - (hi - lo) * local_modes
             if gap:
                 pieces.append(jnp.zeros((terms, PAD_I, gap), weights.dtype))
         cat = jnp.concatenate(pieces, axis=2)
         return cat.reshape(terms * PAD_I, cat.shape[2])
 
-    def scratch(count):
+    def scratch(count, unit=16):
         return [
-            pltpu.VMEM((padded(count) * JS, width), jnp.float32),
+            pltpu.VMEM((padded(count, unit) * JS, width), jnp.float32),
             pltpu.VMEM((2 * local_modes * nfield, width), jnp.float32),
         ]
 
@@ -232,9 +233,9 @@
         out_shape=jax.ShapeDtypeStruct(fields.shape, fields.dtype),
         in_specs=[vmem] * 6,
         out_specs=vmem,
-        scratch_shapes=scratch(1) + mix_scratch,
+        scratch_shapes=scratch(1, 8) + mix_scratch,
         compiler_params=params,
-        cost_estimate=mix_cost(2 * padded(1)),
+        cost_estimate=mix_cost(padded(1) + padded(1, 8)),
     )(diagonal, ops, columns([(2, 3), (3, 4)]), cond, expand, partial)
 
 

time: 47.1 us -> 46.8 us (level)
  waiting for transfers between devices: 14.6 us -> 13.7 us
  local copies, waits for them, and re-layouts: 2.09 us -> 2.86 us
    ppermute x1, waiting for transfers between devices: 5.55 us -> 4.64 us  [body(): counter = lax.ppermute(pack, 'modes', [(i, i ^ 2) for i in range(groups)])]
    unnamed x21, local copies, waits for them, and re-layouts: 0.7 us -> 1.31 us
  transfers between devices with their start and end apart: 5 -> 5, of which waited for: 2 -> 2; matrix products, arithmetic and copies ran while one was open for 1% -> 2% of each run, Pallas kernels for 7% -> 7%
where the time goes in v10:
time: 46.8 us; the launch traced here: 45.9 us
  starting transfers between devices  23.4 us (50%)
  waiting for transfers between devices  13.7 us (29%)
  Pallas kernels  5.42 us (12%)
  local copies, waits for them, and re-layouts  2.86 us (6%)
    ppermute x1, starting transfers between devices, edge_rows(): lax.ppermute(head, axis, [((i + 1) % count, i) for i in range(ends)])  14.1 us
    ppermute x1, waiting for transfers between devices, edge_rows(): lax.ppermute(tail, axis, [(i, (i + 1) % count) for i in range(ends)])  9.04 us
    ppermute x1, waiting for transfers between devices, body(): counter = lax.ppermute(pack, 'modes', [(i, i ^ 2) for i in range(groups)])  4.64 us
    ppermute x1, starting transfers between devices, body(): counter = lax.ppermute(pack, 'modes', [(i, i ^ 2) for i in range(groups)])  3.51 us
    pallas_call x1, Pallas kernels, body(): pl.pallas_call(functools.partial(kernel, 2, False, True, False, True, nfi...  2.38 us
    pallas_call x1, Pallas kernels, body(): pl.pallas_call(functools.partial(kernel, 1, True, True, True, False, nfie...  2.25 us
    ppermute x1, starting transfers between devices, edge_rows(): lax.ppermute(tail, axis, [(i, (i + 1) % count) for i in range(ends)])  1.92 us
    ppermute x1, starting transfers between devices, body(): partner = lax.ppermute(pack, 'modes', [(i, i ^ 1) for i in range(groups)])  1.92 us
  transfers between devices with their start and end apart: 5, of which 2 were waited for; matrix products, arithmetic and copies ran while one was open for 2% of the time, Pallas kernels for 7%

profile of v10, /device:TPU:6, one launch (start us, length us, event | category | flops | bytes accessed | tf_op | source)
XLA Modules:
  0.0 45.9 jit_solution(15442686706839876211)
XLA Ops:
  0.0 1.1 %fusion.7 = (bf16[21,4,1,128]{3,2,1,0:T(2,128)(2,1)S(1)}, bf16[21,4,1,128]{3,2,1,0:T(2,128)(2,1)S(1)}) fusion(bf16[21,4,16,128]{3,2,1,0:T(8,128)(2,1)} %param.8), kind=kLoop, calls=%fused_computation.17 | loop fusion | bytes 86016 | tf_op jit(solution)/shard_map/slice | solution.py:20
  1.1 14.1 %collective-permute-start.1 = (bf16[21,4,1,128]{3,2,1,0:T(2,128)(2,1)S(1)}, bf16[21,4,1,128]{3,2,1,0:T(2,128)(2,1)S(1)}, u32[]{:S(2)}, u32[]{:S(2)}) collective-permute-start(bf16[21,4,1,128]{3,2,1,0:T(2,128)(2,1)S(1)} %get-tuple-element.12), channel_id=1, source_target_pairs={{4,0},{8,4},{12,8},{16,12},{20,16},{24,20},{28,24},{32,28},{36,32}... | collective-permute-start | bytes 64520 | tf_op jit(solution)/shard_map/ppermute | solution.py:22
  15.3 1.9 %collective-permute-start = (bf16[21,4,1,128]{3,1,0,2:T(4,128)(2,1)S(1)}, bf16[21,4,1,128]{3,1,0,2:T(4,128)(2,1)S(1)}, u32[]{:S(2)}, u32[]{:S(2)}) collective-permute-start(bf16[21,4,1,128]{3,1,0,2:T(4,128)(2,1)S(1)} %copy.16), channel_id=1, source_target_pairs={{0,4},{4,8},{8,12},{12,16},{16,20},{20,24},{24,28},{28,32},{32,36}... | collective-permute-start | bytes 64520 | tf_op jit(solution)/shard_map/ppermute | solution.py:21
  17.2 9.0 %collective-permute-done = bf16[21,4,1,128]{3,1,0,2:T(4,128)(2,1)S(1)} collective-permute-done((bf16[21,4,1,128]{3,1,0,2:T(4,128)(2,1)S(1)}, bf16[21,4,1,128]{3,1,0,2:T(4,128)(2,1)S(1)}, u32[]{:S(2)}, u32[]{:S(2)}) %collective-permute-start) | collective-permute-done | bytes 21536 | tf_op jit(solution)/shard_map/ppermute | solution.py:21
  26.4 0.0 copy-start.6
  26.4 3.5 %collective-permute-start.2 = (bf16[1512,128]{1,0:T(8,128)(2,1)S(1)}, bf16[1512,128]{1,0:T(8,128)(2,1)S(1)}, u32[]{:S(2)}, u32[]{:S(2)}) collective-permute-start(bf16[1512,128]{1,0:T(8,128)(2,1)S(1)} %pad_maximum_fusion.refs_0_), channel_id=1, source_target_pairs={{0,2},{1,3},{2,0},{3,1},{4,6},{5,7},{6,4},{7,5},{8,10},{9,11},{10,... | collective-permute-start | bytes 1161224 | tf_op jit(solution)/shard_map/ppermute | solution.py:161
  30.0 0.1 constant_dynamic-slice_fusion.3
  30.1 0.1 pad.7.clone
  30.2 0.1 pad.9.clone
  30.3 0.6 %copy-done.7 = f32[7,3]{0,1:T(4,128)S(1)} copy-done((f32[7,3]{0,1:T(4,128)S(1)}, f32[7,3]{0,1:T(4,128)}, u32[]{:S(2)}) %copy-start.7) | copy-done | bytes 108
  30.9 0.1 copy.14.refs_7_
  31.0 0.1 fusion.6
  31.1 0.1 fusion.8
  31.2 1.9 %collective-permute-start.4 = (bf16[1512,128]{1,0:T(8,128)(2,1)S(1)}, bf16[1512,128]{1,0:T(8,128)(2,1)S(1)}, u32[]{:S(2)}, u32[]{:S(2)}) collective-permute-start(bf16[1512,128]{1,0:T(8,128)(2,1)S(1)} %pad_maximum_fusion.refs_0_), channel_id=1, source_target_pairs={{0,1},{1,0},{2,3},{3,2},{4,5},{5,4},{6,7},{7,6},{8,9},{9,8},{10,11... | collective-permute-start | bytes 1161224 | tf_op jit(solution)/shard_map/ppermute | solution.py:160
  33.1 4.6 %collective-permute-done.2.refs_0_ = bf16[1512,128]{1,0:T(8,128)(2,1)S(1)} collective-permute-done((bf16[1512,128]{1,0:T(8,128)(2,1)S(1)}, bf16[1512,128]{1,0:T(8,128)(2,1)S(1)}, u32[]{:S(2)}, u32[]{:S(2)}) %collective-permute-start.2) | collective-permute-done | bytes 387104 | tf_op jit(solution)/shard_map/ppermute | solution.py:161
  37.8 1.9 %collective-permute-start.3 = (bf16[1512,128]{1,0:T(8,128)(2,1)S(1)}, bf16[1512,128]{1,0:T(8,128)(2,1)S(1)}, u32[]{:S(2)}, u32[]{:S(2)}) collective-permute-start(bf16[1512,128]{1,0:T(8,128)(2,1)S(1)} %collective-permute-done.2.refs_0_), channel_id=1, source_target_pairs={{0,1},{1,0},{2,3},{3,2},{4,5},{5,4},{6,7},{7,6},{8,9},{9,8},{10,11... | collective-permute-start | bytes 1161224 | tf_op jit(solution)/shard_map/ppermute | solution.py:162
  39.7 0.0 copy-start.8
  39.7 0.1 maximum_maximum_fusion
  39.8 0.6 %copy-done.8 = pred[48]{0:T(512)(128)(4,1)S(1)} copy-done((pred[48]{0:T(512)(128)(4,1)S(1)}, pred[48]{0:T(512)(128)(4,1)}, u32[]{:S(2)}) %copy-start.8) | copy-done | bytes 72
  40.4 0.0 copy-start.1
  40.4 0.0 copy-start.2
  40.4 0.8 %shard_map.82.refs_1_ = bf16[16,32,768]{2,1,0:T(8,128)(2,1)S(1)} custom-call(bf16[1512,128]{1,0:T(8,128)(2,1)S(1)} %collective-permute-done.2.refs_0_), custom_call_target="tpu_custom_call" | custom-call | flops 4718592 | bytes 1173504 | tf_op jit(solution)/shard_map/pallas_call | solution.py:219
  41.3 2.4 %shard_map.83 = (f32[21,4,16,128]{3,2,1,0:T(8,128)S(1)}, f32[7,16,128]{2,1,0:T(8,128)S(1)}, f32[7,16,128]{2,1,0:T(8,128)S(1)}) custom-call(bf16[1512,128]{1,0:T(8,128)(2,1)S(1)} %pad_maximum_fusion.refs_0_, bf16[1512,128]{1,0:T(8,128)(2,1)S(1)} %collective-permute-done.4.refs_1_, bf16[168,48]{1,0:T(8,128)(2,1)S(1)} %bitcast.10, f32[7,16,128]{2,1,0:T(8,128)S(1)} %copy-done, ...), custom_call_target="tpu_custom_call" | custom-call | flops 198180864 | bytes 2555904 | tf_op jit(solution)/shard_map/pallas_call | solution.py:210
  43.7 2.3 %shard_map.84 = bf16[21,4,16,128]{3,2,1,0:T(8,128)(2,1)} custom-call(bf16[1512,128]{1,0:T(8,128)(2,1)S(1)} %collective-permute-done.3.refs_0_, bf16[16,32,768]{2,1,0:T(8,128)(2,1)S(1)} %shard_map.82.refs_1_, bf16[168,56]{1,0:T(8,128)(2,1)S(1)} %bitcast.9, f32[7,16,128]{2,1,0:T(8,128)S(1)} %get-tuple-element.8.refs_3_, ...), custom_call_target="tpu_custom_call" | custom-call | flops 231211008 | bytes 2752512 | tf_op jit(solution)/shard_map/pallas_call | solution.py:231
  (24 shorter events, 0.2 us)
Async XLA Ops:
  0.0 26.4 %copy-start.5 = (bf16[21,4,16,128]{3,2,1,0:T(8,128)(2,1)S(1)}, bf16[21,4,16,128]{3,2,1,0:T(8,128)(2,1)}, u32[]{:S(2)}) copy-start(bf16[21,4,16,128]{3,2,1,0:T(8,128)(2,1)} %param.8) | copy-start | bytes 1032196
  1.1 16.1 %collective-permute-start.1 = (bf16[21,4,1,128]{3,2,1,0:T(2,128)(2,1)S(1)}, bf16[21,4,1,128]{3,2,1,0:T(2,128)(2,1)S(1)}, u32[]{:S(2)}, u32[]{:S(2)}) collective-permute-start(bf16[21,4,1,128]{3,2,1,0:T(2,128)(2,1)S(1)} %get-tuple-element.12), channel_id=1, source_target_pairs={{4,0},{8,4},{12,8},{16,12},{20,16},{24,20},{28,24},{32,28},{36,32}... | collective-permute-start | bytes 64520 | tf_op jit(solution)/shard_map/ppermute | solution.py:22
  15.3 11.0 %collective-permute-start = (bf16[21,4,1,128]{3,1,0,2:T(4,128)(2,1)S(1)}, bf16[21,4,1,128]{3,1,0,2:T(4,128)(2,1)S(1)}, u32[]{:S(2)}, u32[]{:S(2)}) collective-permute-start(bf16[21,4,1,128]{3,1,0,2:T(4,128)(2,1)S(1)} %copy.16), channel_id=1, source_target_pairs={{0,4},{4,8},{8,12},{12,16},{16,20},{20,24},{24,28},{28,32},{32,36}... | collective-permute-start | bytes 64520 | tf_op jit(solution)/shard_map/ppermute | solution.py:21
  26.4 3.6 %copy-start.6 = (bf16[7,84,84]{2,1,0:T(8,128)(2,1)S(1)}, bf16[7,84,84]{2,1,0:T(8,128)(2,1)}, u32[]{:S(2)}) copy-start(bf16[7,84,84]{2,1,0:T(8,128)(2,1)} %param.9) | copy-start | bytes 296356
  26.4 11.3 %collective-permute-start.2 = (bf16[1512,128]{1,0:T(8,128)(2,1)S(1)}, bf16[1512,128]{1,0:T(8,128)(2,1)S(1)}, u32[]{:S(2)}, u32[]{:S(2)}) collective-permute-start(bf16[1512,128]{1,0:T(8,128)(2,1)S(1)} %pad_maximum_fusion.refs_0_), channel_id=1, source_target_pairs={{0,2},{1,3},{2,0},{3,1},{4,6},{5,7},{6,4},{7,5},{8,10},{9,11},{10,... | collective-permute-start | bytes 1161224 | tf_op jit(solution)/shard_map/ppermute | solution.py:161
  30.2 0.7 %copy-start.7 = (f32[7,3]{0,1:T(4,128)S(1)}, f32[7,3]{0,1:T(4,128)}, u32[]{:S(2)}) copy-start(f32[7,3]{0,1:T(4,128)} %param.14) | copy-start | bytes 256
  31.2 10.0 %collective-permute-start.4 = (bf16[1512,128]{1,0:T(8,128)(2,1)S(1)}, bf16[1512,128]{1,0:T(8,128)(2,1)S(1)}, u32[]{:S(2)}, u32[]{:S(2)}) collective-permute-start(bf16[1512,128]{1,0:T(8,128)(2,1)S(1)} %pad_maximum_fusion.refs_0_), channel_id=1, source_target_pairs={{0,1},{1,0},{2,3},{3,2},{4,5},{5,4},{6,7},{7,6},{8,9},{9,8},{10,11... | collective-permute-start | bytes 1161224 | tf_op jit(solution)/shard_map/ppermute | solution.py:160
  37.8 5.9 %collective-permute-start.3 = (bf16[1512,128]{1,0:T(8,128)(2,1)S(1)}, bf16[1512,128]{1,0:T(8,128)(2,1)S(1)}, u32[]{:S(2)}, u32[]{:S(2)}) collective-permute-start(bf16[1512,128]{1,0:T(8,128)(2,1)S(1)} %collective-permute-done.2.refs_0_), channel_id=1, source_target_pairs={{0,1},{1,0},{2,3},{3,2},{4,5},{5,4},{6,7},{7,6},{8,9},{9,8},{10,11... | collective-permute-start | bytes 1161224 | tf_op jit(solution)/shard_map/ppermute | solution.py:162
  39.7 0.7 %copy-start.8 = (pred[48]{0:T(512)(128)(4,1)S(1)}, pred[48]{0:T(512)(128)(4,1)}, u32[]{:S(2)}) copy-start(pred[48]{0:T(512)(128)(4,1)} %constant.83.clone.1) | copy-start | bytes 148
  40.3 0.9 %copy-start = (f32[7,16,128]{2,1,0:T(8,128)S(1)}, f32[7,16,128]{2,1,0:T(8,128)}, u32[]{:S(2)}) copy-start(f32[7,16,128]{2,1,0:T(8,128)} %refs_3_.1) | copy-start | bytes 172036
  40.4 0.9 %copy-start.1 = (s32[16,128]{1,0:T(8,128)S(1)}, s32[16,128]{1,0:T(8,128)}, u32[]{:S(2)}) copy-start(s32[16,128]{1,0:T(8,128)} %refs_4_.1) | copy-start | bytes 24580
  40.4 0.9 %copy-start.2 = (s32[16,128]{1,0:T(8,128)S(1)}, s32[16,128]{1,0:T(8,128)}, u32[]{:S(2)}) copy-start(s32[16,128]{1,0:T(8,128)} %refs_5_.1) | copy-start | bytes 24580
  40.4 0.9 %copy-start.3 = (f32[7,8]{1,0:T(8,128)S(1)}, f32[7,8]{1,0:T(8,128)}, u32[]{:S(2)}) copy-start(f32[7,8]{1,0:T(8,128)} %refs_6_.1) | copy-start | bytes 676
  40.4 0.9 %copy-start.4 = (f32[7,8]{1,0:T(8,128)S(1)}, f32[7,8]{1,0:T(8,128)}, u32[]{:S(2)}) copy-start(f32[7,8]{1,0:T(8,128)} %refs_8_.1) | copy-start | bytes 676
